TPU v7x, 768 devices: a whole 4x8x12 slice. The times are simulated.
768 devices in a mesh: pos: 64 (over x, y, core), tile: 12 (over z).
Axes of the slice: x: 4, y: 8, z: 12, core: 2. Of those that a mesh axis runs over, the one named last changes fastest.
Arguments:
- obj_tiles: bfloat16 [1536, 4, 4096], P('pos'), may hold values from -4.1875 to 4.1875
- tile_map: int32 [32, 48], replicated, may hold values from 0 to 1535, as said below
- offsets: int32 [768, 2], replicated, may hold values from 1 to 2943, as said below
- probe: float32 [2, 128, 128], replicated, may hold values from -6 to 6
- intens: float32 [768, 128, 128], P(('pos', 'tile')), may hold values from 0.05 to 2
Outputs:
- obj_grad: float32 [1536, 4, 4096], P('pos')
- probe_grad: float32 [2, 128, 128], replicated
Inputs may be any that keep to these rules, and one draw needn't show every extreme that they name: tile_map holds every storage index once. A tile's owner is its storage index // 24; the owner depends only on the tile row mod 8 and the tile column mod 8, and different such classes have different owners. `offsets`: every patch lies inside the window, and neither its row nor its column offset is a multiple of 64.
All inputs are finite; a program needn't handle non-finite values.
Results may differ from a plain program's by a relative error of at most 0.0023.
Values may be sent and summed in bfloat16 or wider, within the bound.
No kernel may reach another device: no remote copies, remote signals or barrier semaphores. Data moves between devices by JAX's collectives and lax.ppermute only.
A program may use at most 32 MiB of HBM per device.

v0:
```python
import math

import jax
import jax.numpy as jnp
from jax import lax
from jax.sharding import PartitionSpec as P

TS = 64
OWN_R = 8


def matmul_hi(left_op, right_op):
    return jnp.dot(
        left_op, right_op, precision=lax.Precision.HIGHEST, preferred_element_type=jnp.float32
    )


def spectral_tables(width_px):
    positions = jnp.arange(width_px, dtype=jnp.int32)
    phase_idx = positions[:, None] * positions[None, :] % width_px
    angles = phase_idx.astype(jnp.float32) * (2.0 * math.pi / width_px)
    norm_factor = 1.0 / math.sqrt(width_px)
    return (jnp.cos(angles) * norm_factor, -jnp.sin(angles) * norm_factor)


def complex_matmul(left_re, left_im, right_re, right_im):
    out_re = matmul_hi(left_re, right_re) - matmul_hi(left_im, right_im)
    out_im = matmul_hi(left_re, right_im) + matmul_hi(left_im, right_re)
    return (out_re, out_im)


def propagation_matrix(width_px, fwd_re, fwd_im, sign_val):
    positions = jnp.arange(width_px, dtype=jnp.int32)
    centred = (positions + width_px // 2) % width_px - width_px // 2
    angles = (centred * centred).astype(jnp.float32) * (-0.2 / width_px) * sign_val
    phase_re = jnp.cos(angles)[:, None]
    phase_im = jnp.sin(angles)[:, None]
    scaled_re = phase_re * fwd_re - phase_im * fwd_im
    scaled_im = phase_re * fwd_im + phase_im * fwd_re
    return complex_matmul(fwd_re, -fwd_im, scaled_re, scaled_im)


def transform(part_re, part_im, table_re, table_im):
    mid_re, mid_im = complex_matmul(part_re, part_im, table_re, table_im)
    return complex_matmul(table_re, table_im, mid_re, mid_im)


def product(left_re, left_im, right_re, right_im):
    return (left_re * right_re - left_im * right_im, left_re * right_im + left_im * right_re)


def per_device(obj_tiles, tile_map, offsets, probe, intens):
    owners = lax.axis_size("pos")
    layers = lax.axis_size("tile")
    me_pos = lax.axis_index("pos")
    me_tile = lax.axis_index("tile")
    tiles_dev = obj_tiles.shape[0]
    tile_edge = TS
    width_px = probe.shape[-1]
    tile_span = width_px // tile_edge + 1
    cols_own = owners // OWN_R
    cols_cap = (tile_span + cols_own - 1) // cols_own
    slots = (tile_span + OWN_R - 1) // OWN_R * cols_cap
    span_idx = jnp.arange(tile_span, dtype=jnp.int32)
    slot_grid = (span_idx[:, None] // OWN_R * cols_cap + span_idx[None, :] // cols_own).reshape(-1)

    def footprint(corner):
        row_ids = corner[0] // tile_edge + span_idx
        col_ids = corner[1] // tile_edge + span_idx
        store_id = tile_map[row_ids[:, None], col_ids[None, :]].reshape(-1)
        owner_id = store_id // tiles_dev
        return (owner_id, store_id - owner_id * tiles_dev)

    by_device = offsets.reshape(owners, layers, 2)
    peer_corners = lax.dynamic_index_in_dim(by_device, me_tile, 1, keepdims=False)
    peer_owner, peer_local = jax.vmap(footprint)(peer_corners)
    slot_ids = jnp.arange(slots, dtype=jnp.int32)
    matches = (peer_owner == me_pos)[:, :, None] & (
        slot_grid[None, :, None] == slot_ids[None, None, :]
    )
    send_local = jnp.sum(jnp.where(matches, peer_local[:, :, None], 0), axis=1)
    send_live = jnp.any(matches, axis=1)
    chosen = jnp.where(
        send_live[:, :, None, None], obj_tiles[send_local], jnp.zeros((), obj_tiles.dtype)
    )
    my_corner = lax.dynamic_index_in_dim(offsets, me_pos * layers + me_tile, 0, keepdims=False)
    my_owner, my_local = footprint(my_corner)
    flat_slot = my_owner * slots + slot_grid
    inner_y = my_corner[0] % tile_edge
    inner_x = my_corner[1] % tile_edge
    zero_idx = jnp.zeros((), jnp.int32)
    fwd_re, fwd_im = spectral_tables(width_px)
    ahead_re, ahead_im = propagation_matrix(width_px, fwd_re, fwd_im, 1.0)
    behind_re, behind_im = propagation_matrix(width_px, fwd_re, fwd_im, -1.0)
    probe_re = probe[0]
    probe_im = probe[1]
    received = lax.all_to_all(chosen, "pos", split_axis=0, concat_axis=0, tiled=True)
    n_comps = received.shape[2]
    pieces = received.reshape(owners * slots, n_comps, tile_edge * tile_edge)[flat_slot]
    region = pieces.reshape(tile_span, tile_span, n_comps, tile_edge, tile_edge).transpose(
        2, 0, 3, 1, 4
    )
    region = region.reshape(n_comps, tile_span * tile_edge, tile_span * tile_edge)
    patch_px = lax.dynamic_slice(
        region, (zero_idx, inner_y, inner_x), (n_comps, width_px, width_px)
    )
    fetched = patch_px.astype(jnp.float32)
    entry_patch = fetched[:2]
    leaving = fetched[2:]
    first_re, first_im = product(probe_re, probe_im, entry_patch[0], entry_patch[1])
    spread_re, spread_im = transform(first_re, first_im, ahead_re, ahead_im)
    second_re, second_im = product(spread_re, spread_im, leaving[0], leaving[1])
    far_re, far_im = transform(second_re, second_im, fwd_re, fwd_im)
    excess = far_re * far_re + far_im * far_im - intens[0]
    back_re, back_im = transform(excess * far_re, excess * far_im, fwd_re, -fwd_im)
    exit_re, exit_im = product(spread_re, -spread_im, back_re, back_im)
    mid_re, mid_im = product(leaving[0], -leaving[1], back_re, back_im)
    inner_re, inner_im = transform(mid_re, mid_im, behind_re, behind_im)
    entry_re, entry_im = product(probe_re, -probe_im, inner_re, inner_im)
    grad_re, grad_im = product(entry_patch[0], -entry_patch[1], inner_re, inner_im)
    patch_grad = jnp.stack([entry_re, entry_im, exit_re, exit_im]).astype(jnp.bfloat16)
    region = jnp.zeros((4, tile_span * tile_edge, tile_span * tile_edge), jnp.bfloat16)
    region = lax.dynamic_update_slice(region, patch_grad, (zero_idx, inner_y, inner_x))
    pieces = region.reshape(4, tile_span, tile_edge, tile_span, tile_edge).transpose(1, 3, 0, 2, 4)
    pieces = pieces.reshape(tile_span * tile_span, 4, tile_edge * tile_edge)
    outgoing = (
        jnp.zeros((owners * slots, 4, tile_edge * tile_edge), jnp.bfloat16)
        .at[flat_slot]
        .set(pieces)
    )
    outgoing = outgoing.reshape(owners, slots, 4, tile_edge * tile_edge)
    returned = lax.all_to_all(outgoing, "pos", split_axis=0, concat_axis=0, tiled=True)
    tile_ids = jnp.arange(tiles_dev, dtype=jnp.int32)
    selector = (
        (send_local.reshape(-1)[None, :] == tile_ids[:, None]) & send_live.reshape(-1)[None, :]
    ).astype(jnp.bfloat16)
    local_sum = jnp.dot(
        selector,
        returned.reshape(owners * slots, 4 * tile_edge * tile_edge),
        preferred_element_type=jnp.float32,
    )
    probe_part = jnp.stack([grad_re, grad_im])
    tile_total = lax.psum(local_sum, "tile")
    probe_total = lax.psum(probe_part, ("pos", "tile"))
    return (tile_total.reshape(tiles_dev, 4, tile_edge * tile_edge), probe_total)


def solution(mesh):
    in_specs = (P("pos", None, None), P(), P(), P(), P(("pos", "tile"), None, None))
    out_specs = (P("pos", None, None), P())
    return jax.shard_map(
        per_device, mesh=mesh, in_specs=in_specs, out_specs=out_specs, check_vma=False
    )
```

profile of v0, /device:TPU:6, one launch (start us, length us, event | category | flops | bytes accessed | tf_op | source)
XLA Modules:
  0.0 707.6 jit_solution(6085053265046931182)
XLA Ops:
  7.2 0.8 constant_dynamic-slice_fusion
  8.0 0.5 fusion.187
  10.5 0.8 reshape.470
  12.8 4.1 gather_fusion
  17.3 2.4 gather_fusion.2
  19.7 2.3 bitcast_select_fusion
  22.0 14.1 %all-to-all-start = ((bf16[64,1,4,4096]{3,2,1,0:T(4,128)(2,1)}), bf16[64,1,4,4096]{3,2,1,0:T(4,128)(2,1)S(1)}, u32[]{:S(2)}, u32[]{:S(2)}) async-start(bf16[64,1,4,4096]{3,2,1,0:T(4,128)(2,1)} %bitcast_select_fusion), calls=%async_computation | async-start | bytes 4194304 | tf_op jit(solution)/shard_map/all_to_all | solution.py:97
  38.9 0.7 gather_fusion.1
  43.9 41.0 %all-to-all-done = bf16[64,1,4,4096]{3,2,1,0:T(4,128)(2,1)S(1)} async-done(((bf16[64,1,4,4096]{3,2,1,0:T(4,128)(2,1)}), bf16[64,1,4,4096]{3,2,1,0:T(4,128)(2,1)S(1)}, u32[]{:S(2)}, u32[]{:S(2)}) %all-to-all-start) | async-done | bytes 2097184 | tf_op jit(solution)/shard_map/all_to_all | solution.py:97
  84.9 0.8 gather_fusion.3
  86.2 0.5 copy.17
  96.0 0.7 multiply_add_fusion
  98.5 2.9 dynamic_update_slice.3
  102.2 2.4 broadcast_in_dim.24
  104.6 2.5 scatter_fusion
  107.1 8.1 %all-to-all-start.1 = ((bf16[64,1,4,4096]{3,2,1,0:T(4,128)(2,1)}), bf16[64,1,4,4096]{3,2,1,0:T(4,128)(2,1)S(1)}, u32[]{:S(2)}, u32[]{:S(2)}) async-start(bf16[64,1,4,4096]{3,2,1,0:T(4,128)(2,1)} %bitcast.24), calls=%async_computation.1 | async-start | bytes 4194304 | tf_op jit(solution)/shard_map/all_to_all | solution.py:132
  115.3 0.7 pad_maximum_fusion.1
  116.0 48.2 %all-to-all-done.1 = bf16[64,1,4,4096]{3,2,1,0:T(4,128)(2,1)S(1)} async-done(((bf16[64,1,4,4096]{3,2,1,0:T(4,128)(2,1)}), bf16[64,1,4,4096]{3,2,1,0:T(4,128)(2,1)S(1)}, u32[]{:S(2)}, u32[]{:S(2)}) %all-to-all-start.1) | async-done | bytes 2097184 | tf_op jit(solution)/shard_map/all_to_all | solution.py:132
  164.2 1.2 copy.15
  165.9 2.2 reshape.479
  168.1 414.3 %all-reduce.5.cloned.1.call-done = f32[2,128,128]{2,1,0:T(8,128)} async-done(((f32[2,128,128]{2,1,0:T(8,128)}), f32[2,128,128]{2,1,0:T(8,128)}) %all-reduce.5.cloned.1.call-update) | async-done | bytes 131088 | tf_op jit(solution)/shard_map/psum | solution.py:144
  582.3 115.0 %all-reduce.3.cloned.1.call-done = f32[24,4,4096]{2,1,0:T(4,128)} async-done(((f32[24,4,4096]{2,1,0:T(4,128)}), f32[24,4,4096]{2,1,0:T(4,128)}) %all-reduce.3.cloned.1.call-update) | async-done | bytes 1572880 | tf_op jit(solution)/shard_map/psum | solution.py:143
  697.4 2.7 copy.22
  700.1 0.7 copy.23
  (85 shorter events, 18.1 us)
Async XLA Ops:
  7.2 10.2 %copy-start = (bf16[24,4,4096]{2,1,0:T(4,128)(2,1)S(1)}, bf16[24,4,4096]{2,1,0:T(4,128)(2,1)}, u32[]{:S(2)}) copy-start(bf16[24,4,4096]{2,1,0:T(4,128)(2,1)} %param.5) | copy-start | bytes 2359300
  7.2 5.6 copy-start.1
  22.0 62.9 %all-to-all-start = ((bf16[64,1,4,4096]{3,2,1,0:T(4,128)(2,1)}), bf16[64,1,4,4096]{3,2,1,0:T(4,128)(2,1)S(1)}, u32[]{:S(2)}, u32[]{:S(2)}) async-start(bf16[64,1,4,4096]{3,2,1,0:T(4,128)(2,1)} %bitcast_select_fusion), calls=%async_computation | async-start | bytes 4194304 | tf_op jit(solution)/shard_map/all_to_all | solution.py:97
  85.7 1.6 copy-start.2
  87.6 5.2 copy-start.4
  107.1 57.1 %all-to-all-start.1 = ((bf16[64,1,4,4096]{3,2,1,0:T(4,128)(2,1)}), bf16[64,1,4,4096]{3,2,1,0:T(4,128)(2,1)S(1)}, u32[]{:S(2)}, u32[]{:S(2)}) async-start(bf16[64,1,4,4096]{3,2,1,0:T(4,128)(2,1)} %bitcast.24), calls=%async_computation.1 | async-start | bytes 4194304 | tf_op jit(solution)/shard_map/all_to_all | solution.py:132
  115.2 467.1 %all-reduce.5.cloned.1.call-start = ((), (), s32[]{:S(2)}) async-start(), calls=%async_computation.3 | async-start | bytes 262144 | tf_op jit(solution)/shard_map/psum | solution.py:144
  116.0 581.4 %all-reduce.3.cloned.1.call-start = ((), (), s32[]{:S(2)}) async-start(), calls=%async_computation.2 | async-start | bytes 3145728 | tf_op jit(solution)/shard_map/psum | solution.py:143
  582.3 117.7 %copy-start.3 = (f32[2,128,128]{2,1,0:T(8,128)S(1)}, f32[2,128,128]{2,1,0:T(8,128)}, u32[]{:S(2)}) copy-start(f32[2,128,128]{2,1,0:T(8,128)} %all-reduce.5.cloned.1.call-done) | copy-start | bytes 393220
Sparse Core Ops, SparseCore 0:
  122.0 460.2 all-reduce.4
  585.4 111.9 all-reduce.2
where the time goes:
time: 708 us
  waiting for transfers between devices  619 us (87%)
  local copies, waits for them, and re-layouts  27.7 us (4%)
  starting transfers between devices  22.3 us (3%)
  between operations  19.9 us (3%)
  matrix products  15.1 us (2%)
    psum x1, waiting for transfers between devices, per_device(): probe_total = lax.psum(probe_part, ('pos', 'tile'))  414 us
    psum x1, waiting for transfers between devices, per_device(): tile_total = lax.psum(local_sum, 'tile')  115 us
    all_to_all x1, waiting for transfers between devices, per_device(): lax.all_to_all(outgoing, 'pos', split_axis=0, concat_axis=0, tiled=True)  48.2 us
    all_to_all x1, waiting for transfers between devices, per_device(): lax.all_to_all(chosen, 'pos', split_axis=0, concat_axis=0, tiled=True)  41 us
    dot_general x40, matrix products, matmul_hi(): jnp.dot(left_op, right_op, precision=lax.Precision.HIGHEST, preferred_ele...  14.7 us
  transfers between devices with their start and end apart: 4, of which 4 were waited for; matrix products, arithmetic and copies ran while one was open for 1% of the time, Pallas kernels for 0%

commit v1 on v0

--- a/solution.py
+++ b/solution.py
@@ -49,43 +49,52 @@
     return (left_re * right_re - left_im * right_im, left_re * right_im + left_im * right_re)
 
 
+def one_hot(index, size, live=None):
+    hit = index[:, None] == jnp.arange(size, dtype=index.dtype)[None, :]
+    if live is not None:
+        hit = hit & live[:, None]
+    return hit.astype(jnp.bfloat16)
+
+
 def per_device(obj_tiles, tile_map, offsets, probe, intens):
     owners = lax.axis_size("pos")
     layers = lax.axis_size("tile")
     me_pos = lax.axis_index("pos")
     me_tile = lax.axis_index("tile")
     tiles_dev = obj_tiles.shape[0]
+    n_comps = obj_tiles.shape[1]
     tile_edge = TS
     width_px = probe.shape[-1]
     tile_span = width_px // tile_edge + 1
-    cols_own = owners // OWN_R
-    cols_cap = (tile_span + cols_own - 1) // cols_own
-    slots = (tile_span + OWN_R - 1) // OWN_R * cols_cap
+    own_c = owners // OWN_R
+    grid_r, grid_c = tile_map.shape
     span_idx = jnp.arange(tile_span, dtype=jnp.int32)
-    slot_grid = (span_idx[:, None] // OWN_R * cols_cap + span_idx[None, :] // cols_own).reshape(-1)
 
-    def footprint(corner):
-        row_ids = corner[0] // tile_edge + span_idx
-        col_ids = corner[1] // tile_edge + span_idx
-        store_id = tile_map[row_ids[:, None], col_ids[None, :]].reshape(-1)
-        owner_id = store_id // tiles_dev
-        return (owner_id, store_id - owner_id * tiles_dev)
+    mine = (tile_map // tiles_dev) == me_pos
+    class_r = jnp.sum(jnp.where(jnp.any(mine[:OWN_R], axis=1), jnp.arange(OWN_R), 0))
+    class_c = jnp.sum(jnp.where(jnp.any(mine[:, :own_c], axis=0), jnp.arange(own_c), 0))
+    blocks = tile_map.reshape(grid_r // OWN_R, OWN_R, grid_c // own_c, own_c)
+    my_blocks = lax.dynamic_index_in_dim(blocks, class_r, 1, keepdims=False)
+    my_blocks = lax.dynamic_index_in_dim(my_blocks, class_c, 2, keepdims=False)
+    my_blocks = my_blocks - me_pos * tiles_dev
 
     by_device = offsets.reshape(owners, layers, 2)
     peer_corners = lax.dynamic_index_in_dim(by_device, me_tile, 1, keepdims=False)
-    peer_owner, peer_local = jax.vmap(footprint)(peer_corners)
-    slot_ids = jnp.arange(slots, dtype=jnp.int32)
-    matches = (peer_owner == me_pos)[:, :, None] & (
-        slot_grid[None, :, None] == slot_ids[None, None, :]
-    )
-    send_local = jnp.sum(jnp.where(matches, peer_local[:, :, None], 0), axis=1)
-    send_live = jnp.any(matches, axis=1)
-    chosen = jnp.where(
-        send_live[:, :, None, None], obj_tiles[send_local], jnp.zeros((), obj_tiles.dtype)
-    )
+    peer_r = peer_corners[:, 0] // tile_edge
+    peer_c = peer_corners[:, 1] // tile_edge
+    step_r = (class_r - peer_r) % OWN_R
+    step_c = (class_c - peer_c) % own_c
+    send_live = (step_r < tile_span) & (step_c < tile_span)
+    hit_r = (peer_r + jnp.minimum(step_r, tile_span - 1)) // OWN_R
+    hit_c = (peer_c + jnp.minimum(step_c, tile_span - 1)) // own_c
+    send_local = my_blocks.reshape(-1)[hit_r * (grid_c // own_c) + hit_c]
+    send_sel = one_hot(send_local, tiles_dev, send_live)
+    chosen = obj_tiles[send_local]
+
     my_corner = lax.dynamic_index_in_dim(offsets, me_pos * layers + me_tile, 0, keepdims=False)
-    my_owner, my_local = footprint(my_corner)
-    flat_slot = my_owner * slots + slot_grid
+    row_ids = my_corner[0] // tile_edge + span_idx
+    col_ids = my_corner[1] // tile_edge + span_idx
+    my_owner = (tile_map[row_ids[:, None], col_ids[None, :]] // tiles_dev).reshape(-1)
     inner_y = my_corner[0] % tile_edge
     inner_x = my_corner[1] % tile_edge
     zero_idx = jnp.zeros((), jnp.int32)
@@ -95,8 +104,7 @@
     probe_re = probe[0]
     probe_im = probe[1]
     received = lax.all_to_all(chosen, "pos", split_axis=0, concat_axis=0, tiled=True)
-    n_comps = received.shape[2]
-    pieces = received.reshape(owners * slots, n_comps, tile_edge * tile_edge)[flat_slot]
+    pieces = received[my_owner]
     region = pieces.reshape(tile_span, tile_span, n_comps, tile_edge, tile_edge).transpose(
         2, 0, 3, 1, 4
     )
@@ -119,30 +127,40 @@
     entry_re, entry_im = product(probe_re, -probe_im, inner_re, inner_im)
     grad_re, grad_im = product(entry_patch[0], -entry_patch[1], inner_re, inner_im)
     patch_grad = jnp.stack([entry_re, entry_im, exit_re, exit_im]).astype(jnp.bfloat16)
-    region = jnp.zeros((4, tile_span * tile_edge, tile_span * tile_edge), jnp.bfloat16)
-    region = lax.dynamic_update_slice(region, patch_grad, (zero_idx, inner_y, inner_x))
-    pieces = region.reshape(4, tile_span, tile_edge, tile_span, tile_edge).transpose(1, 3, 0, 2, 4)
-    pieces = pieces.reshape(tile_span * tile_span, 4, tile_edge * tile_edge)
-    outgoing = (
-        jnp.zeros((owners * slots, 4, tile_edge * tile_edge), jnp.bfloat16)
-        .at[flat_slot]
-        .set(pieces)
+
+    region_px = tile_span * tile_edge
+    shift_y = one_hot(jnp.arange(region_px, dtype=jnp.int32) - inner_y, width_px)
+    shift_x = one_hot(jnp.arange(region_px, dtype=jnp.int32) - inner_x, width_px)
+    shift_y = shift_y.reshape(tile_span, tile_edge, width_px)
+    shift_x = shift_x.reshape(tile_span, tile_edge, width_px)
+    rows_cut = jnp.einsum("irk,ckm->cirm", shift_y, patch_grad, preferred_element_type=jnp.float32)
+    rows_cut = rows_cut.astype(jnp.bfloat16)
+    tiles_cut = jnp.einsum("cirm,jsm->ijcrs", rows_cut, shift_x, preferred_element_type=jnp.float32)
+    tiles_cut = tiles_cut.astype(jnp.bfloat16).reshape(
+        tile_span * tile_span, n_comps, tile_edge * tile_edge
     )
-    outgoing = outgoing.reshape(owners, slots, 4, tile_edge * tile_edge)
+    slot_of = jnp.sum(
+        jnp.where(my_owner[None, :] == jnp.arange(owners)[:, None], jnp.arange(my_owner.size), 0),
+        axis=1,
+    )
+    outgoing = tiles_cut[slot_of]
     returned = lax.all_to_all(outgoing, "pos", split_axis=0, concat_axis=0, tiled=True)
-    tile_ids = jnp.arange(tiles_dev, dtype=jnp.int32)
-    selector = (
-        (send_local.reshape(-1)[None, :] == tile_ids[:, None]) & send_live.reshape(-1)[None, :]
-    ).astype(jnp.bfloat16)
-    local_sum = jnp.dot(
-        selector,
-        returned.reshape(owners * slots, 4 * tile_edge * tile_edge),
-        preferred_element_type=jnp.float32,
-    )
+    local_sum = jnp.einsum("nk,ncp->kcp", send_sel, returned, preferred_element_type=jnp.float32)
     probe_part = jnp.stack([grad_re, grad_im])
     tile_total = lax.psum(local_sum, "tile")
-    probe_total = lax.psum(probe_part, ("pos", "tile"))
-    return (tile_total.reshape(tiles_dev, 4, tile_edge * tile_edge), probe_total)
+    probe_total = reduce_probe(probe_part, owners, layers)
+    return (tile_total, probe_total)
+
+
+def reduce_probe(probe_part, owners, layers):
+    piece_len = probe_part.size // owners
+    pieces = probe_part.reshape(owners, piece_len)
+    mine = jnp.sum(lax.all_to_all(pieces, "pos", 0, 0, tiled=True), axis=0)
+    spread = jnp.broadcast_to(mine[None], (layers, piece_len))
+    mine = jnp.sum(lax.all_to_all(spread, "tile", 0, 0, tiled=True), axis=0)
+    spread = jnp.broadcast_to(mine[None], (owners, piece_len))
+    gathered = lax.all_to_all(spread, "pos", 0, 0, tiled=True)
+    return gathered.reshape(probe_part.shape)
 
 
 def solution(mesh):

time: 708 us -> 302 us (0.43)
  waiting for transfers between devices: 619 us -> 109 us
  blocking collectives: 0 us -> 111 us
  local copies, waits for them, and re-layouts: 27.7 us -> 19.2 us
  starting transfers between devices: 22.3 us -> 14.2 us
    psum x1 -> x0, waiting for transfers between devices: 414 us -> none  [per_device(): probe_total = lax.psum(probe_part, ('pos', 'tile'))]
    all_to_all x0 -> x4, blocking collectives: none -> 111 us  [the longest x1 56.9 us: per_device(): lax.all_to_all(outgoing, 'pos', split_axis=0, concat_axis=0, tiled=True)]
    psum x1, waiting for transfers between devices: 115 us -> 64.5 us  [per_device(): tile_total = lax.psum(local_sum, 'tile')]
    all_to_all x1 -> x0, waiting for transfers between devices: 48.2 us -> none  [per_device(): lax.all_to_all(outgoing, 'pos', split_axis=0, concat_axis=0, tiled=True)]
    all_to_all x1 -> x0, starting transfers between devices: 8.09 us -> none  [per_device(): lax.all_to_all(outgoing, 'pos', split_axis=0, concat_axis=0, tiled=True)]
  transfers between devices with their start and end apart: 4 -> 2, of which waited for: 4 -> 2; matrix products, arithmetic and copies ran while one was open for 1% -> 1% of each run, Pallas kernels for 0% -> 0%
where the time goes in v1:
time: 302 us; the launch traced here: 301 us
  blocking collectives  111 us (37%)
  waiting for transfers between devices  109 us (36%)
  between operations  23.7 us (8%)
  local copies, waits for them, and re-layouts  19.2 us (6%)
  matrix products  18.7 us (6%)
  starting transfers between devices  14.2 us (5%)
  other arithmetic  5.02 us (2%)
    psum x1, waiting for transfers between devices, per_device(): tile_total = lax.psum(local_sum, 'tile')  64.5 us
    all_to_all x1, blocking collectives, per_device(): lax.all_to_all(outgoing, 'pos', split_axis=0, concat_axis=0, tiled=True)  56.9 us
    all_to_all x1, waiting for transfers between devices, per_device(): lax.all_to_all(chosen, 'pos', split_axis=0, concat_axis=0, tiled=True)  44.6 us
    all_to_all x1, blocking collectives, reduce_probe(): mine = jnp.sum(lax.all_to_all(spread, 'tile', 0, 0, tiled=True), axis=0)  22.2 us
    all_to_all x1, blocking collectives, reduce_probe(): mine = jnp.sum(lax.all_to_all(pieces, 'pos', 0, 0, tiled=True), axis=0)  16.8 us
    all_to_all x1, blocking collectives, reduce_probe(): gathered = lax.all_to_all(spread, 'pos', 0, 0, tiled=True)  15.3 us
    dot_general x40, matrix products, matmul_hi(): jnp.dot(left_op, right_op, precision=lax.Precision.HIGHEST, preferred_ele...  14.7 us
    all_to_all x1, starting transfers between devices, per_device(): lax.all_to_all(chosen, 'pos', split_axis=0, concat_axis=0, tiled=True)  13.9 us
  transfers between devices with their start and end apart: 2, of which 2 were waited for; matrix products, arithmetic and copies ran while one was open for 1% of the time, Pallas kernels for 0%

profile of v1, /device:TPU:6, one launch (start us, length us, event | category | flops | bytes accessed | tf_op | source)
XLA Modules:
  0.0 301.0 jit_solution(6493998128225711411)
XLA Ops:
  7.2 0.8 constant_dynamic-slice_fusion
  13.7 0.8 reshape.246
  14.5 0.7 fusion.63
  15.4 0.6 select_reduce_fusion.1
  16.1 0.6 select_reduce_fusion.2
  19.3 0.8 reshape.308
  20.3 1.4 gather_fusion.2
  22.0 1.3 and_bitcast_fusion
  25.2 0.9 fusion.213
  26.2 0.8 gather_fusion
  27.0 3.6 %gather_fusion.1 = bf16[64,4,4096]{2,1,0:T(4,128)(2,1)} fusion(bf16[24,4,4096]{2,1,0:T(4,128)(2,1)S(1)} %copy-done, s32[1024]{0:T(1024)S(1)} %pad_clamp_fusion.2), kind=kCustom, calls=%fused_computation.1 | custom fusion | bytes 4194560 | tf_op jit(solution)/shard_map/gather | solution.py:92
  30.6 13.9 %all-to-all-start = ((bf16[64,4,4096]{2,1,0:T(4,128)(2,1)}), bf16[64,4,4096]{2,1,0:T(4,128)(2,1)S(1)}, u32[]{:S(2)}, u32[]{:S(2)}) async-start(bf16[64,4,4096]{2,1,0:T(4,128)(2,1)} %gather_fusion.1), calls=%async_computation | async-start | bytes 4194304 | tf_op jit(solution)/shard_map/all_to_all | solution.py:106
  48.9 44.6 %all-to-all-done = bf16[64,4,4096]{2,1,0:T(4,128)(2,1)S(1)} async-done(((bf16[64,4,4096]{2,1,0:T(4,128)(2,1)}), bf16[64,4,4096]{2,1,0:T(4,128)(2,1)S(1)}, u32[]{:S(2)}, u32[]{:S(2)}) %all-to-all-start) | async-done | bytes 2097184 | tf_op jit(solution)/shard_map/all_to_all | solution.py:106
  93.5 0.8 gather_fusion.3
  104.6 0.6 multiply_add_fusion
  108.2 2.4 gather_fusion.4
  110.6 56.9 %all_to_all.31 = bf16[64,4,4096]{2,1,0:T(4,128)(2,1)S(1)} all-to-all(bf16[64,4,4096]{2,1,0:T(4,128)(2,1)S(1)} %gather_fusion.4), channel_id=1, replica_groups=mesh['pos'=64,'tile'=12] {'pos'}, dimensions={0} | all-to-all | bytes 4194304 | tf_op jit(solution)/shard_map/all_to_all | solution.py:147
  167.5 3.5 %fusion = f32[24,4,4096]{2,0,1:T(8,128)} fusion(bf16[64,4,4096]{2,1,0:T(4,128)(2,1)S(1)} %all_to_all.31, s32[64]{0:T(128)S(1)} %gather_fusion, pred[64]{0:T(512)(128)(4,1)S(1)} %get-tuple-element.14), kind=kOutput, calls=%fused_computation.5 | convolution fusion | flops 50334720 | bytes 3670336 | tf_op jit(solution)/shard_map/nk,ncp->kcp/dot_general | solution.py:148
  171.0 16.8 %all_to_all.32 = f32[64,1,512]{2,1,0:T(1,128)S(1)} all-to-all(f32[64,1,512]{2,1,0:T(1,128)S(1)} %bitcast.209), channel_id=1, replica_groups=mesh['pos'=64,'tile'=12] {'pos'}, dimensions={0} | all-to-all | bytes 262144 | tf_op jit(solution)/shard_map/all_to_all | solution.py:158
  187.9 22.2 %all_to_all.33 = f32[12,1,512]{2,1,0:T(1,128)S(1)} all-to-all(f32[12,1,512]{2,1,0:T(1,128)S(1)} %broadcast_in_dim.24), channel_id=1, replica_groups=mesh['pos'=64,'tile'=12] {'tile'}, dimensions={0} | all-to-all | bytes 49152 | tf_op jit(solution)/shard_map/all_to_all | solution.py:160
  210.2 15.3 %all_to_all.34 = f32[64,1,512]{2,1,0:T(1,128)S(1)} all-to-all(f32[64,1,512]{2,1,0:T(1,128)S(1)} %broadcast_in_dim.25), channel_id=1, replica_groups=mesh['pos'=64,'tile'=12] {'pos'}, dimensions={0} | all-to-all | bytes 262144 | tf_op jit(solution)/shard_map/all_to_all | solution.py:162
  225.4 64.5 %all-reduce.2.cloned.1.call-done = f32[24,4,4096]{2,0,1:T(8,128)} async-done(((f32[24,4,4096]{2,0,1:T(8,128)}), f32[24,4,4096]{2,0,1:T(8,128)}) %all-reduce.2.cloned.1.call-update) | async-done | bytes 1572880 | tf_op jit(solution)/shard_map/psum | solution.py:150
  290.0 3.6 %copy.43 = f32[24,4,4096]{2,1,0:T(4,128)} copy(f32[24,4,4096]{2,0,1:T(8,128)} %all-reduce.2.cloned.1.call-done) | data formatting | bytes 3145728
  293.5 0.7 copy.56
  (82 shorter events, 19.3 us)
Async XLA Ops:
  7.2 19.8 %copy-start = (bf16[24,4,4096]{2,1,0:T(4,128)(2,1)S(1)}, bf16[24,4,4096]{2,1,0:T(4,128)(2,1)}, u32[]{:S(2)}) copy-start(bf16[24,4,4096]{2,1,0:T(4,128)(2,1)} %param.5) | copy-start | bytes 2359300
  30.6 62.9 %all-to-all-start = ((bf16[64,4,4096]{2,1,0:T(4,128)(2,1)}), bf16[64,4,4096]{2,1,0:T(4,128)(2,1)S(1)}, u32[]{:S(2)}, u32[]{:S(2)}) async-start(bf16[64,4,4096]{2,1,0:T(4,128)(2,1)} %gather_fusion.1), calls=%async_computation | async-start | bytes 4194304 | tf_op jit(solution)/shard_map/all_to_all | solution.py:106
  44.5 245.5 %all-reduce.2.cloned.1.call-start = ((), (), s32[]{:S(2)}) async-start(), calls=%async_computation.5 | async-start | bytes 3145728 | tf_op jit(solution)/shard_map/psum | solution.py:150
  94.3 1.6 copy-start.1
  96.1 5.2 %copy-start.2 = (f32[1,128,128]{2,1,0:T(8,128)S(1)}, f32[1,128,128]{2,1,0:T(8,128)}, u32[]{:S(2)}) copy-start(f32[1,128,128]{2,1,0:T(8,128)} %param.9) | copy-start | bytes 196612
Sparse Core Ops, SparseCore 0:
  171.1 118.8 all-reduce.1

commit v2 on v1

--- a/solution.py
+++ b/solution.py
@@ -71,24 +71,19 @@
     span_idx = jnp.arange(tile_span, dtype=jnp.int32)
 
     mine = (tile_map // tiles_dev) == me_pos
-    class_r = jnp.sum(jnp.where(jnp.any(mine[:OWN_R], axis=1), jnp.arange(OWN_R), 0))
-    class_c = jnp.sum(jnp.where(jnp.any(mine[:, :own_c], axis=0), jnp.arange(own_c), 0))
-    blocks = tile_map.reshape(grid_r // OWN_R, OWN_R, grid_c // own_c, own_c)
-    my_blocks = lax.dynamic_index_in_dim(blocks, class_r, 1, keepdims=False)
-    my_blocks = lax.dynamic_index_in_dim(my_blocks, class_c, 2, keepdims=False)
-    my_blocks = my_blocks - me_pos * tiles_dev
-
+    local_plus = jnp.where(mine, tile_map - me_pos * tiles_dev + 1, 0).astype(jnp.bfloat16)
     by_device = offsets.reshape(owners, layers, 2)
     peer_corners = lax.dynamic_index_in_dim(by_device, me_tile, 1, keepdims=False)
-    peer_r = peer_corners[:, 0] // tile_edge
-    peer_c = peer_corners[:, 1] // tile_edge
-    step_r = (class_r - peer_r) % OWN_R
-    step_c = (class_c - peer_c) % own_c
-    send_live = (step_r < tile_span) & (step_c < tile_span)
-    hit_r = (peer_r + jnp.minimum(step_r, tile_span - 1)) // OWN_R
-    hit_c = (peer_c + jnp.minimum(step_c, tile_span - 1)) // own_c
-    send_local = my_blocks.reshape(-1)[hit_r * (grid_c // own_c) + hit_c]
-    send_sel = one_hot(send_local, tiles_dev, send_live)
+    peer_r = peer_corners[:, 0:1] // tile_edge
+    peer_c = peer_corners[:, 1:2] // tile_edge
+    grid_rows = jnp.arange(grid_r, dtype=jnp.int32)[None, :]
+    grid_cols = jnp.arange(grid_c, dtype=jnp.int32)[None, :]
+    row_in = ((grid_rows >= peer_r) & (grid_rows < peer_r + tile_span)).astype(jnp.bfloat16)
+    col_in = ((grid_cols >= peer_c) & (grid_cols < peer_c + tile_span)).astype(jnp.float32)
+    by_col = jnp.dot(row_in, local_plus, preferred_element_type=jnp.float32)
+    found = jnp.sum(by_col * col_in, axis=1).astype(jnp.int32)
+    send_live = found > 0
+    send_local = jnp.maximum(found - 1, 0)
     chosen = obj_tiles[send_local]
 
     my_corner = lax.dynamic_index_in_dim(offsets, me_pos * layers + me_tile, 0, keepdims=False)
@@ -145,11 +140,16 @@
     )
     outgoing = tiles_cut[slot_of]
     returned = lax.all_to_all(outgoing, "pos", split_axis=0, concat_axis=0, tiled=True)
-    local_sum = jnp.einsum("nk,ncp->kcp", send_sel, returned, preferred_element_type=jnp.float32)
+    selector = one_hot(send_local, tiles_dev, send_live).T
+    local_sum = jnp.dot(
+        selector,
+        returned.reshape(owners, n_comps * tile_edge * tile_edge),
+        preferred_element_type=jnp.float32,
+    )
     probe_part = jnp.stack([grad_re, grad_im])
     tile_total = lax.psum(local_sum, "tile")
     probe_total = reduce_probe(probe_part, owners, layers)
-    return (tile_total, probe_total)
+    return (tile_total.reshape(tiles_dev, n_comps, tile_edge * tile_edge), probe_total)
 
 
 def reduce_probe(probe_part, owners, layers):

time: 302 us -> 285 us (0.944)
  blocking collectives: 111 us -> 54.2 us
  waiting for transfers between devices: 109 us -> 151 us
  starting transfers between devices: 14.2 us -> 22.4 us
  other arithmetic: 5.02 us -> 0.69 us
  between operations: 23.7 us -> 19.8 us
    all_to_all x1 -> x0, blocking collectives: 56.9 us -> none  [per_device(): lax.all_to_all(outgoing, 'pos', split_axis=0, concat_axis=0, tiled=True)]
    all_to_all x0 -> x1, waiting for transfers between devices: none -> 48.9 us  [per_device(): lax.all_to_all(outgoing, 'pos', split_axis=0, concat_axis=0, tiled=True)]
    all_to_all x0 -> x1, starting transfers between devices: none -> 8.12 us  [per_device(): lax.all_to_all(outgoing, 'pos', split_axis=0, concat_axis=0, tiled=True)]
    all_to_all x1, waiting for transfers between devices: 44.6 us -> 37.2 us  [per_device(): lax.all_to_all(chosen, 'pos', split_axis=0, concat_axis=0, tiled=True)]
  transfers between devices with their start and end apart: 2 -> 3, of which waited for: 2 -> 3; matrix products, arithmetic and copies ran while one was open for 1% -> 2% of each run, Pallas kernels for 0% -> 0%
where the time goes in v2:
time: 285 us; the launch traced here: 284 us
  waiting for transfers between devices  151 us (53%)
  blocking collectives  54.2 us (19%)
  starting transfers between devices  22.4 us (8%)
  local copies, waits for them, and re-layouts  20.1 us (7%)
  between operations  19.8 us (7%)
  matrix products  16.8 us (6%)
    psum x1, waiting for transfers between devices, per_device(): tile_total = lax.psum(local_sum, 'tile')  64.5 us
    all_to_all x1, waiting for transfers between devices, per_device(): lax.all_to_all(outgoing, 'pos', split_axis=0, concat_axis=0, tiled=True)  48.9 us
    all_to_all x1, waiting for transfers between devices, per_device(): lax.all_to_all(chosen, 'pos', split_axis=0, concat_axis=0, tiled=True)  37.2 us
    all_to_all x1, blocking collectives, reduce_probe(): mine = jnp.sum(lax.all_to_all(spread, 'tile', 0, 0, tiled=True), axis=0)  22.2 us
    all_to_all x1, blocking collectives, reduce_probe(): mine = jnp.sum(lax.all_to_all(pieces, 'pos', 0, 0, tiled=True), axis=0)  16.8 us
    all_to_all x1, blocking collectives, reduce_probe(): gathered = lax.all_to_all(spread, 'pos', 0, 0, tiled=True)  15.3 us
    dot_general x40, matrix products, matmul_hi(): jnp.dot(left_op, right_op, precision=lax.Precision.HIGHEST, preferred_ele...  14.7 us
    all_to_all x1, starting transfers between devices, per_device(): lax.all_to_all(chosen, 'pos', split_axis=0, concat_axis=0, tiled=True)  14.2 us
  transfers between devices with their start and end apart: 3, of which 3 were waited for; matrix products, arithmetic and copies ran while one was open for 2% of the time, Pallas kernels for 0%

profile of v2, /device:TPU:6, one launch (start us, length us, event | category | flops | bytes accessed | tf_op | source)
XLA Modules:
  0.0 284.5 jit_solution(16423452267284814567)
XLA Ops:
  7.2 0.9 reshape.250
  8.3 1.0 fusion.2
  9.3 3.6 %gather_fusion = bf16[64,4,4096]{2,1,0:T(4,128)(2,1)} fusion(bf16[24,4,4096]{2,1,0:T(4,128)(2,1)S(1)} %copy-done, s32[1024]{0:T(1024)S(1)} %pad_clamp_fusion.2), kind=kCustom, calls=%fused_computation | custom fusion | bytes 4194560 | tf_op jit(solution)/shard_map/gather | solution.py:87
  12.8 14.2 %all-to-all-start = ((bf16[64,4,4096]{2,1,0:T(4,128)(2,1)}), bf16[64,4,4096]{2,1,0:T(4,128)(2,1)S(1)}, u32[]{:S(2)}, u32[]{:S(2)}) async-start(bf16[64,4,4096]{2,1,0:T(4,128)(2,1)} %gather_fusion), calls=%async_computation | async-start | bytes 4194304 | tf_op jit(solution)/shard_map/all_to_all | solution.py:101
  27.1 0.8 constant_dynamic-slice_fusion
  27.9 0.5 fusion.216
  33.8 0.7 gather_fusion.1
  38.7 37.2 %all-to-all-done = bf16[64,4,4096]{2,1,0:T(4,128)(2,1)S(1)} async-done(((bf16[64,4,4096]{2,1,0:T(4,128)(2,1)}), bf16[64,4,4096]{2,1,0:T(4,128)(2,1)S(1)}, u32[]{:S(2)}, u32[]{:S(2)}) %all-to-all-start) | async-done | bytes 2097184 | tf_op jit(solution)/shard_map/all_to_all | solution.py:101
  75.9 0.8 gather_fusion.2
  77.2 0.5 copy.23
  87.0 0.7 multiply_add_fusion
  89.4 0.6 fusion
  90.7 3.6 %gather_fusion.3 = bf16[64,4,4096]{2,1,0:T(4,128)(2,1)} fusion(bf16[9,4,4096]{2,1,0:T(4,128)(2,1)S(1)} %reshape.253, s32[1024]{0:T(1024)S(1)} %pad_clamp_fusion), kind=kCustom, calls=%fused_computation.3 | custom fusion | bytes 4194560 | tf_op jit(solution)/shard_map/gather | solution.py:141
  94.3 8.1 %all-to-all-start.1 = ((bf16[64,4,4096]{2,1,0:T(4,128)(2,1)}), bf16[64,4,4096]{2,1,0:T(4,128)(2,1)S(1)}, u32[]{:S(2)}, u32[]{:S(2)}) async-start(bf16[64,4,4096]{2,1,0:T(4,128)(2,1)} %gather_fusion.3), calls=%async_computation.1 | async-start | bytes 4194304 | tf_op jit(solution)/shard_map/all_to_all | solution.py:142
  102.5 48.9 %all-to-all-done.1 = bf16[64,4,4096]{2,1,0:T(4,128)(2,1)S(1)} async-done(((bf16[64,4,4096]{2,1,0:T(4,128)(2,1)}), bf16[64,4,4096]{2,1,0:T(4,128)(2,1)S(1)}, u32[]{:S(2)}, u32[]{:S(2)}) %all-to-all-start.1) | async-done | bytes 2097184 | tf_op jit(solution)/shard_map/all_to_all | solution.py:142
  151.3 1.2 copy.21
  152.6 0.5 fusion.65
  153.1 2.2 reshape.255
  155.4 16.8 %all_to_all.31 = f32[64,1,512]{2,1,0:T(1,128)S(1)} all-to-all(f32[64,1,512]{2,1,0:T(1,128)S(1)} %bitcast.208), channel_id=1, replica_groups=mesh['pos'=64,'tile'=12] {'pos'}, dimensions={0} | all-to-all | bytes 262144 | tf_op jit(solution)/shard_map/all_to_all | solution.py:158
  172.3 22.2 %all_to_all.32 = f32[12,1,512]{2,1,0:T(1,128)S(1)} all-to-all(f32[12,1,512]{2,1,0:T(1,128)S(1)} %broadcast_in_dim.20), channel_id=1, replica_groups=mesh['pos'=64,'tile'=12] {'tile'}, dimensions={0} | all-to-all | bytes 49152 | tf_op jit(solution)/shard_map/all_to_all | solution.py:160
  194.6 15.3 %all_to_all.33 = f32[64,1,512]{2,1,0:T(1,128)S(1)} all-to-all(f32[64,1,512]{2,1,0:T(1,128)S(1)} %broadcast_in_dim.21), channel_id=1, replica_groups=mesh['pos'=64,'tile'=12] {'pos'}, dimensions={0} | all-to-all | bytes 262144 | tf_op jit(solution)/shard_map/all_to_all | solution.py:162
  209.8 64.5 %all-reduce.2.cloned.1.call-done = f32[24,4,4096]{2,1,0:T(4,128)} async-done(((f32[24,4,4096]{2,1,0:T(4,128)}), f32[24,4,4096]{2,1,0:T(4,128)}) %all-reduce.2.cloned.1.call-update) | async-done | bytes 1572880 | tf_op jit(solution)/shard_map/psum | solution.py:150
  274.3 2.7 copy.26
  277.0 0.7 copy.27
  (77 shorter events, 16.8 us)
Async XLA Ops:
  7.2 2.1 copy-start
  12.8 20.9 %copy-start.1 = (s32[32,48]{1,0:T(8,128)S(1)}, s32[32,48]{1,0:T(8,128)}, u32[]{:S(2)}) copy-start(s32[32,48]{1,0:T(8,128)} %param.6) | copy-start | bytes 18436
  12.8 63.0 %all-to-all-start = ((bf16[64,4,4096]{2,1,0:T(4,128)(2,1)}), bf16[64,4,4096]{2,1,0:T(4,128)(2,1)S(1)}, u32[]{:S(2)}, u32[]{:S(2)}) async-start(bf16[64,4,4096]{2,1,0:T(4,128)(2,1)} %gather_fusion), calls=%async_computation | async-start | bytes 4194304 | tf_op jit(solution)/shard_map/all_to_all | solution.py:101
  76.7 1.6 copy-start.2
  78.5 5.2 %copy-start.3 = (f32[1,128,128]{2,1,0:T(8,128)S(1)}, f32[1,128,128]{2,1,0:T(8,128)}, u32[]{:S(2)}) copy-start(f32[1,128,128]{2,1,0:T(8,128)} %param.9) | copy-start | bytes 196612
  94.3 57.1 %all-to-all-start.1 = ((bf16[64,4,4096]{2,1,0:T(4,128)(2,1)}), bf16[64,4,4096]{2,1,0:T(4,128)(2,1)S(1)}, u32[]{:S(2)}, u32[]{:S(2)}) async-start(bf16[64,4,4096]{2,1,0:T(4,128)(2,1)} %gather_fusion.3), calls=%async_computation.1 | async-start | bytes 4194304 | tf_op jit(solution)/shard_map/all_to_all | solution.py:142
  102.4 171.9 %all-reduce.2.cloned.1.call-start = ((), (), s32[]{:S(2)}) async-start(), calls=%async_computation.5 | async-start | bytes 3145728 | tf_op jit(solution)/shard_map/psum | solution.py:150
Sparse Core Ops, SparseCore 0:
  155.5 118.7 all-reduce.1

commit v3 on v2

--- a/solution.py
+++ b/solution.py
@@ -40,9 +40,25 @@
     return complex_matmul(fwd_re, -fwd_im, scaled_re, scaled_im)
 
 
-def transform(part_re, part_im, table_re, table_im):
-    mid_re, mid_im = complex_matmul(part_re, part_im, table_re, table_im)
-    return complex_matmul(table_re, table_im, mid_re, mid_im)
+def stacked_table(table_re, table_im):
+    column = jnp.concatenate([table_re, table_im], axis=0)
+    block = jnp.concatenate(
+        [jnp.concatenate([table_re, -table_im], axis=1), jnp.concatenate([table_im, table_re], axis=1)],
+        axis=0,
+    )
+    return column, block
+
+
+def transform(part_re, part_im, table):
+    column, block = table
+    left = jnp.concatenate(
+        [jnp.concatenate([part_re, -part_im], axis=1), jnp.concatenate([part_im, part_re], axis=1)],
+        axis=0,
+    )
+    mid = matmul_hi(left, column)
+    out = matmul_hi(block, mid)
+    width = part_re.shape[0]
+    return out[:width], out[width:]
 
 
 def product(left_re, left_im, right_re, right_im):
@@ -96,6 +112,10 @@
     fwd_re, fwd_im = spectral_tables(width_px)
     ahead_re, ahead_im = propagation_matrix(width_px, fwd_re, fwd_im, 1.0)
     behind_re, behind_im = propagation_matrix(width_px, fwd_re, fwd_im, -1.0)
+    ahead = stacked_table(ahead_re, ahead_im)
+    forward = stacked_table(fwd_re, fwd_im)
+    backward = stacked_table(fwd_re, -fwd_im)
+    behind = stacked_table(behind_re, behind_im)
     probe_re = probe[0]
     probe_im = probe[1]
     received = lax.all_to_all(chosen, "pos", split_axis=0, concat_axis=0, tiled=True)
@@ -111,14 +131,14 @@
     entry_patch = fetched[:2]
     leaving = fetched[2:]
     first_re, first_im = product(probe_re, probe_im, entry_patch[0], entry_patch[1])
-    spread_re, spread_im = transform(first_re, first_im, ahead_re, ahead_im)
+    spread_re, spread_im = transform(first_re, first_im, ahead)
     second_re, second_im = product(spread_re, spread_im, leaving[0], leaving[1])
-    far_re, far_im = transform(second_re, second_im, fwd_re, fwd_im)
+    far_re, far_im = transform(second_re, second_im, forward)
     excess = far_re * far_re + far_im * far_im - intens[0]
-    back_re, back_im = transform(excess * far_re, excess * far_im, fwd_re, -fwd_im)
+    back_re, back_im = transform(excess * far_re, excess * far_im, backward)
     exit_re, exit_im = product(spread_re, -spread_im, back_re, back_im)
     mid_re, mid_im = product(leaving[0], -leaving[1], back_re, back_im)
-    inner_re, inner_im = transform(mid_re, mid_im, behind_re, behind_im)
+    inner_re, inner_im = transform(mid_re, mid_im, behind)
     entry_re, entry_im = product(probe_re, -probe_im, inner_re, inner_im)
     grad_re, grad_im = product(entry_patch[0], -entry_patch[1], inner_re, inner_im)
     patch_grad = jnp.stack([entry_re, entry_im, exit_re, exit_im]).astype(jnp.bfloat16)
@@ -134,11 +154,9 @@
     tiles_cut = tiles_cut.astype(jnp.bfloat16).reshape(
         tile_span * tile_span, n_comps, tile_edge * tile_edge
     )
-    slot_of = jnp.sum(
-        jnp.where(my_owner[None, :] == jnp.arange(owners)[:, None], jnp.arange(my_owner.size), 0),
-        axis=1,
+    outgoing = jnp.zeros((owners, n_comps, tile_edge * tile_edge), jnp.bfloat16).at[my_owner].set(
+        tiles_cut
     )
-    outgoing = tiles_cut[slot_of]
     returned = lax.all_to_all(outgoing, "pos", split_axis=0, concat_axis=0, tiled=True)
     selector = one_hot(send_local, tiles_dev, send_live).T
     local_sum = jnp.dot(

time: 285 us -> 280 us (0.982)
  waiting for transfers between devices: 151 us -> 146 us
  matrix products: 16.8 us -> 13 us
    all_to_all x1, waiting for transfers between devices: 37.2 us -> 32.6 us  [per_device(): lax.all_to_all(chosen, 'pos', split_axis=0, concat_axis=0, tiled=True)]
    dot_general x40 -> x16, matrix products: 14.7 us -> 11 us  [matmul_hi(): jnp.dot(left_op, right_op, precision=lax.Precision.HIGHEST, preferred_ele...]
    gather x1 -> x0, local copies, waits for them, and re-layouts: 3.56 us -> none  [per_device(): outgoing = tiles_cut[slot_of]]
  transfers between devices with their start and end apart: 3 -> 3, of which waited for: 3 -> 3; matrix products, arithmetic and copies ran while one was open for 2% -> 4% of each run, Pallas kernels for 0% -> 0%
where the time goes in v3:
time: 280 us; the launch traced here: 279 us
  waiting for transfers between devices  146 us (52%)
  blocking collectives  54.2 us (19%)
  starting transfers between devices  22.4 us (8%)
  local copies, waits for them, and re-layouts  22.2 us (8%)
  between operations  19.8 us (7%)
  matrix products  13 us (5%)
    psum x1, waiting for transfers between devices, per_device(): tile_total = lax.psum(local_sum, 'tile')  64.4 us
    all_to_all x1, waiting for transfers between devices, per_device(): lax.all_to_all(outgoing, 'pos', split_axis=0, concat_axis=0, tiled=True)  48.9 us
    all_to_all x1, waiting for transfers between devices, per_device(): lax.all_to_all(chosen, 'pos', split_axis=0, concat_axis=0, tiled=True)  32.6 us
    all_to_all x1, blocking collectives, reduce_probe(): mine = jnp.sum(lax.all_to_all(spread, 'tile', 0, 0, tiled=True), axis=0)  22 us
    all_to_all x1, blocking collectives, reduce_probe(): mine = jnp.sum(lax.all_to_all(pieces, 'pos', 0, 0, tiled=True), axis=0)  16.8 us
    all_to_all x1, blocking collectives, reduce_probe(): gathered = lax.all_to_all(spread, 'pos', 0, 0, tiled=True)  15.4 us
    all_to_all x1, starting transfers between devices, per_device(): lax.all_to_all(chosen, 'pos', split_axis=0, concat_axis=0, tiled=True)  14.2 us
    dot_general x16, matrix products, matmul_hi(): jnp.dot(left_op, right_op, precision=lax.Precision.HIGHEST, preferred_ele...  11 us
  transfers between devices with their start and end apart: 3, of which 3 were waited for; matrix products, arithmetic and copies ran while one was open for 4% of the time, Pallas kernels for 0%

profile of v3, /device:TPU:6, one launch (start us, length us, event | category | flops | bytes accessed | tf_op | source)
XLA Modules:
  0.0 279.2 jit_solution(14764895102334127077)
XLA Ops:
  7.2 0.9 reshape.209
  8.3 1.0 fusion.2
  9.3 3.6 %gather_fusion.1 = bf16[64,4,4096]{2,1,0:T(4,128)(2,1)} fusion(bf16[24,4,4096]{2,1,0:T(4,128)(2,1)S(1)} %copy-done, s32[1024]{0:T(1024)S(1)} %pad_clamp_fusion.1), kind=kCustom, calls=%fused_computation.1 | custom fusion | bytes 4194560 | tf_op jit(solution)/shard_map/gather | solution.py:103
  12.8 14.2 %all-to-all-start = ((bf16[64,4,4096]{2,1,0:T(4,128)(2,1)}), bf16[64,4,4096]{2,1,0:T(4,128)(2,1)S(1)}, u32[]{:S(2)}, u32[]{:S(2)}) async-start(bf16[64,4,4096]{2,1,0:T(4,128)(2,1)} %gather_fusion.1), calls=%async_computation | async-start | bytes 4194304 | tf_op jit(solution)/shard_map/all_to_all | solution.py:121
  27.1 0.8 constant_dynamic-slice_fusion.1
  33.9 0.7 gather_fusion
  35.3 0.9 fusion.103
  38.5 1.2 convolution_subtract_fusion
  39.6 1.2 convolution_subtract_fusion.1
  40.8 1.2 fusion.203
  42.1 1.2 fusion.204
  43.3 32.6 %all-to-all-done = bf16[64,4,4096]{2,1,0:T(4,128)(2,1)S(1)} async-done(((bf16[64,4,4096]{2,1,0:T(4,128)(2,1)}), bf16[64,4,4096]{2,1,0:T(4,128)(2,1)S(1)}, u32[]{:S(2)}, u32[]{:S(2)}) %all-to-all-start) | async-done | bytes 2097184 | tf_op jit(solution)/shard_map/all_to_all | solution.py:121
  75.9 0.8 gather_fusion.2
  84.0 2.5 broadcast_in_dim.12
  86.6 2.4 scatter_fusion
  89.0 8.1 %all-to-all-start.1 = ((bf16[64,4,4096]{2,1,0:T(4,128)(2,1)}), bf16[64,4,4096]{2,1,0:T(4,128)(2,1)S(1)}, u32[]{:S(2)}, u32[]{:S(2)}) async-start(bf16[64,4,4096]{2,1,0:T(4,128)(2,1)} %scatter_fusion), calls=%async_computation.1 | async-start | bytes 4194304 | tf_op jit(solution)/shard_map/all_to_all | solution.py:160
  97.2 48.9 %all-to-all-done.1 = bf16[64,4,4096]{2,1,0:T(4,128)(2,1)S(1)} async-done(((bf16[64,4,4096]{2,1,0:T(4,128)(2,1)}), bf16[64,4,4096]{2,1,0:T(4,128)(2,1)S(1)}, u32[]{:S(2)}, u32[]{:S(2)}) %all-to-all-start.1) | async-done | bytes 2097184 | tf_op jit(solution)/shard_map/all_to_all | solution.py:160
  146.1 1.2 copy.63
  147.8 2.2 reshape.214
  150.2 16.8 %all_to_all.31 = f32[64,1,512]{2,1,0:T(1,128)S(1)} all-to-all(f32[64,1,512]{2,1,0:T(1,128)S(1)} %bitcast.167), channel_id=1, replica_groups=mesh['pos'=64,'tile'=12] {'pos'}, dimensions={0} | all-to-all | bytes 262144 | tf_op jit(solution)/shard_map/all_to_all | solution.py:176
  167.1 22.0 %all_to_all.32 = f32[12,1,512]{2,1,0:T(1,128)S(1)} all-to-all(f32[12,1,512]{2,1,0:T(1,128)S(1)} %broadcast_in_dim.15), channel_id=1, replica_groups=mesh['pos'=64,'tile'=12] {'tile'}, dimensions={0} | all-to-all | bytes 49152 | tf_op jit(solution)/shard_map/all_to_all | solution.py:178
  189.3 15.4 %all_to_all.33 = f32[64,1,512]{2,1,0:T(1,128)S(1)} all-to-all(f32[64,1,512]{2,1,0:T(1,128)S(1)} %broadcast_in_dim.16), channel_id=1, replica_groups=mesh['pos'=64,'tile'=12] {'pos'}, dimensions={0} | all-to-all | bytes 262144 | tf_op jit(solution)/shard_map/all_to_all | solution.py:180
  204.6 64.4 %all-reduce.2.cloned.1.call-done = f32[24,4,4096]{2,1,0:T(4,128)} async-done(((f32[24,4,4096]{2,1,0:T(4,128)}), f32[24,4,4096]{2,1,0:T(4,128)}) %all-reduce.2.cloned.1.call-update) | async-done | bytes 1572880 | tf_op jit(solution)/shard_map/psum | solution.py:168
  269.0 2.7 copy.69
  (77 shorter events, 12.6 us)
Async XLA Ops:
  7.2 2.1 copy-start
  12.8 21.0 %copy-start.1 = (s32[32,48]{1,0:T(8,128)S(1)}, s32[32,48]{1,0:T(8,128)}, u32[]{:S(2)}) copy-start(s32[32,48]{1,0:T(8,128)} %param.6) | copy-start | bytes 18436
  12.8 63.0 %all-to-all-start = ((bf16[64,4,4096]{2,1,0:T(4,128)(2,1)}), bf16[64,4,4096]{2,1,0:T(4,128)(2,1)S(1)}, u32[]{:S(2)}, u32[]{:S(2)}) async-start(bf16[64,4,4096]{2,1,0:T(4,128)(2,1)} %gather_fusion.1), calls=%async_computation | async-start | bytes 4194304 | tf_op jit(solution)/shard_map/all_to_all | solution.py:121
  27.1 7.5 %copy-start.2 = (f32[2,128,128]{2,1,0:T(8,128)S(1)}, f32[2,128,128]{2,1,0:T(8,128)}, u32[]{:S(2)}) copy-start(f32[2,128,128]{2,1,0:T(8,128)} %param.8) | copy-start | bytes 393220
  27.1 7.7 %copy-start.3 = (f32[1,128,128]{2,1,0:T(8,128)S(1)}, f32[1,128,128]{2,1,0:T(8,128)}, u32[]{:S(2)}) copy-start(f32[1,128,128]{2,1,0:T(8,128)} %param.9) | copy-start | bytes 196612
  77.1 1.4 copy-start.8
  77.2 1.4 copy-start.10
  77.2 2.0 copy-start.9
  77.7 1.9 copy-start.4
  79.1 2.5 copy-start.5
  79.1 2.5 copy-start.7
  79.5 2.7 copy-start.6
  89.0 57.1 %all-to-all-start.1 = ((bf16[64,4,4096]{2,1,0:T(4,128)(2,1)}), bf16[64,4,4096]{2,1,0:T(4,128)(2,1)S(1)}, u32[]{:S(2)}, u32[]{:S(2)}) async-start(bf16[64,4,4096]{2,1,0:T(4,128)(2,1)} %scatter_fusion), calls=%async_computation.1 | async-start | bytes 4194304 | tf_op jit(solution)/shard_map/all_to_all | solution.py:160
  97.1 171.8 %all-reduce.2.cloned.1.call-start = ((), (), s32[]{:S(2)}) async-start(), calls=%async_computation.5 | async-start | bytes 3145728 | tf_op jit(solution)/shard_map/psum | solution.py:168
Sparse Core Ops, SparseCore 0:
  150.2 118.7 all-reduce.1

commit v4 on v3

--- a/solution.py
+++ b/solution.py
@@ -154,9 +154,12 @@
     tiles_cut = tiles_cut.astype(jnp.bfloat16).reshape(
         tile_span * tile_span, n_comps, tile_edge * tile_edge
     )
-    outgoing = jnp.zeros((owners, n_comps, tile_edge * tile_edge), jnp.bfloat16).at[my_owner].set(
-        tiles_cut
+    outgoing = jnp.dot(
+        one_hot(my_owner, owners).T,
+        tiles_cut.reshape(tile_span * tile_span, n_comps * tile_edge * tile_edge),
+        preferred_element_type=jnp.float32,
     )
+    outgoing = outgoing.astype(jnp.bfloat16).reshape(owners, n_comps, tile_edge * tile_edge)
     returned = lax.all_to_all(outgoing, "pos", split_axis=0, concat_axis=0, tiled=True)
     selector = one_hot(send_local, tiles_dev, send_live).T
     local_sum = jnp.dot(

time: 280 us -> 279 us (level)
  no operation moved by 1% of the time
where the time goes in v4:
time: 279 us; the launch traced here: 278 us
  waiting for transfers between devices  146 us (52%)
  blocking collectives  54.2 us (19%)
  starting transfers between devices  22.5 us (8%)
  local copies, waits for them, and re-layouts  20.2 us (7%)
  between operations  19.8 us (7%)
  matrix products  14.1 us (5%)
    psum x1, waiting for transfers between devices, per_device(): tile_total = lax.psum(local_sum, 'tile')  64.4 us
    all_to_all x1, waiting for transfers between devices, per_device(): lax.all_to_all(outgoing, 'pos', split_axis=0, concat_axis=0, tiled=True)  48.9 us
    all_to_all x1, waiting for transfers between devices, per_device(): lax.all_to_all(chosen, 'pos', split_axis=0, concat_axis=0, tiled=True)  32.6 us
    all_to_all x1, blocking collectives, reduce_probe(): mine = jnp.sum(lax.all_to_all(spread, 'tile', 0, 0, tiled=True), axis=0)  22.3 us
    all_to_all x1, blocking collectives, reduce_probe(): mine = jnp.sum(lax.all_to_all(pieces, 'pos', 0, 0, tiled=True), axis=0)  16.8 us
    all_to_all x1, blocking collectives, reduce_probe(): gathered = lax.all_to_all(spread, 'pos', 0, 0, tiled=True)  15.1 us
    all_to_all x1, starting transfers between devices, per_device(): lax.all_to_all(chosen, 'pos', split_axis=0, concat_axis=0, tiled=True)  14.2 us
    dot_general x16, matrix products, matmul_hi(): jnp.dot(left_op, right_op, precision=lax.Precision.HIGHEST, preferred_ele...  11 us
  transfers between devices with their start and end apart: 3, of which 3 were waited for; matrix products, arithmetic and copies ran while one was open for 4% of the time, Pallas kernels for 0%

profile of v4, /device:TPU:6, one launch (start us, length us, event | category | flops | bytes accessed | tf_op | source)
XLA Modules:
  0.0 278.3 jit_solution(14833751792704451704)
XLA Ops:
  7.2 0.9 reshape.226
  8.3 1.0 fusion.2
  9.3 3.6 %gather_fusion.1 = bf16[64,4,4096]{2,1,0:T(4,128)(2,1)} fusion(bf16[24,4,4096]{2,1,0:T(4,128)(2,1)S(1)} %copy-done, s32[1024]{0:T(1024)S(1)} %pad_clamp_fusion.1), kind=kCustom, calls=%fused_computation.1 | custom fusion | bytes 4194560 | tf_op jit(solution)/shard_map/gather | solution.py:103
  12.8 14.2 %all-to-all-start = ((bf16[64,4,4096]{2,1,0:T(4,128)(2,1)}), bf16[64,4,4096]{2,1,0:T(4,128)(2,1)S(1)}, u32[]{:S(2)}, u32[]{:S(2)}) async-start(bf16[64,4,4096]{2,1,0:T(4,128)(2,1)} %gather_fusion.1), calls=%async_computation | async-start | bytes 4194304 | tf_op jit(solution)/shard_map/all_to_all | solution.py:121
  27.1 0.8 constant_dynamic-slice_fusion.1
  33.9 0.7 gather_fusion
  35.3 0.9 fusion.103
  38.5 1.2 convolution_subtract_fusion
  39.7 1.2 convolution_subtract_fusion.1
  40.9 1.2 fusion.204
  42.1 1.2 fusion.205
  43.3 32.6 %all-to-all-done = bf16[64,4,4096]{2,1,0:T(4,128)(2,1)S(1)} async-done(((bf16[64,4,4096]{2,1,0:T(4,128)(2,1)}), bf16[64,4,4096]{2,1,0:T(4,128)(2,1)S(1)}, u32[]{:S(2)}, u32[]{:S(2)}) %all-to-all-start) | async-done | bytes 2097184 | tf_op jit(solution)/shard_map/all_to_all | solution.py:121
  75.9 0.8 gather_fusion.2
  84.2 1.1 convolution_convert_fusion
  85.3 2.8 %reshape.229 = bf16[64,4,4096]{2,1,0:T(4,128)(2,1)} reshape(bf16[64,16384]{1,0:T(8,128)(2,1)S(1)} %convolution_convert_fusion) | data formatting | bytes 4194304 | tf_op jit(solution)/shard_map/reshape | solution.py:162
  88.1 8.2 %all-to-all-start.1 = ((bf16[64,4,4096]{2,1,0:T(4,128)(2,1)}), bf16[64,4,4096]{2,1,0:T(4,128)(2,1)S(1)}, u32[]{:S(2)}, u32[]{:S(2)}) async-start(bf16[64,4,4096]{2,1,0:T(4,128)(2,1)} %reshape.229), calls=%async_computation.1 | async-start | bytes 4194304 | tf_op jit(solution)/shard_map/all_to_all | solution.py:163
  96.4 48.9 %all-to-all-done.1 = bf16[64,4,4096]{2,1,0:T(4,128)(2,1)S(1)} async-done(((bf16[64,4,4096]{2,1,0:T(4,128)(2,1)}), bf16[64,4,4096]{2,1,0:T(4,128)(2,1)S(1)}, u32[]{:S(2)}, u32[]{:S(2)}) %all-to-all-start.1) | async-done | bytes 2097184 | tf_op jit(solution)/shard_map/all_to_all | solution.py:163
  145.3 1.2 copy.63
  147.0 2.2 reshape.231
  149.4 16.8 %all_to_all.31 = f32[64,1,512]{2,1,0:T(1,128)S(1)} all-to-all(f32[64,1,512]{2,1,0:T(1,128)S(1)} %bitcast.170), channel_id=1, replica_groups=mesh['pos'=64,'tile'=12] {'pos'}, dimensions={0} | all-to-all | bytes 262144 | tf_op jit(solution)/shard_map/all_to_all | solution.py:179
  166.3 22.3 %all_to_all.32 = f32[12,1,512]{2,1,0:T(1,128)S(1)} all-to-all(f32[12,1,512]{2,1,0:T(1,128)S(1)} %broadcast_in_dim.12), channel_id=1, replica_groups=mesh['pos'=64,'tile'=12] {'tile'}, dimensions={0} | all-to-all | bytes 49152 | tf_op jit(solution)/shard_map/all_to_all | solution.py:181
  188.7 15.1 %all_to_all.33 = f32[64,1,512]{2,1,0:T(1,128)S(1)} all-to-all(f32[64,1,512]{2,1,0:T(1,128)S(1)} %broadcast_in_dim.13), channel_id=1, replica_groups=mesh['pos'=64,'tile'=12] {'pos'}, dimensions={0} | all-to-all | bytes 262144 | tf_op jit(solution)/shard_map/all_to_all | solution.py:183
  203.8 64.4 %all-reduce.2.cloned.1.call-done = f32[24,4,4096]{2,1,0:T(4,128)} async-done(((f32[24,4,4096]{2,1,0:T(4,128)}), f32[24,4,4096]{2,1,0:T(4,128)}) %all-reduce.2.cloned.1.call-update) | async-done | bytes 1572880 | tf_op jit(solution)/shard_map/psum | solution.py:171
  268.1 2.7 copy.68
  (82 shorter events, 12.7 us)
Async XLA Ops:
  7.2 2.1 copy-start
  9.2 3.6 %copy-start.5 = (f32[64]{0:T(128)}, f32[64]{0:T(128)S(1)}, u32[]{:S(2)}) copy-start(f32[64]{0:T(128)S(1)} %fusion.2) | copy-start | bytes 772
  12.8 21.0 %copy-start.1 = (s32[32,48]{1,0:T(8,128)S(1)}, s32[32,48]{1,0:T(8,128)}, u32[]{:S(2)}) copy-start(s32[32,48]{1,0:T(8,128)} %param.6) | copy-start | bytes 18436
  12.8 63.0 %all-to-all-start = ((bf16[64,4,4096]{2,1,0:T(4,128)(2,1)}), bf16[64,4,4096]{2,1,0:T(4,128)(2,1)S(1)}, u32[]{:S(2)}, u32[]{:S(2)}) async-start(bf16[64,4,4096]{2,1,0:T(4,128)(2,1)} %gather_fusion.1), calls=%async_computation | async-start | bytes 4194304 | tf_op jit(solution)/shard_map/all_to_all | solution.py:121
  27.1 7.5 %copy-start.2 = (f32[2,128,128]{2,1,0:T(8,128)S(1)}, f32[2,128,128]{2,1,0:T(8,128)}, u32[]{:S(2)}) copy-start(f32[2,128,128]{2,1,0:T(8,128)} %param.8) | copy-start | bytes 393220
  27.1 7.7 %copy-start.3 = (f32[1,128,128]{2,1,0:T(8,128)S(1)}, f32[1,128,128]{2,1,0:T(8,128)}, u32[]{:S(2)}) copy-start(f32[1,128,128]{2,1,0:T(8,128)} %param.9) | copy-start | bytes 196612
  77.2 1.4 copy-start.10
  77.2 1.4 copy-start.12
  77.2 2.0 copy-start.11
  77.7 1.9 copy-start.4
  79.1 2.5 copy-start.7
  79.2 2.5 copy-start.9
  79.6 2.7 copy-start.8
  88.1 8.3 %copy-start.6 = (f32[64]{0:T(128)S(1)}, f32[64]{0:T(128)}, u32[]{:S(2)}) copy-start(f32[64]{0:T(128)} %copy-done.5) | copy-start | bytes 772
  88.1 57.2 %all-to-all-start.1 = ((bf16[64,4,4096]{2,1,0:T(4,128)(2,1)}), bf16[64,4,4096]{2,1,0:T(4,128)(2,1)S(1)}, u32[]{:S(2)}, u32[]{:S(2)}) async-start(bf16[64,4,4096]{2,1,0:T(4,128)(2,1)} %reshape.229), calls=%async_computation.1 | async-start | bytes 4194304 | tf_op jit(solution)/shard_map/all_to_all | solution.py:163
  96.3 171.8 %all-reduce.2.cloned.1.call-start = ((), (), s32[]{:S(2)}) async-start(), calls=%async_computation.5 | async-start | bytes 3145728 | tf_op jit(solution)/shard_map/psum | solution.py:171
Sparse Core Ops, SparseCore 0:
  149.4 118.7 all-reduce.1

commit v5 on v3

--- a/solution.py
+++ b/solution.py
@@ -151,23 +151,71 @@
     rows_cut = jnp.einsum("irk,ckm->cirm", shift_y, patch_grad, preferred_element_type=jnp.float32)
     rows_cut = rows_cut.astype(jnp.bfloat16)
     tiles_cut = jnp.einsum("cirm,jsm->ijcrs", rows_cut, shift_x, preferred_element_type=jnp.float32)
-    tiles_cut = tiles_cut.astype(jnp.bfloat16).reshape(
-        tile_span * tile_span, n_comps, tile_edge * tile_edge
-    )
-    outgoing = jnp.zeros((owners, n_comps, tile_edge * tile_edge), jnp.bfloat16).at[my_owner].set(
-        tiles_cut
-    )
-    returned = lax.all_to_all(outgoing, "pos", split_axis=0, concat_axis=0, tiled=True)
-    selector = one_hot(send_local, tiles_dev, send_live).T
-    local_sum = jnp.dot(
-        selector,
-        returned.reshape(owners, n_comps * tile_edge * tile_edge),
-        preferred_element_type=jnp.float32,
-    )
+    n_foot = tile_span * tile_span
+    tile_px = n_comps * tile_edge * tile_edge
+    tiles_cut = tiles_cut.astype(jnp.bfloat16).reshape(n_foot, tile_px)
+
+    cut_len = -(-tile_px // layers)
+    cut_len = -(-cut_len // 128) * 128
+    pad_px = cut_len * layers - tile_px
+    cut = jnp.pad(tiles_cut, ((0, 0), (0, pad_px))).reshape(n_foot, layers, cut_len)
+    from_column = lax.all_to_all(cut.transpose(1, 0, 2), "tile", 0, 0, tiled=True)
+
+    col_corners = lax.dynamic_index_in_dim(by_device, me_pos, 0, keepdims=False)
+    col_rows = col_corners[:, 0:1] // tile_edge + span_idx[None, :]
+    col_cols = col_corners[:, 1:2] // tile_edge + span_idx[None, :]
+    col_owner = tile_map[col_rows[:, :, None], col_cols[:, None, :]].reshape(layers, n_foot)
+    col_owner = col_owner // tiles_dev
+    to_owner = (col_owner[:, :, None] == jnp.arange(owners)[None, None, :]).astype(jnp.bfloat16)
+    outgoing = jnp.einsum("tsp,tsx->ptx", to_owner, from_column, preferred_element_type=jnp.float32)
+    outgoing = outgoing.astype(jnp.bfloat16)
+    returned = lax.all_to_all(outgoing, "pos", 0, 0, tiled=True)
+
+    all_r = offsets[:, 0:1] // tile_edge
+    all_c = offsets[:, 1:2] // tile_edge
+    all_row_in = ((grid_rows >= all_r) & (grid_rows < all_r + tile_span)).astype(jnp.bfloat16)
+    all_col_in = ((grid_cols >= all_c) & (grid_cols < all_c + tile_span)).astype(jnp.float32)
+    all_found = jnp.sum(
+        jnp.dot(all_row_in, local_plus, preferred_element_type=jnp.float32) * all_col_in, axis=1
+    ).astype(jnp.int32)
+    all_sel = one_hot(jnp.maximum(all_found - 1, 0), tiles_dev, all_found > 0)
+    all_sel = all_sel.reshape(owners, layers, tiles_dev)
+    my_slice = jnp.einsum("qtk,qtx->kx", all_sel, returned, preferred_element_type=jnp.float32)
+
     probe_part = jnp.stack([grad_re, grad_im])
-    tile_total = lax.psum(local_sum, "tile")
-    probe_total = reduce_probe(probe_part, owners, layers)
+    piece_len = probe_part.size // owners
+    probe_row = jnp.sum(
+        lax.all_to_all(probe_part.reshape(owners, piece_len), "pos", 0, 0, tiled=True), axis=0
+    )
+    probe_cut = jnp.pad(probe_row, (0, cut_len - piece_len))[None]
+    gathered = ring_gather(jnp.concatenate([my_slice, probe_cut], axis=0), layers)
+    slices = gathered[:, :tiles_dev]
+    tile_total = slices.transpose(1, 0, 2).reshape(tiles_dev, layers * cut_len)[:, :tile_px]
+    probe_piece = jnp.sum(gathered[:, tiles_dev, :piece_len], axis=0)
+    spread = jnp.broadcast_to(probe_piece[None], (owners, piece_len))
+    probe_total = lax.all_to_all(spread, "pos", 0, 0, tiled=True).reshape(probe_part.shape)
     return (tile_total.reshape(tiles_dev, n_comps, tile_edge * tile_edge), probe_total)
+
+
+def ring_gather(values, size):
+    me = lax.axis_index("tile")
+    to_right = [(i, (i + 1) % size) for i in range(size)]
+    to_left = [(i, (i - 1) % size) for i in range(size)]
+    back = [values]
+    ahead = []
+    going_right = values
+    going_left = values
+    for step in range(1, size // 2 + 1):
+        going_right = lax.ppermute(going_right, "tile", to_right)
+        back.append(going_right)
+        if step < size - size // 2:
+            going_left = lax.ppermute(going_left, "tile", to_left)
+            ahead.append(going_left)
+    by_offset = [back[0]] + ahead + [back[size - d] for d in range(len(ahead) + 1, size)]
+    gathered = jnp.zeros((size,) + values.shape, values.dtype)
+    for offset, part in enumerate(by_offset):
+        gathered = lax.dynamic_update_index_in_dim(gathered, part, (me + offset) % size, 0)
+    return gathered
 
 
 def reduce_probe(probe_part, owners, layers):

time: 280 us -> 350 us (1.25)
  local copies, waits for them, and re-layouts: 22.2 us -> 95 us
  starting transfers between devices: 22.4 us -> 84.3 us
  blocking collectives: 54.2 us -> 0 us
  between operations: 19.8 us -> 7.08 us
  waiting for transfers between devices: 146 us -> 140 us
    psum x1 -> x0, waiting for transfers between devices: 64.4 us -> none  [per_device(): tile_total = lax.psum(local_sum, 'tile')]
    dynamic_update_slice x0 -> x12, local copies, waits for them, and re-layouts: none -> 57.8 us  [ring_gather(): lax.dynamic_update_index_in_dim(gathered, part, (me + offset) % size, 0)]
    all_to_all x3 -> x0, blocking collectives: 54.2 us -> none  [the longest x1 22 us: reduce_probe(): mine = jnp.sum(lax.all_to_all(spread, 'tile', 0, 0, tiled=True), axis=0)]
    all_to_all x1 -> x4, waiting for transfers between devices: 48.9 us -> 95.1 us  [the longest x1 64.4 us: per_device(): returned = lax.all_to_all(outgoing, 'pos', 0, 0, tiled=True)]
    ppermute x0 -> x11, starting transfers between devices: none -> 36.2 us  [the longest x5 18.9 us: ring_gather(): going_left = lax.ppermute(going_left, 'tile', to_left)]
    all_to_all x1 -> x4, starting transfers between devices: 8.14 us -> 33.8 us  [the longest x1 12 us: per_device(): lax.all_to_all(cut.transpose(1, 0, 2), 'tile', 0, 0, tiled=True)]
    broadcast_in_dim x3 -> x15, local copies, waits for them, and re-layouts: 2.64 us -> 15.8 us  [the longest x12 14.9 us: ring_gather(): lax.dynamic_update_index_in_dim(gathered, part, (me + offset) % size, 0)]
    ppermute x0 -> x11, waiting for transfers between devices: none -> 12.2 us  [the longest x6 11 us: ring_gather(): going_right = lax.ppermute(going_right, 'tile', to_right)]
  transfers between devices with their start and end apart: 3 -> 16, of which waited for: 3 -> 13; matrix products, arithmetic and copies ran while one was open for 4% -> 19% of each run, Pallas kernels for 0% -> 0%
where the time goes in v5:
time: 350 us; the launch traced here: 346 us
  waiting for transfers between devices  140 us (40%)
  local copies, waits for them, and re-layouts  95 us (27%)
  starting transfers between devices  84.3 us (24%)
  matrix products  16.1 us (5%)
  between operations  7.08 us (2%)
    all_to_all x1, waiting for transfers between devices, per_device(): returned = lax.all_to_all(outgoing, 'pos', 0, 0, tiled=True)  64.4 us
    dynamic_update_slice x12, local copies, waits for them, and re-layouts, ring_gather(): lax.dynamic_update_index_in_dim(gathered, part, (me + offset) % size, 0)  57.8 us
    all_to_all x1, waiting for transfers between devices, per_device(): lax.all_to_all(chosen, 'pos', split_axis=0, concat_axis=0, tiled=True)  32.6 us
    all_to_all x1, waiting for transfers between devices, per_device(): lax.all_to_all(cut.transpose(1, 0, 2), 'tile', 0, 0, tiled=True)  20.4 us
    ppermute x5, starting transfers between devices, ring_gather(): going_left = lax.ppermute(going_left, 'tile', to_left)  18.9 us
    ppermute x6, starting transfers between devices, ring_gather(): going_right = lax.ppermute(going_right, 'tile', to_right)  17.4 us
    broadcast_in_dim x12, local copies, waits for them, and re-layouts, ring_gather(): lax.dynamic_update_index_in_dim(gathered, part, (me + offset) % size, 0)  14.9 us
    all_to_all x1, starting transfers between devices, per_device(): lax.all_to_all(chosen, 'pos', split_axis=0, concat_axis=0, tiled=True)  14.2 us
  transfers between devices with their start and end apart: 16, of which 13 were waited for; matrix products, arithmetic and copies ran while one was open for 19% of the time, Pallas kernels for 0%

profile of v5, /device:TPU:6, one launch (start us, length us, event | category | flops | bytes accessed | tf_op | source)
XLA Modules:
  0.0 345.7 jit_solution(1551687342180905999)
XLA Ops:
  6.9 14.2 %all-to-all-start = ((bf16[64,4,4096]{2,1,0:T(4,128)(2,1)}), bf16[64,4,4096]{2,1,0:T(4,128)(2,1)S(1)}, u32[]{:S(2)}, u32[]{:S(2)}) async-start(bf16[64,4,4096]{2,1,0:T(4,128)(2,1)} %gather_fusion), calls=%async_computation | async-start | bytes 4194304 | tf_op jit(solution)/shard_map/all_to_all | solution.py:121
  37.3 32.6 %all-to-all-done = bf16[64,4,4096]{2,1,0:T(4,128)(2,1)S(1)} async-done(((bf16[64,4,4096]{2,1,0:T(4,128)(2,1)}), bf16[64,4,4096]{2,1,0:T(4,128)(2,1)S(1)}, u32[]{:S(2)}, u32[]{:S(2)}) %all-to-all-start) | async-done | bytes 2097184 | tf_op jit(solution)/shard_map/all_to_all | solution.py:121
  79.8 12.0 %all-to-all-start.1 = ((bf16[12,9,1408]{2,1,0:T(8,128)(2,1)}), bf16[12,9,1408]{2,1,0:T(8,128)(2,1)S(1)}, u32[]{:S(2)}, u32[]{:S(2)}) async-start(bf16[12,9,1408]{2,1,0:T(8,128)(2,1)} %bitcast.192), calls=%async_computation.1 | async-start | bytes 1081344 | tf_op jit(solution)/shard_map/all_to_all | solution.py:162
  94.7 20.4 %all-to-all-done.1 = bf16[12,9,1408]{2,1,0:T(8,128)(2,1)S(1)} async-done(((bf16[12,9,1408]{2,1,0:T(8,128)(2,1)}), bf16[12,9,1408]{2,1,0:T(8,128)(2,1)S(1)}, u32[]{:S(2)}, u32[]{:S(2)}) %all-to-all-start.1) | async-done | bytes 304160 | tf_op jit(solution)/shard_map/all_to_all | solution.py:162
  115.1 8.3 %all-to-all-start.3 = ((f32[64,1,512]{2,1,0:T(1,128)}), f32[64,1,512]{2,1,0:T(1,128)S(1)}, u32[]{:S(2)}, u32[]{:S(2)}) async-start(f32[64,1,512]{2,1,0:T(1,128)} %bitcast.36), calls=%async_computation.3 | async-start | bytes 262144 | tf_op jit(solution)/shard_map/all_to_all | solution.py:188
  132.3 6.9 %all-to-all-start.2 = ((bf16[64,12,1408]{2,1,0:T(8,128)(2,1)}), bf16[64,12,1408]{2,1,0:T(8,128)(2,1)}, u32[]{:S(2)}, u32[]{:S(2)}) async-start(bf16[64,12,1408]{2,1,0:T(8,128)(2,1)} %copy.99), calls=%async_computation.2 | async-start | bytes 5767168 | tf_op jit(solution)/shard_map/all_to_all | solution.py:172
  140.3 64.4 %all-to-all-done.2 = bf16[64,12,1408]{2,1,0:T(8,128)(2,1)} async-done(((bf16[64,12,1408]{2,1,0:T(8,128)(2,1)}), bf16[64,12,1408]{2,1,0:T(8,128)(2,1)}, u32[]{:S(2)}, u32[]{:S(2)}) %all-to-all-start.2) | async-done | bytes 2162720 | tf_op jit(solution)/shard_map/all_to_all | solution.py:172
  207.0 5.2 %collective-permute-start.5 = (f32[25,1408]{1,0:T(8,128)S(1)}, f32[25,1408]{1,0:T(8,128)S(1)}, u32[]{:S(2)}, u32[]{:S(2)}) collective-permute-start(f32[25,1408]{1,0:T(8,128)S(1)} %get-tuple-element.28), channel_id=1, source_target_pairs={{0,1},{1,2},{2,3},{3,4},{4,5},{5,6},{6,7},{7,8},{8,9},{9,10},{10,1... | collective-permute-start | bytes 422408 | tf_op jit(solution)/shard_map/ppermute | solution.py:209
  238.2 5.1 %collective-permute-start.3 = (f32[25,1408]{1,0:T(8,128)S(1)}, f32[25,1408]{1,0:T(8,128)}, u32[]{:S(2)}, u32[]{:S(2)}) collective-permute-start(f32[25,1408]{1,0:T(8,128)S(1)} %collective-permute-done.2), channel_id=1, source_target_pairs={{0,11},{1,0},{2,1},{3,2},{4,3},{5,4},{6,5},{7,6},{8,7},{9,8},{10,9... | collective-permute-start | bytes 422408 | tf_op jit(solution)/shard_map/ppermute | solution.py:212
  246.9 5.3 %collective-permute-start.4 = (f32[25,1408]{1,0:T(8,128)}, f32[25,1408]{1,0:T(8,128)}, u32[]{:S(2)}, u32[]{:S(2)}) collective-permute-start(f32[25,1408]{1,0:T(8,128)} %collective-permute-done.3), channel_id=1, source_target_pairs={{0,11},{1,0},{2,1},{3,2},{4,3},{5,4},{6,5},{7,6},{8,7},{9,8},{10,9... | collective-permute-start | bytes 422408 | tf_op jit(solution)/shard_map/ppermute | solution.py:212
  256.2 5.0 %dynamic_update_slice.37 = f32[12,25,1408]{2,0,1:T(8,128)S(1)} dynamic-update-slice(f32[12,25,1408]{2,0,1:T(8,128)S(1)} %broadcast_in_dim.96, f32[1,25,1408]{2,0,1:T(1,128)S(1)} %copy.103, s32[]{:T(128)S(6)} %select_n.342, s32[]{:T(128)} %constant.240.clone.1, s32[]{:T(128)} %constant.240.clone.1) | dynamic-update-slice | bytes 281604 | tf_op jit(solution)/shard_map/jit(dynamic_update_index_in_dim)/dynamic_update_slice | solution.py:217
  262.4 4.7 %dynamic_update_slice.38 = f32[12,25,1408]{2,0,1:T(8,128)S(1)} dynamic-update-slice(f32[12,25,1408]{2,0,1:T(8,128)S(1)} %dynamic_update_slice.37, f32[1,25,1408]{2,0,1:T(1,128)S(1)} %copy.104, s32[]{:T(128)S(6)} %select_n.344, s32[]{:T(128)} %constant.240.clone.1, s32[]{:T(128)} %constant.240.clone.1) | dynamic-update-slice | bytes 281604 | tf_op jit(solution)/shard_map/jit(dynamic_update_index_in_dim)/dynamic_update_slice | solution.py:217
  269.3 4.7 %dynamic_update_slice.39 = f32[12,25,1408]{2,0,1:T(8,128)S(1)} dynamic-update-slice(f32[12,25,1408]{2,0,1:T(8,128)S(1)} %dynamic_update_slice.38, f32[1,25,1408]{2,0,1:T(1,128)S(1)} %copy.105, s32[]{:T(128)S(6)} %select_n.346, s32[]{:T(128)} %constant.240.clone.1, s32[]{:T(128)} %constant.240.clone.1) | dynamic-update-slice | bytes 281604 | tf_op jit(solution)/shard_map/jit(dynamic_update_index_in_dim)/dynamic_update_slice | solution.py:217
  276.8 4.9 %dynamic_update_slice.40 = f32[12,25,1408]{2,0,1:T(8,128)S(1)} dynamic-update-slice(f32[12,25,1408]{2,0,1:T(8,128)S(1)} %dynamic_update_slice.39, f32[1,25,1408]{2,0,1:T(1,128)} %copy.106, s32[]{:T(128)S(6)} %select_n.348, s32[]{:T(128)} %constant.240.clone.1, s32[]{:T(128)} %constant.240.clone.1) | dynamic-update-slice | bytes 281604 | tf_op jit(solution)/shard_map/jit(dynamic_update_index_in_dim)/dynamic_update_slice | solution.py:217
  285.1 4.8 %dynamic_update_slice.41 = f32[12,25,1408]{2,0,1:T(8,128)S(1)} dynamic-update-slice(f32[12,25,1408]{2,0,1:T(8,128)S(1)} %dynamic_update_slice.40, f32[1,25,1408]{2,0,1:T(1,128)} %copy.107, s32[]{:T(128)S(6)} %select_n.350, s32[]{:T(128)} %constant.240.clone.1, s32[]{:T(128)} %constant.240.clone.1) | dynamic-update-slice | bytes 281604 | tf_op jit(solution)/shard_map/jit(dynamic_update_index_in_dim)/dynamic_update_slice | solution.py:217
  293.5 4.8 %dynamic_update_slice.42 = f32[12,25,1408]{2,0,1:T(8,128)S(1)} dynamic-update-slice(f32[12,25,1408]{2,0,1:T(8,128)S(1)} %dynamic_update_slice.41, f32[1,25,1408]{2,0,1:T(1,128)} %copy.108, s32[]{:T(128)S(6)} %select_n.352, s32[]{:T(128)} %constant.240.clone.1, s32[]{:T(128)} %constant.240.clone.1) | dynamic-update-slice | bytes 281604 | tf_op jit(solution)/shard_map/jit(dynamic_update_index_in_dim)/dynamic_update_slice | solution.py:217
  300.0 4.8 %dynamic_update_slice.43 = f32[12,25,1408]{2,0,1:T(8,128)S(1)} dynamic-update-slice(f32[12,25,1408]{2,0,1:T(8,128)S(1)} %dynamic_update_slice.42, f32[1,25,1408]{2,0,1:T(1,128)} %copy.109, s32[]{:T(128)S(6)} %select_n.354, s32[]{:T(128)} %constant.240.clone.1, s32[]{:T(128)} %constant.240.clone.1) | dynamic-update-slice | bytes 281604 | tf_op jit(solution)/shard_map/jit(dynamic_update_index_in_dim)/dynamic_update_slice | solution.py:217
  304.9 4.9 %dynamic_update_slice.44 = f32[12,25,1408]{2,0,1:T(8,128)S(1)} dynamic-update-slice(f32[12,25,1408]{2,0,1:T(8,128)S(1)} %dynamic_update_slice.43, f32[1,25,1408]{2,0,1:T(1,128)} %copy.110, s32[]{:T(128)S(6)} %select_n.356, s32[]{:T(128)} %constant.240.clone.1, s32[]{:T(128)} %constant.240.clone.1) | dynamic-update-slice | bytes 281604 | tf_op jit(solution)/shard_map/jit(dynamic_update_index_in_dim)/dynamic_update_slice | solution.py:217
  309.8 4.9 %dynamic_update_slice.45 = f32[12,25,1408]{2,0,1:T(8,128)S(1)} dynamic-update-slice(f32[12,25,1408]{2,0,1:T(8,128)S(1)} %dynamic_update_slice.44, f32[1,25,1408]{2,0,1:T(1,128)} %copy.111, s32[]{:T(128)S(6)} %select_n.358, s32[]{:T(128)} %constant.240.clone.1, s32[]{:T(128)} %constant.240.clone.1) | dynamic-update-slice | bytes 281604 | tf_op jit(solution)/shard_map/jit(dynamic_update_index_in_dim)/dynamic_update_slice | solution.py:217
  314.8 4.7 %dynamic_update_slice.46 = f32[12,25,1408]{2,0,1:T(8,128)S(1)} dynamic-update-slice(f32[12,25,1408]{2,0,1:T(8,128)S(1)} %dynamic_update_slice.45, f32[1,25,1408]{2,0,1:T(1,128)S(1)} %copy.112, s32[]{:T(128)S(6)} %select_n.360, s32[]{:T(128)} %constant.240.clone.1, s32[]{:T(128)} %constant.240.clone.1) | dynamic-update-slice | bytes 281604 | tf_op jit(solution)/shard_map/jit(dynamic_update_index_in_dim)/dynamic_update_slice | solution.py:217
  319.5 4.7 %dynamic_update_slice.47 = f32[12,25,1408]{2,0,1:T(8,128)S(1)} dynamic-update-slice(f32[12,25,1408]{2,0,1:T(8,128)S(1)} %dynamic_update_slice.46, f32[1,25,1408]{2,0,1:T(1,128)S(1)} %copy.113, s32[]{:T(128)S(6)} %select_n.362, s32[]{:T(128)} %constant.240.clone.1, s32[]{:T(128)} %constant.240.clone.1) | dynamic-update-slice | bytes 281604 | tf_op jit(solution)/shard_map/jit(dynamic_update_index_in_dim)/dynamic_update_slice | solution.py:217
  324.2 4.7 %dynamic_update_slice.48 = f32[12,25,1408]{2,0,1:T(8,128)S(1)} dynamic-update-slice(f32[12,25,1408]{2,0,1:T(8,128)S(1)} %dynamic_update_slice.47, f32[1,25,1408]{2,0,1:T(1,128)S(1)} %copy.114, s32[]{:T(128)S(6)} %select_n.364, s32[]{:T(128)} %constant.240.clone.1, s32[]{:T(128)} %constant.240.clone.1) | dynamic-update-slice | bytes 281604 | tf_op jit(solution)/shard_map/jit(dynamic_update_index_in_dim)/dynamic_update_slice | solution.py:217
  329.6 6.6 %all-to-all-start.4 = ((f32[64,1,512]{2,1,0:T(1,128)}), f32[64,1,512]{2,1,0:T(1,128)S(1)}, u32[]{:S(2)}, u32[]{:S(2)}) async-start(f32[64,1,512]{2,1,0:T(1,128)} %broadcast_in_dim.114), calls=%async_computation.4 | async-start | bytes 262144 | tf_op jit(solution)/shard_map/all_to_all | solution.py:196
  339.2 5.9 %all-to-all-done.4 = f32[64,1,512]{2,1,0:T(1,128)S(1)} async-done(((f32[64,1,512]{2,1,0:T(1,128)}), f32[64,1,512]{2,1,0:T(1,128)S(1)}, u32[]{:S(2)}, u32[]{:S(2)}) %all-to-all-start.4) | async-done | bytes 131104 | tf_op jit(solution)/shard_map/all_to_all | solution.py:196
  (168 shorter events, 94.0 us)
Async XLA Ops:
  6.9 14.3 %copy-start.11 = (s32[768,2]{0,1:T(2,128)S(1)}, s32[768,2]{0,1:T(2,128)}, u32[]{:S(2)}) copy-start(s32[768,2]{0,1:T(2,128)} %param.7) | copy-start | bytes 18436
  6.9 20.3 %copy-start.1 = (s32[32,48]{1,0:T(8,128)S(1)}, s32[32,48]{1,0:T(8,128)}, u32[]{:S(2)}) copy-start(s32[32,48]{1,0:T(8,128)} %param.6) | copy-start | bytes 18436
  6.9 21.0 %copy-start.8 = (f32[2,128,128]{2,1,0:T(8,128)S(1)}, f32[2,128,128]{2,1,0:T(8,128)}, u32[]{:S(2)}) copy-start(f32[2,128,128]{2,1,0:T(8,128)} %param.8) | copy-start | bytes 393220
  6.9 63.0 %all-to-all-start = ((bf16[64,4,4096]{2,1,0:T(4,128)(2,1)}), bf16[64,4,4096]{2,1,0:T(4,128)(2,1)S(1)}, u32[]{:S(2)}, u32[]{:S(2)}) async-start(bf16[64,4,4096]{2,1,0:T(4,128)(2,1)} %gather_fusion), calls=%async_computation | async-start | bytes 4194304 | tf_op jit(solution)/shard_map/all_to_all | solution.py:121
  79.8 35.3 %all-to-all-start.1 = ((bf16[12,9,1408]{2,1,0:T(8,128)(2,1)}), bf16[12,9,1408]{2,1,0:T(8,128)(2,1)S(1)}, u32[]{:S(2)}, u32[]{:S(2)}) async-start(bf16[12,9,1408]{2,1,0:T(8,128)(2,1)} %bitcast.192), calls=%async_computation.1 | async-start | bytes 1081344 | tf_op jit(solution)/shard_map/all_to_all | solution.py:162
  115.1 17.1 %all-to-all-start.3 = ((f32[64,1,512]{2,1,0:T(1,128)}), f32[64,1,512]{2,1,0:T(1,128)S(1)}, u32[]{:S(2)}, u32[]{:S(2)}) async-start(f32[64,1,512]{2,1,0:T(1,128)} %bitcast.36), calls=%async_computation.3 | async-start | bytes 262144 | tf_op jit(solution)/shard_map/all_to_all | solution.py:188
  132.3 72.5 %all-to-all-start.2 = ((bf16[64,12,1408]{2,1,0:T(8,128)(2,1)}), bf16[64,12,1408]{2,1,0:T(8,128)(2,1)}, u32[]{:S(2)}, u32[]{:S(2)}) async-start(bf16[64,12,1408]{2,1,0:T(8,128)(2,1)} %copy.99), calls=%async_computation.2 | async-start | bytes 5767168 | tf_op jit(solution)/shard_map/all_to_all | solution.py:172
  207.0 9.1 %collective-permute-start.5 = (f32[25,1408]{1,0:T(8,128)S(1)}, f32[25,1408]{1,0:T(8,128)S(1)}, u32[]{:S(2)}, u32[]{:S(2)}) collective-permute-start(f32[25,1408]{1,0:T(8,128)S(1)} %get-tuple-element.28), channel_id=1, source_target_pairs={{0,1},{1,2},{2,3},{3,4},{4,5},{5,6},{6,7},{7,8},{8,9},{9,10},{10,1... | collective-permute-start | bytes 422408 | tf_op jit(solution)/shard_map/ppermute | solution.py:209
  212.2 8.2 %collective-permute-start = (f32[25,1408]{1,0:T(8,128)S(1)}, f32[25,1408]{1,0:T(8,128)S(1)}, u32[]{:S(2)}, u32[]{:S(2)}) collective-permute-start(f32[25,1408]{1,0:T(8,128)S(1)} %get-tuple-element.28), channel_id=1, source_target_pairs={{0,11},{1,0},{2,1},{3,2},{4,3},{5,4},{6,5},{7,6},{8,7},{9,8},{10,9... | collective-permute-start | bytes 422408 | tf_op jit(solution)/shard_map/ppermute | solution.py:212
  216.2 10.3 %collective-permute-start.6 = (f32[25,1408]{1,0:T(8,128)S(1)}, f32[25,1408]{1,0:T(8,128)S(1)}, u32[]{:S(2)}, u32[]{:S(2)}) collective-permute-start(f32[25,1408]{1,0:T(8,128)S(1)} %collective-permute-done.5), channel_id=1, source_target_pairs={{0,1},{1,2},{2,3},{3,4},{4,5},{5,6},{6,7},{7,8},{8,9},{9,10},{10,1... | collective-permute-start | bytes 422408 | tf_op jit(solution)/shard_map/ppermute | solution.py:209
  220.5 35.3 %copy-start.3 = (f32[25,1408]{1,0:T(8,128)}, f32[25,1408]{1,0:T(8,128)S(1)}, u32[]{:S(2)}) copy-start(f32[25,1408]{1,0:T(8,128)S(1)} %collective-permute-done) | copy-start | bytes 422404
  220.5 9.3 %collective-permute-start.1 = (f32[25,1408]{1,0:T(8,128)S(1)}, f32[25,1408]{1,0:T(8,128)S(1)}, u32[]{:S(2)}, u32[]{:S(2)}) collective-permute-start(f32[25,1408]{1,0:T(8,128)S(1)} %collective-permute-done), channel_id=1, source_target_pairs={{0,11},{1,0},{2,1},{3,2},{4,3},{5,4},{6,5},{7,6},{8,7},{9,8},{10,9... | collective-permute-start | bytes 422408 | tf_op jit(solution)/shard_map/ppermute | solution.py:212
  226.5 29.4 %copy-start.2 = (f32[25,1408]{1,0:T(8,128)}, f32[25,1408]{1,0:T(8,128)S(1)}, u32[]{:S(2)}) copy-start(f32[25,1408]{1,0:T(8,128)S(1)} %collective-permute-done.6) | copy-start | bytes 422404
  226.5 9.7 %collective-permute-start.7 = (f32[25,1408]{1,0:T(8,128)S(1)}, f32[25,1408]{1,0:T(8,128)S(1)}, u32[]{:S(2)}, u32[]{:S(2)}) collective-permute-start(f32[25,1408]{1,0:T(8,128)S(1)} %collective-permute-done.6), channel_id=1, source_target_pairs={{0,1},{1,2},{2,3},{3,4},{4,5},{5,6},{6,7},{7,8},{8,9},{9,10},{10,1... | collective-permute-start | bytes 422408 | tf_op jit(solution)/shard_map/ppermute | solution.py:209
  229.7 26.1 %copy-start.5 = (f32[25,1408]{1,0:T(8,128)}, f32[25,1408]{1,0:T(8,128)S(1)}, u32[]{:S(2)}) copy-start(f32[25,1408]{1,0:T(8,128)S(1)} %collective-permute-done.1) | copy-start | bytes 422404
  229.7 8.4 %collective-permute-start.2 = (f32[25,1408]{1,0:T(8,128)S(1)}, f32[25,1408]{1,0:T(8,128)S(1)}, u32[]{:S(2)}, u32[]{:S(2)}) collective-permute-start(f32[25,1408]{1,0:T(8,128)S(1)} %collective-permute-done.1), channel_id=1, source_target_pairs={{0,11},{1,0},{2,1},{3,2},{4,3},{5,4},{6,5},{7,6},{8,7},{9,8},{10,9... | collective-permute-start | bytes 422408 | tf_op jit(solution)/shard_map/ppermute | solution.py:212
  236.1 19.7 %copy-start.4 = (f32[25,1408]{1,0:T(8,128)}, f32[25,1408]{1,0:T(8,128)S(1)}, u32[]{:S(2)}) copy-start(f32[25,1408]{1,0:T(8,128)S(1)} %collective-permute-done.7) | copy-start | bytes 422404
  236.1 8.8 %collective-permute-start.8 = (f32[25,1408]{1,0:T(8,128)S(1)}, f32[25,1408]{1,0:T(8,128)S(1)}, u32[]{:S(2)}, u32[]{:S(2)}) collective-permute-start(f32[25,1408]{1,0:T(8,128)S(1)} %collective-permute-done.7), channel_id=1, source_target_pairs={{0,1},{1,2},{2,3},{3,4},{4,5},{5,6},{6,7},{7,8},{8,9},{9,10},{10,1... | collective-permute-start | bytes 422408 | tf_op jit(solution)/shard_map/ppermute | solution.py:209
  238.1 17.7 %copy-start.7 = (f32[25,1408]{1,0:T(8,128)}, f32[25,1408]{1,0:T(8,128)S(1)}, u32[]{:S(2)}) copy-start(f32[25,1408]{1,0:T(8,128)S(1)} %collective-permute-done.2) | copy-start | bytes 422404
  238.2 8.7 %collective-permute-start.3 = (f32[25,1408]{1,0:T(8,128)S(1)}, f32[25,1408]{1,0:T(8,128)}, u32[]{:S(2)}, u32[]{:S(2)}) collective-permute-start(f32[25,1408]{1,0:T(8,128)S(1)} %collective-permute-done.2), channel_id=1, source_target_pairs={{0,11},{1,0},{2,1},{3,2},{4,3},{5,4},{6,5},{7,6},{8,7},{9,8},{10,9... | collective-permute-start | bytes 422408 | tf_op jit(solution)/shard_map/ppermute | solution.py:212
  245.0 8.7 %collective-permute-start.9 = (f32[25,1408]{1,0:T(8,128)S(1)}, f32[25,1408]{1,0:T(8,128)}, u32[]{:S(2)}, u32[]{:S(2)}) collective-permute-start(f32[25,1408]{1,0:T(8,128)S(1)} %collective-permute-done.8), channel_id=1, source_target_pairs={{0,1},{1,2},{2,3},{3,4},{4,5},{5,6},{6,7},{7,8},{8,9},{9,10},{10,1... | collective-permute-start | bytes 422408 | tf_op jit(solution)/shard_map/ppermute | solution.py:209
  246.9 43.1 %collective-permute-start.4 = (f32[25,1408]{1,0:T(8,128)}, f32[25,1408]{1,0:T(8,128)}, u32[]{:S(2)}, u32[]{:S(2)}) collective-permute-start(f32[25,1408]{1,0:T(8,128)} %collective-permute-done.3), channel_id=1, source_target_pairs={{0,11},{1,0},{2,1},{3,2},{4,3},{5,4},{6,5},{7,6},{8,7},{9,8},{10,9... | collective-permute-start | bytes 422408 | tf_op jit(solution)/shard_map/ppermute | solution.py:212
  253.7 44.6 %collective-permute-start.10 = (f32[25,1408]{1,0:T(8,128)}, f32[25,1408]{1,0:T(8,128)}, u32[]{:S(2)}, u32[]{:S(2)}) collective-permute-start(f32[25,1408]{1,0:T(8,128)} %collective-permute-done.9), channel_id=1, source_target_pairs={{0,1},{1,2},{2,3},{3,4},{4,5},{5,6},{6,7},{7,8},{8,9},{9,10},{10,1... | collective-permute-start | bytes 422408 | tf_op jit(solution)/shard_map/ppermute | solution.py:209
  329.6 15.4 %all-to-all-start.4 = ((f32[64,1,512]{2,1,0:T(1,128)}), f32[64,1,512]{2,1,0:T(1,128)S(1)}, u32[]{:S(2)}, u32[]{:S(2)}) async-start(f32[64,1,512]{2,1,0:T(1,128)} %broadcast_in_dim.114), calls=%async_computation.4 | async-start | bytes 262144 | tf_op jit(solution)/shard_map/all_to_all | solution.py:196
  (12 other events, 49.6 us)

commit v6 on v5

--- a/solution.py
+++ b/solution.py
@@ -159,7 +159,9 @@
     cut_len = -(-cut_len // 128) * 128
     pad_px = cut_len * layers - tile_px
     cut = jnp.pad(tiles_cut, ((0, 0), (0, pad_px))).reshape(n_foot, layers, cut_len)
-    from_column = lax.all_to_all(cut.transpose(1, 0, 2), "tile", 0, 0, tiled=True)
+    cut = cut.transpose(1, 0, 2).reshape(layers, n_foot, cut_len // 128, 128)
+    from_column = lax.all_to_all(cut, "tile", 0, 0, tiled=True)
+    from_column = from_column.reshape(layers, n_foot, cut_len)
 
     col_corners = lax.dynamic_index_in_dim(by_device, me_pos, 0, keepdims=False)
     col_rows = col_corners[:, 0:1] // tile_edge + span_idx[None, :]
@@ -167,9 +169,22 @@
     col_owner = tile_map[col_rows[:, :, None], col_cols[:, None, :]].reshape(layers, n_foot)
     col_owner = col_owner // tiles_dev
     to_owner = (col_owner[:, :, None] == jnp.arange(owners)[None, None, :]).astype(jnp.bfloat16)
-    outgoing = jnp.einsum("tsp,tsx->ptx", to_owner, from_column, preferred_element_type=jnp.float32)
-    outgoing = outgoing.astype(jnp.bfloat16)
-    returned = lax.all_to_all(outgoing, "pos", 0, 0, tiled=True)
+    by_owner = jnp.einsum("tsp,tsx->ptx", to_owner, from_column, preferred_element_type=jnp.float32)
+    by_owner = by_owner.astype(jnp.bfloat16).reshape(owners, layers * cut_len)
+
+    probe_part = jnp.stack([grad_re, grad_im])
+    piece_len = probe_part.size // owners
+    probe_hi = probe_part.reshape(owners, piece_len).astype(jnp.bfloat16)
+    probe_lo = (probe_part.reshape(owners, piece_len) - probe_hi.astype(jnp.float32)).astype(jnp.bfloat16)
+    slot_len = layers * cut_len + 2 * piece_len
+    slot_len = -(-slot_len // 128) * 128
+    outgoing = jnp.concatenate([by_owner, probe_hi, probe_lo], axis=1)
+    outgoing = jnp.pad(outgoing, ((0, 0), (0, slot_len - outgoing.shape[1])))
+    outgoing = outgoing.reshape(owners, slot_len // 128, 128)
+    returned = lax.all_to_all(outgoing, "pos", 0, 0, tiled=True).reshape(owners, slot_len)
+    from_owners = returned[:, : layers * cut_len].reshape(owners, layers, cut_len)
+    probe_back = returned[:, layers * cut_len : layers * cut_len + 2 * piece_len].astype(jnp.float32)
+    probe_row = jnp.sum(probe_back[:, :piece_len], axis=0) + jnp.sum(probe_back[:, piece_len:], axis=0)
 
     all_r = offsets[:, 0:1] // tile_edge
     all_c = offsets[:, 1:2] // tile_edge
@@ -180,13 +195,8 @@
     ).astype(jnp.int32)
     all_sel = one_hot(jnp.maximum(all_found - 1, 0), tiles_dev, all_found > 0)
     all_sel = all_sel.reshape(owners, layers, tiles_dev)
-    my_slice = jnp.einsum("qtk,qtx->kx", all_sel, returned, preferred_element_type=jnp.float32)
-
-    probe_part = jnp.stack([grad_re, grad_im])
-    piece_len = probe_part.size // owners
-    probe_row = jnp.sum(
-        lax.all_to_all(probe_part.reshape(owners, piece_len), "pos", 0, 0, tiled=True), axis=0
-    )
+    my_slice = jnp.einsum("qtk,qtx->kx", all_sel, from_owners, preferred_element_type=jnp.float32)
+
     probe_cut = jnp.pad(probe_row, (0, cut_len - piece_len))[None]
     gathered = ring_gather(jnp.concatenate([my_slice, probe_cut], axis=0), layers)
     slices = gathered[:, :tiles_dev]
@@ -212,10 +222,8 @@
             going_left = lax.ppermute(going_left, "tile", to_left)
             ahead.append(going_left)
     by_offset = [back[0]] + ahead + [back[size - d] for d in range(len(ahead) + 1, size)]
-    gathered = jnp.zeros((size,) + values.shape, values.dtype)
-    for offset, part in enumerate(by_offset):
-        gathered = lax.dynamic_update_index_in_dim(gathered, part, (me + offset) % size, 0)
-    return gathered
+    order = (jnp.arange(size, dtype=jnp.int32) - me) % size
+    return jnp.stack(by_offset)[order]
 
 
 def reduce_probe(probe_part, owners, layers):

time: 350 us -> 266 us (0.76)
  local copies, waits for them, and re-layouts: 95 us -> 31.3 us
  waiting for transfers between devices: 140 us -> 129 us
  starting transfers between devices: 84.3 us -> 78.4 us
    dynamic_update_slice x12 -> x0, local copies, waits for them, and re-layouts: 57.8 us -> none  [ring_gather(): lax.dynamic_update_index_in_dim(gathered, part, (me + offset) % size, 0)]
    all_to_all x3 -> x2, waiting for transfers between devices: 89.3 us -> 73.4 us  [the longest x1 53.2 us: per_device(): lax.all_to_all(outgoing, 'pos', 0, 0, tiled=True).reshape(owners, slot_len)]
    broadcast_in_dim x13 -> x0, local copies, waits for them, and re-layouts: 15.1 us -> none  [the longest x12 14.9 us: ring_gather(): lax.dynamic_update_index_in_dim(gathered, part, (me + offset) % size, 0)]
    all_to_all x3 -> x2, starting transfers between devices: 27.2 us -> 20.1 us  [the longest x1 12 us: per_device(): from_column = lax.all_to_all(cut, 'tile', 0, 0, tiled=True)]
    unnamed x46 -> x41, local copies, waits for them, and re-layouts: 2.25 us -> 8.67 us
    ppermute x5, starting transfers between devices: 18.9 us -> 25.3 us  [ring_gather(): going_left = lax.ppermute(going_left, 'tile', to_left)]
    ppermute x6, starting transfers between devices: 17.4 us -> 12.4 us  [ring_gather(): going_right = lax.ppermute(going_right, 'tile', to_right)]
    reshape x0 -> x7, local copies, waits for them, and re-layouts: none -> 4.35 us  [the longest x1 2.55 us: per_device(): outgoing = outgoing.reshape(owners, slot_len // 128, 128)]
  transfers between devices with their start and end apart: 16 -> 15, of which waited for: 13 -> 14; matrix products, arithmetic and copies ran while one was open for 19% -> 8% of each run, Pallas kernels for 0% -> 0%
where the time goes in v6:
time: 266 us; the launch traced here: 263 us
  waiting for transfers between devices  129 us (48%)
  starting transfers between devices  78.4 us (29%)
  local copies, waits for them, and re-layouts  31.3 us (12%)
  matrix products  14.3 us (5%)
  between operations  6.73 us (3%)
  other arithmetic  3.59 us (1%)
    all_to_all x1, waiting for transfers between devices, per_device(): lax.all_to_all(outgoing, 'pos', 0, 0, tiled=True).reshape(owners, slot_len)  53.2 us
    all_to_all x1, waiting for transfers between devices, per_device(): lax.all_to_all(chosen, 'pos', split_axis=0, concat_axis=0, tiled=True)  31.3 us
    ppermute x5, starting transfers between devices, ring_gather(): going_left = lax.ppermute(going_left, 'tile', to_left)  25.3 us
    all_to_all x1, waiting for transfers between devices, per_device(): from_column = lax.all_to_all(cut, 'tile', 0, 0, tiled=True)  20.2 us
    all_to_all x1, starting transfers between devices, per_device(): lax.all_to_all(chosen, 'pos', split_axis=0, concat_axis=0, tiled=True)  14.1 us
    ppermute x6, waiting for transfers between devices, ring_gather(): going_right = lax.ppermute(going_right, 'tile', to_right)  14 us
    ppermute x6, starting transfers between devices, ring_gather(): going_right = lax.ppermute(going_right, 'tile', to_right)  12.4 us
    all_to_all x1, starting transfers between devices, per_device(): from_column = lax.all_to_all(cut, 'tile', 0, 0, tiled=True)  12 us
  transfers between devices with their start and end apart: 15, of which 14 were waited for; matrix products, arithmetic and copies ran while one was open for 8% of the time, Pallas kernels for 0%

profile of v6, /device:TPU:6, one launch (start us, length us, event | category | flops | bytes accessed | tf_op | source)
XLA Modules:
  0.0 263.0 jit_solution(10745842439748171525)
XLA Ops:
  2.8 3.6 %gather_fusion = bf16[64,4,4096]{2,1,0:T(4,128)(2,1)} fusion(bf16[24,4,4096]{2,1,0:T(4,128)(2,1)S(1)} %copy-done, s32[1024]{0:T(1024)S(1)} %pad_clamp_fusion.2), kind=kCustom, calls=%fused_computation | custom fusion | bytes 4194560 | tf_op jit(solution)/shard_map/gather | solution.py:103
  6.3 14.1 %all-to-all-start = ((bf16[64,4,4096]{2,1,0:T(4,128)(2,1)}), bf16[64,4,4096]{2,1,0:T(4,128)(2,1)S(1)}, u32[]{:S(2)}, u32[]{:S(2)}) async-start(bf16[64,4,4096]{2,1,0:T(4,128)(2,1)} %gather_fusion), calls=%async_computation | async-start | bytes 4194304 | tf_op jit(solution)/shard_map/all_to_all | solution.py:121
  38.0 31.3 %all-to-all-done = bf16[64,4,4096]{2,1,0:T(4,128)(2,1)S(1)} async-done(((bf16[64,4,4096]{2,1,0:T(4,128)(2,1)}), bf16[64,4,4096]{2,1,0:T(4,128)(2,1)S(1)}, u32[]{:S(2)}, u32[]{:S(2)}) %all-to-all-start) | async-done | bytes 2097184 | tf_op jit(solution)/shard_map/all_to_all | solution.py:121
  79.3 12.0 %all-to-all-start.1 = ((bf16[12,9,11,128]{3,2,1,0:T(8,128)(2,1)}), bf16[12,9,11,128]{3,2,1,0:T(8,128)(2,1)S(1)}, u32[]{:S(2)}, u32[]{:S(2)}) async-start(bf16[12,9,11,128]{3,2,1,0:T(8,128)(2,1)} %copy.57), calls=%async_computation.1 | async-start | bytes 884736 | tf_op jit(solution)/shard_map/all_to_all | solution.py:163
  91.7 20.2 %all-to-all-done.1 = bf16[12,9,11,128]{3,2,1,0:T(8,128)(2,1)S(1)} async-done(((bf16[12,9,11,128]{3,2,1,0:T(8,128)(2,1)}), bf16[12,9,11,128]{3,2,1,0:T(8,128)(2,1)S(1)}, u32[]{:S(2)}, u32[]{:S(2)}) %all-to-all-start.1) | async-done | bytes 304160 | tf_op jit(solution)/shard_map/all_to_all | solution.py:163
  114.1 2.6 reshape.390
  116.6 8.1 %all-to-all-start.2 = ((bf16[64,140,128]{2,1,0:T(8,128)(2,1)}), bf16[64,140,128]{2,1,0:T(8,128)(2,1)S(1)}, u32[]{:S(2)}, u32[]{:S(2)}) async-start(bf16[64,140,128]{2,1,0:T(8,128)(2,1)} %reshape.390), calls=%async_computation.2 | async-start | bytes 4718592 | tf_op jit(solution)/shard_map/all_to_all | solution.py:184
  125.7 53.2 %all-to-all-done.2 = bf16[64,140,128]{2,1,0:T(8,128)(2,1)S(1)} async-done(((bf16[64,140,128]{2,1,0:T(8,128)(2,1)}), bf16[64,140,128]{2,1,0:T(8,128)(2,1)S(1)}, u32[]{:S(2)}, u32[]{:S(2)}) %all-to-all-start.2) | async-done | bytes 2293792 | tf_op jit(solution)/shard_map/all_to_all | solution.py:184
  180.2 4.0 %collective-permute-start = (f32[25,1408]{1,0:T(8,128)S(1)}, f32[25,1408]{1,0:T(8,128)S(1)}, u32[]{:S(2)}, u32[]{:S(2)}) collective-permute-start(f32[25,1408]{1,0:T(8,128)S(1)} %pad_maximum_fusion.7), channel_id=1, source_target_pairs={{0,11},{1,0},{2,1},{3,2},{4,3},{5,4},{6,5},{7,6},{8,7},{9,8},{10,9... | collective-permute-start | bytes 422408 | tf_op jit(solution)/shard_map/ppermute | solution.py:222
  184.2 2.8 %collective-permute-start.5 = (f32[25,1408]{1,0:T(8,128)S(1)}, f32[25,1408]{1,0:T(8,128)S(1)}, u32[]{:S(2)}, u32[]{:S(2)}) collective-permute-start(f32[25,1408]{1,0:T(8,128)S(1)} %pad_maximum_fusion.7), channel_id=1, source_target_pairs={{0,1},{1,2},{2,3},{3,4},{4,5},{5,6},{6,7},{7,8},{8,9},{9,10},{10,1... | collective-permute-start | bytes 422408 | tf_op jit(solution)/shard_map/ppermute | solution.py:219
  188.7 4.5 %collective-permute-start.1 = (f32[25,1408]{1,0:T(8,128)S(1)}, f32[25,1408]{1,0:T(8,128)S(1)}, u32[]{:S(2)}, u32[]{:S(2)}) collective-permute-start(f32[25,1408]{1,0:T(8,128)S(1)} %collective-permute-done), channel_id=1, source_target_pairs={{0,11},{1,0},{2,1},{3,2},{4,3},{5,4},{6,5},{7,6},{8,7},{9,8},{10,9... | collective-permute-start | bytes 422408 | tf_op jit(solution)/shard_map/ppermute | solution.py:222
  193.6 1.9 collective-permute-start.6
  197.9 5.6 %collective-permute-start.2 = (f32[25,1408]{1,0:T(8,128)S(1)}, f32[25,1408]{1,0:T(8,128)S(1)}, u32[]{:S(2)}, u32[]{:S(2)}) collective-permute-start(f32[25,1408]{1,0:T(8,128)S(1)} %collective-permute-done.1), channel_id=1, source_target_pairs={{0,11},{1,0},{2,1},{3,2},{4,3},{5,4},{6,5},{7,6},{8,7},{9,8},{10,9... | collective-permute-start | bytes 422408 | tf_op jit(solution)/shard_map/ppermute | solution.py:222
  204.0 1.9 collective-permute-start.7
  207.5 5.6 %collective-permute-start.3 = (f32[25,1408]{1,0:T(8,128)S(1)}, f32[25,1408]{1,0:T(8,128)S(1)}, u32[]{:S(2)}, u32[]{:S(2)}) collective-permute-start(f32[25,1408]{1,0:T(8,128)S(1)} %collective-permute-done.2), channel_id=1, source_target_pairs={{0,11},{1,0},{2,1},{3,2},{4,3},{5,4},{6,5},{7,6},{8,7},{9,8},{10,9... | collective-permute-start | bytes 422408 | tf_op jit(solution)/shard_map/ppermute | solution.py:222
  213.7 1.9 collective-permute-start.8
  216.4 5.6 %collective-permute-start.4 = (f32[25,1408]{1,0:T(8,128)S(1)}, f32[25,1408]{1,0:T(8,128)S(1)}, u32[]{:S(2)}, u32[]{:S(2)}) collective-permute-start(f32[25,1408]{1,0:T(8,128)S(1)} %collective-permute-done.3), channel_id=1, source_target_pairs={{0,11},{1,0},{2,1},{3,2},{4,3},{5,4},{6,5},{7,6},{8,7},{9,8},{10,9... | collective-permute-start | bytes 422408 | tf_op jit(solution)/shard_map/ppermute | solution.py:222
  222.5 1.9 collective-permute-start.9
  225.1 6.0 %collective-permute-done.9 = f32[25,1408]{1,0:T(8,128)S(1)} collective-permute-done((f32[25,1408]{1,0:T(8,128)S(1)}, f32[25,1408]{1,0:T(8,128)S(1)}, u32[]{:S(2)}, u32[]{:S(2)}) %collective-permute-start.9) | collective-permute-done | bytes 140832 | tf_op jit(solution)/shard_map/ppermute | solution.py:219
  233.7 6.0 %collective-permute-done.10 = f32[25,1408]{1,0:T(8,128)S(1)} collective-permute-done((f32[25,1408]{1,0:T(8,128)S(1)}, f32[25,1408]{1,0:T(8,128)S(1)}, u32[]{:S(2)}, u32[]{:S(2)}) %collective-permute-start.10) | collective-permute-done | bytes 140832 | tf_op jit(solution)/shard_map/ppermute | solution.py:219
  243.8 2.3 gather_fusion.4
  246.9 6.6 %all-to-all-start.3 = ((f32[64,1,512]{2,1,0:T(1,128)}), f32[64,1,512]{2,1,0:T(1,128)S(1)}, u32[]{:S(2)}, u32[]{:S(2)}) async-start(f32[64,1,512]{2,1,0:T(1,128)} %broadcast_in_dim.19), calls=%async_computation.3 | async-start | bytes 262144 | tf_op jit(solution)/shard_map/all_to_all | solution.py:206
  253.8 2.2 reshape.394
  256.0 6.3 %all-to-all-done.3 = f32[64,1,512]{2,1,0:T(1,128)S(1)} async-done(((f32[64,1,512]{2,1,0:T(1,128)}), f32[64,1,512]{2,1,0:T(1,128)S(1)}, u32[]{:S(2)}, u32[]{:S(2)}) %all-to-all-start.3) | async-done | bytes 131104 | tf_op jit(solution)/shard_map/all_to_all | solution.py:206
  (150 shorter events, 46.1 us)
Async XLA Ops:
  0.6 2.1 copy-start
  6.3 14.1 %copy-start.5 = (s32[768,2]{0,1:T(2,128)S(1)}, s32[768,2]{0,1:T(2,128)}, u32[]{:S(2)}) copy-start(s32[768,2]{0,1:T(2,128)} %param.7) | copy-start | bytes 18436
  6.3 20.1 %copy-start.1 = (s32[32,48]{1,0:T(8,128)S(1)}, s32[32,48]{1,0:T(8,128)}, u32[]{:S(2)}) copy-start(s32[32,48]{1,0:T(8,128)} %param.6) | copy-start | bytes 18436
  6.3 20.8 %copy-start.2 = (f32[2,128,128]{2,1,0:T(8,128)S(1)}, f32[2,128,128]{2,1,0:T(8,128)}, u32[]{:S(2)}) copy-start(f32[2,128,128]{2,1,0:T(8,128)} %param.8) | copy-start | bytes 393220
  6.3 63.0 %all-to-all-start = ((bf16[64,4,4096]{2,1,0:T(4,128)(2,1)}), bf16[64,4,4096]{2,1,0:T(4,128)(2,1)S(1)}, u32[]{:S(2)}, u32[]{:S(2)}) async-start(bf16[64,4,4096]{2,1,0:T(4,128)(2,1)} %gather_fusion), calls=%async_computation | async-start | bytes 4194304 | tf_op jit(solution)/shard_map/all_to_all | solution.py:121
  20.4 7.0 %copy-start.3 = (f32[1,128,128]{2,1,0:T(8,128)S(1)}, f32[1,128,128]{2,1,0:T(8,128)}, u32[]{:S(2)}) copy-start(f32[1,128,128]{2,1,0:T(8,128)} %param.9) | copy-start | bytes 196612
  70.7 2.0 copy-start.10
  72.6 2.6 copy-start.6
  72.6 2.6 copy-start.8
  73.0 2.8 %copy-start.7 = (f32[128,128]{0,1:T(8,128)S(1)}, f32[128,128]{0,1:T(8,128)}, u32[]{:S(2)}) copy-start(f32[128,128]{0,1:T(8,128)} %get-tuple-element.49) | copy-start | bytes 196612
  79.3 32.6 %all-to-all-start.1 = ((bf16[12,9,11,128]{3,2,1,0:T(8,128)(2,1)}), bf16[12,9,11,128]{3,2,1,0:T(8,128)(2,1)S(1)}, u32[]{:S(2)}, u32[]{:S(2)}) async-start(bf16[12,9,11,128]{3,2,1,0:T(8,128)(2,1)} %copy.57), calls=%async_computation.1 | async-start | bytes 884736 | tf_op jit(solution)/shard_map/all_to_all | solution.py:163
  116.6 62.3 %all-to-all-start.2 = ((bf16[64,140,128]{2,1,0:T(8,128)(2,1)}), bf16[64,140,128]{2,1,0:T(8,128)(2,1)S(1)}, u32[]{:S(2)}, u32[]{:S(2)}) async-start(bf16[64,140,128]{2,1,0:T(8,128)(2,1)} %reshape.390), calls=%async_computation.2 | async-start | bytes 4718592 | tf_op jit(solution)/shard_map/all_to_all | solution.py:184
  180.2 8.5 %collective-permute-start = (f32[25,1408]{1,0:T(8,128)S(1)}, f32[25,1408]{1,0:T(8,128)S(1)}, u32[]{:S(2)}, u32[]{:S(2)}) collective-permute-start(f32[25,1408]{1,0:T(8,128)S(1)} %pad_maximum_fusion.7), channel_id=1, source_target_pairs={{0,11},{1,0},{2,1},{3,2},{4,3},{5,4},{6,5},{7,6},{8,7},{9,8},{10,9... | collective-permute-start | bytes 422408 | tf_op jit(solution)/shard_map/ppermute | solution.py:222
  184.2 9.3 %collective-permute-start.5 = (f32[25,1408]{1,0:T(8,128)S(1)}, f32[25,1408]{1,0:T(8,128)S(1)}, u32[]{:S(2)}, u32[]{:S(2)}) collective-permute-start(f32[25,1408]{1,0:T(8,128)S(1)} %pad_maximum_fusion.7), channel_id=1, source_target_pairs={{0,1},{1,2},{2,3},{3,4},{4,5},{5,6},{6,7},{7,8},{8,9},{9,10},{10,1... | collective-permute-start | bytes 422408 | tf_op jit(solution)/shard_map/ppermute | solution.py:219
  188.7 9.1 %collective-permute-start.1 = (f32[25,1408]{1,0:T(8,128)S(1)}, f32[25,1408]{1,0:T(8,128)S(1)}, u32[]{:S(2)}, u32[]{:S(2)}) collective-permute-start(f32[25,1408]{1,0:T(8,128)S(1)} %collective-permute-done), channel_id=1, source_target_pairs={{0,11},{1,0},{2,1},{3,2},{4,3},{5,4},{6,5},{7,6},{8,7},{9,8},{10,9... | collective-permute-start | bytes 422408 | tf_op jit(solution)/shard_map/ppermute | solution.py:222
  193.6 10.5 %collective-permute-start.6 = (f32[25,1408]{1,0:T(8,128)S(1)}, f32[25,1408]{1,0:T(8,128)S(1)}, u32[]{:S(2)}, u32[]{:S(2)}) collective-permute-start(f32[25,1408]{1,0:T(8,128)S(1)} %collective-permute-done.5), channel_id=1, source_target_pairs={{0,1},{1,2},{2,3},{3,4},{4,5},{5,6},{6,7},{7,8},{8,9},{9,10},{10,1... | collective-permute-start | bytes 422408 | tf_op jit(solution)/shard_map/ppermute | solution.py:219
  197.9 9.7 %collective-permute-start.2 = (f32[25,1408]{1,0:T(8,128)S(1)}, f32[25,1408]{1,0:T(8,128)S(1)}, u32[]{:S(2)}, u32[]{:S(2)}) collective-permute-start(f32[25,1408]{1,0:T(8,128)S(1)} %collective-permute-done.1), channel_id=1, source_target_pairs={{0,11},{1,0},{2,1},{3,2},{4,3},{5,4},{6,5},{7,6},{8,7},{9,8},{10,9... | collective-permute-start | bytes 422408 | tf_op jit(solution)/shard_map/ppermute | solution.py:222
  204.0 9.7 %collective-permute-start.7 = (f32[25,1408]{1,0:T(8,128)S(1)}, f32[25,1408]{1,0:T(8,128)S(1)}, u32[]{:S(2)}, u32[]{:S(2)}) collective-permute-start(f32[25,1408]{1,0:T(8,128)S(1)} %collective-permute-done.6), channel_id=1, source_target_pairs={{0,1},{1,2},{2,3},{3,4},{4,5},{5,6},{6,7},{7,8},{8,9},{9,10},{10,1... | collective-permute-start | bytes 422408 | tf_op jit(solution)/shard_map/ppermute | solution.py:219
  207.5 8.8 %collective-permute-start.3 = (f32[25,1408]{1,0:T(8,128)S(1)}, f32[25,1408]{1,0:T(8,128)S(1)}, u32[]{:S(2)}, u32[]{:S(2)}) collective-permute-start(f32[25,1408]{1,0:T(8,128)S(1)} %collective-permute-done.2), channel_id=1, source_target_pairs={{0,11},{1,0},{2,1},{3,2},{4,3},{5,4},{6,5},{7,6},{8,7},{9,8},{10,9... | collective-permute-start | bytes 422408 | tf_op jit(solution)/shard_map/ppermute | solution.py:222
  213.7 8.8 %collective-permute-start.8 = (f32[25,1408]{1,0:T(8,128)S(1)}, f32[25,1408]{1,0:T(8,128)S(1)}, u32[]{:S(2)}, u32[]{:S(2)}) collective-permute-start(f32[25,1408]{1,0:T(8,128)S(1)} %collective-permute-done.7), channel_id=1, source_target_pairs={{0,1},{1,2},{2,3},{3,4},{4,5},{5,6},{6,7},{7,8},{8,9},{9,10},{10,1... | collective-permute-start | bytes 422408 | tf_op jit(solution)/shard_map/ppermute | solution.py:219
  216.4 16.7 %collective-permute-start.4 = (f32[25,1408]{1,0:T(8,128)S(1)}, f32[25,1408]{1,0:T(8,128)S(1)}, u32[]{:S(2)}, u32[]{:S(2)}) collective-permute-start(f32[25,1408]{1,0:T(8,128)S(1)} %collective-permute-done.3), channel_id=1, source_target_pairs={{0,11},{1,0},{2,1},{3,2},{4,3},{5,4},{6,5},{7,6},{8,7},{9,8},{10,9... | collective-permute-start | bytes 422408 | tf_op jit(solution)/shard_map/ppermute | solution.py:222
  222.5 8.6 %collective-permute-start.9 = (f32[25,1408]{1,0:T(8,128)S(1)}, f32[25,1408]{1,0:T(8,128)S(1)}, u32[]{:S(2)}, u32[]{:S(2)}) collective-permute-start(f32[25,1408]{1,0:T(8,128)S(1)} %collective-permute-done.8), channel_id=1, source_target_pairs={{0,1},{1,2},{2,3},{3,4},{4,5},{5,6},{6,7},{7,8},{8,9},{9,10},{10,1... | collective-permute-start | bytes 422408 | tf_op jit(solution)/shard_map/ppermute | solution.py:219
  231.1 8.6 %collective-permute-start.10 = (f32[25,1408]{1,0:T(8,128)S(1)}, f32[25,1408]{1,0:T(8,128)S(1)}, u32[]{:S(2)}, u32[]{:S(2)}) collective-permute-start(f32[25,1408]{1,0:T(8,128)S(1)} %collective-permute-done.9), channel_id=1, source_target_pairs={{0,1},{1,2},{2,3},{3,4},{4,5},{5,6},{6,7},{7,8},{8,9},{9,10},{10,1... | collective-permute-start | bytes 422408 | tf_op jit(solution)/shard_map/ppermute | solution.py:219
  246.9 15.4 %all-to-all-start.3 = ((f32[64,1,512]{2,1,0:T(1,128)}), f32[64,1,512]{2,1,0:T(1,128)S(1)}, u32[]{:S(2)}, u32[]{:S(2)}) async-start(f32[64,1,512]{2,1,0:T(1,128)} %broadcast_in_dim.19), calls=%async_computation.3 | async-start | bytes 262144 | tf_op jit(solution)/shard_map/all_to_all | solution.py:206
  (3 other events, 4.6 us)

commit v7 on v6

--- a/solution.py
+++ b/solution.py
@@ -197,33 +197,35 @@
     all_sel = all_sel.reshape(owners, layers, tiles_dev)
     my_slice = jnp.einsum("qtk,qtx->kx", all_sel, from_owners, preferred_element_type=jnp.float32)
 
-    probe_cut = jnp.pad(probe_row, (0, cut_len - piece_len))[None]
-    gathered = ring_gather(jnp.concatenate([my_slice, probe_cut], axis=0), layers)
-    slices = gathered[:, :tiles_dev]
-    tile_total = slices.transpose(1, 0, 2).reshape(tiles_dev, layers * cut_len)[:, :tile_px]
-    probe_piece = jnp.sum(gathered[:, tiles_dev, :piece_len], axis=0)
+    spread = jnp.broadcast_to(probe_row[None], (layers, piece_len))
+    probe_piece = jnp.sum(lax.all_to_all(spread, "tile", 0, 0, tiled=True), axis=0)
     spread = jnp.broadcast_to(probe_piece[None], (owners, piece_len))
     probe_total = lax.all_to_all(spread, "pos", 0, 0, tiled=True).reshape(probe_part.shape)
+    slices = ring_gather(my_slice, layers)
+    tile_total = slices.transpose(1, 0, 2).reshape(tiles_dev, layers * cut_len)[:, :tile_px]
     return (tile_total.reshape(tiles_dev, n_comps, tile_edge * tile_edge), probe_total)
 
 
-def ring_gather(values, size):
+def ring_gather(values, size, stride=3):
     me = lax.axis_index("tile")
-    to_right = [(i, (i + 1) % size) for i in range(size)]
-    to_left = [(i, (i - 1) % size) for i in range(size)]
-    back = [values]
-    ahead = []
-    going_right = values
-    going_left = values
-    for step in range(1, size // 2 + 1):
-        going_right = lax.ppermute(going_right, "tile", to_right)
-        back.append(going_right)
-        if step < size - size // 2:
-            going_left = lax.ppermute(going_left, "tile", to_left)
-            ahead.append(going_left)
-    by_offset = [back[0]] + ahead + [back[size - d] for d in range(len(ahead) + 1, size)]
+    if size % stride or size <= stride:
+        stride = 1
+    groups = size // stride
+
+    def shifted(x, shift):
+        return lax.ppermute(x, "tile", [(i, (i + shift) % size) for i in range(size)])
+
+    bundle = jnp.stack([values] + [shifted(values, stride * w) for w in range(1, groups)])
+    bundles = [bundle]
+    source = {(-stride * w) % size: (0, w) for w in range(groups)}
+    for r in range(1, stride):
+        shift = r if r <= stride // 2 else r - stride
+        bundles.append(shifted(bundle, shift))
+        for w in range(groups):
+            source[(-shift - stride * w) % size] = (r, w)
+    by_offset = jnp.stack([bundles[source[d][0]][source[d][1]] for d in range(size)])
     order = (jnp.arange(size, dtype=jnp.int32) - me) % size
-    return jnp.stack(by_offset)[order]
+    return by_offset[order]
 
 
 def reduce_probe(probe_part, owners, layers):

time: 266 us -> 267 us (level)
  blocking collectives: 0 us -> 17.9 us
  starting transfers between devices: 78.4 us -> 64.8 us
    all_to_all x0 -> x1, blocking collectives: none -> 17.9 us  [per_device(): lax.all_to_all(spread, 'tile', 0, 0, tiled=True)]
    ppermute x11 -> x5, starting transfers between devices: 37.6 us -> 22.3 us  [shifted(): lax.ppermute(x, 'tile', [(i, (i + shift) % size) for i in range(size)])]
    ppermute x11 -> x5, waiting for transfers between devices: 17.6 us -> 17.3 us  [shifted(): lax.ppermute(x, 'tile', [(i, (i + shift) % size) for i in range(size)])]
    unnamed x41 -> x40, local copies, waits for them, and re-layouts: 8.67 us -> 8.36 us
  transfers between devices with their start and end apart: 15 -> 9, of which waited for: 14 -> 7; matrix products, arithmetic and copies ran while one was open for 8% -> 6% of each run, Pallas kernels for 0% -> 0%
where the time goes in v7:
time: 267 us; the launch traced here: 266 us
  waiting for transfers between devices  128 us (48%)
  starting transfers between devices  64.8 us (24%)
  local copies, waits for them, and re-layouts  30.8 us (12%)
  blocking collectives  17.9 us (7%)
  matrix products  14.9 us (6%)
  between operations  6.63 us (2%)
  other arithmetic  2.95 us (1%)
    all_to_all x1, waiting for transfers between devices, per_device(): lax.all_to_all(outgoing, 'pos', 0, 0, tiled=True).reshape(owners, slot_len)  53.3 us
    all_to_all x1, waiting for transfers between devices, per_device(): lax.all_to_all(chosen, 'pos', split_axis=0, concat_axis=0, tiled=True)  31.3 us
    ppermute x5, starting transfers between devices, shifted(): lax.ppermute(x, 'tile', [(i, (i + shift) % size) for i in range(size)])  22.3 us
    all_to_all x1, waiting for transfers between devices, per_device(): from_column = lax.all_to_all(cut, 'tile', 0, 0, tiled=True)  20.2 us
    all_to_all x1, blocking collectives, per_device(): lax.all_to_all(spread, 'tile', 0, 0, tiled=True)  17.9 us
    ppermute x5, waiting for transfers between devices, shifted(): lax.ppermute(x, 'tile', [(i, (i + shift) % size) for i in range(size)])  17.3 us
    all_to_all x1, starting transfers between devices, per_device(): lax.all_to_all(chosen, 'pos', split_axis=0, concat_axis=0, tiled=True)  14.1 us
    all_to_all x1, starting transfers between devices, per_device(): from_column = lax.all_to_all(cut, 'tile', 0, 0, tiled=True)  12 us
  transfers between devices with their start and end apart: 9, of which 7 were waited for; matrix products, arithmetic and copies ran while one was open for 6% of the time, Pallas kernels for 0%

profile of v7, /device:TPU:6, one launch (start us, length us, event | category | flops | bytes accessed | tf_op | source)
XLA Modules:
  0.0 266.4 jit_solution(16127606063630781711)
XLA Ops:
  2.8 3.6 %gather_fusion = bf16[64,4,4096]{2,1,0:T(4,128)(2,1)} fusion(bf16[24,4,4096]{2,1,0:T(4,128)(2,1)S(1)} %copy-done, s32[1024]{0:T(1024)S(1)} %pad_clamp_fusion.2), kind=kCustom, calls=%fused_computation | custom fusion | bytes 4194560 | tf_op jit(solution)/shard_map/gather | solution.py:103
  6.3 14.1 %all-to-all-start = ((bf16[64,4,4096]{2,1,0:T(4,128)(2,1)}), bf16[64,4,4096]{2,1,0:T(4,128)(2,1)S(1)}, u32[]{:S(2)}, u32[]{:S(2)}) async-start(bf16[64,4,4096]{2,1,0:T(4,128)(2,1)} %gather_fusion), calls=%async_computation | async-start | bytes 4194304 | tf_op jit(solution)/shard_map/all_to_all | solution.py:121
  27.5 1.9 gather_fusion.3
  35.6 1.2 fusion.219
  38.0 31.3 %all-to-all-done = bf16[64,4,4096]{2,1,0:T(4,128)(2,1)S(1)} async-done(((bf16[64,4,4096]{2,1,0:T(4,128)(2,1)}), bf16[64,4,4096]{2,1,0:T(4,128)(2,1)S(1)}, u32[]{:S(2)}, u32[]{:S(2)}) %all-to-all-start) | async-done | bytes 2097184 | tf_op jit(solution)/shard_map/all_to_all | solution.py:121
  79.3 12.0 %all-to-all-start.1 = ((bf16[12,9,11,128]{3,2,1,0:T(8,128)(2,1)}), bf16[12,9,11,128]{3,2,1,0:T(8,128)(2,1)S(1)}, u32[]{:S(2)}, u32[]{:S(2)}) async-start(bf16[12,9,11,128]{3,2,1,0:T(8,128)(2,1)} %copy.75), calls=%async_computation.1 | async-start | bytes 884736 | tf_op jit(solution)/shard_map/all_to_all | solution.py:163
  91.7 20.2 %all-to-all-done.1 = bf16[12,9,11,128]{3,2,1,0:T(8,128)(2,1)S(1)} async-done(((bf16[12,9,11,128]{3,2,1,0:T(8,128)(2,1)}), bf16[12,9,11,128]{3,2,1,0:T(8,128)(2,1)S(1)}, u32[]{:S(2)}, u32[]{:S(2)}) %all-to-all-start.1) | async-done | bytes 304160 | tf_op jit(solution)/shard_map/all_to_all | solution.py:163
  112.1 1.6 fusion
  114.1 2.5 reshape.401
  116.6 8.1 %all-to-all-start.2 = ((bf16[64,140,128]{2,1,0:T(8,128)(2,1)}), bf16[64,140,128]{2,1,0:T(8,128)(2,1)S(1)}, u32[]{:S(2)}, u32[]{:S(2)}) async-start(bf16[64,140,128]{2,1,0:T(8,128)(2,1)} %reshape.401), calls=%async_computation.2 | async-start | bytes 4718592 | tf_op jit(solution)/shard_map/all_to_all | solution.py:184
  125.6 53.3 %all-to-all-done.2 = bf16[64,140,128]{2,1,0:T(8,128)(2,1)S(1)} async-done(((bf16[64,140,128]{2,1,0:T(8,128)(2,1)}), bf16[64,140,128]{2,1,0:T(8,128)(2,1)S(1)}, u32[]{:S(2)}, u32[]{:S(2)}) %all-to-all-start.2) | async-done | bytes 2293792 | tf_op jit(solution)/shard_map/all_to_all | solution.py:184
  180.8 4.7 %collective-permute-start.1 = (f32[24,1408]{1,0:T(8,128)S(1)}, f32[24,1408]{1,0:T(8,128)S(1)}, u32[]{:S(2)}, u32[]{:S(2)}) collective-permute-start(f32[24,1408]{1,0:T(8,128)S(1)} %bitcast.218), channel_id=1, source_target_pairs={{0,6},{1,7},{2,8},{3,9},{4,10},{5,11},{6,0},{7,1},{8,2},{9,3},{10,... | collective-permute-start | bytes 405512 | tf_op jit(solution)/shard_map/ppermute | solution.py:216
  185.5 5.4 %collective-permute-start = (f32[24,1408]{1,0:T(8,128)S(1)}, f32[24,1408]{1,0:T(8,128)S(1)}, u32[]{:S(2)}, u32[]{:S(2)}) collective-permute-start(f32[24,1408]{1,0:T(8,128)S(1)} %bitcast.219), channel_id=1, source_target_pairs={{0,3},{1,4},{2,5},{3,6},{4,7},{5,8},{6,9},{7,10},{8,11},{9,0},{10,... | collective-permute-start | bytes 405512 | tf_op jit(solution)/shard_map/ppermute | solution.py:216
  190.9 3.4 %collective-permute-start.2 = (f32[24,1408]{1,0:T(8,128)S(1)}, f32[24,1408]{1,0:T(8,128)S(1)}, u32[]{:S(2)}, u32[]{:S(2)}) collective-permute-start(f32[24,1408]{1,0:T(8,128)S(1)} %bitcast.220), channel_id=1, source_target_pairs={{0,9},{1,10},{2,11},{3,0},{4,1},{5,2},{6,3},{7,4},{8,5},{9,6},{10,... | collective-permute-start | bytes 405512 | tf_op jit(solution)/shard_map/ppermute | solution.py:216
  194.3 5.9 %collective-permute-done.1 = f32[24,1408]{1,0:T(8,128)S(1)} collective-permute-done((f32[24,1408]{1,0:T(8,128)S(1)}, f32[24,1408]{1,0:T(8,128)S(1)}, u32[]{:S(2)}, u32[]{:S(2)}) %collective-permute-start.1) | collective-permute-done | bytes 135200 | tf_op jit(solution)/shard_map/ppermute | solution.py:216
  200.2 3.5 %collective-permute-done = f32[24,1408]{1,0:T(8,128)S(1)} collective-permute-done((f32[24,1408]{1,0:T(8,128)S(1)}, f32[24,1408]{1,0:T(8,128)S(1)}, u32[]{:S(2)}, u32[]{:S(2)}) %collective-permute-start) | collective-permute-done | bytes 135200 | tf_op jit(solution)/shard_map/ppermute | solution.py:216
  203.8 6.2 %collective-permute-start.3 = (f32[4,24,1408]{2,1,0:T(8,128)S(1)}, f32[4,24,1408]{2,1,0:T(8,128)S(1)}, u32[]{:S(2)}, u32[]{:S(2)}) collective-permute-start(f32[4,24,1408]{2,1,0:T(8,128)S(1)} %pad_maximum_fusion.1), channel_id=1, source_target_pairs={{0,11},{1,0},{2,1},{3,2},{4,3},{5,4},{6,5},{7,6},{8,7},{9,8},{10,9... | collective-permute-start | bytes 1622024 | tf_op jit(solution)/shard_map/ppermute | solution.py:216
  210.1 17.9 %all_to_all.27 = f32[12,1,512]{2,1,0:T(1,128)S(1)} all-to-all(f32[12,1,512]{2,1,0:T(1,128)S(1)} %broadcast_in_dim.18), channel_id=1, replica_groups=mesh['pos'=64,'tile'=12] {'tile'}, dimensions={0} | all-to-all | bytes 49152 | tf_op jit(solution)/shard_map/all_to_all | solution.py:201
  228.8 8.3 %all-to-all-start.4 = ((f32[64,1,512]{2,1,0:T(1,128)}), f32[64,1,512]{2,1,0:T(1,128)S(1)}, u32[]{:S(2)}, u32[]{:S(2)}) async-start(f32[64,1,512]{2,1,0:T(1,128)} %broadcast_in_dim.19), calls=%async_computation.4 | async-start | bytes 262144 | tf_op jit(solution)/shard_map/all_to_all | solution.py:203
  237.1 2.5 collective-permute-start.4
  239.7 6.3 %all-to-all-done.4 = f32[64,1,512]{2,1,0:T(1,128)S(1)} async-done(((f32[64,1,512]{2,1,0:T(1,128)}), f32[64,1,512]{2,1,0:T(1,128)S(1)}, u32[]{:S(2)}, u32[]{:S(2)}) %all-to-all-start.4) | async-done | bytes 131104 | tf_op jit(solution)/shard_map/all_to_all | solution.py:203
  246.7 7.9 %collective-permute-done.4 = f32[4,24,1408]{2,1,0:T(8,128)S(1)} collective-permute-done((f32[4,24,1408]{2,1,0:T(8,128)S(1)}, f32[4,24,1408]{2,1,0:T(8,128)S(1)}, u32[]{:S(2)}, u32[]{:S(2)}) %collective-permute-start.4) | collective-permute-done | bytes 540704 | tf_op jit(solution)/shard_map/ppermute | solution.py:216
  261.2 2.1 gather_fusion.4
  263.5 2.2 reshape.405
  (136 shorter events, 33.6 us)
Async XLA Ops:
  0.6 2.1 copy-start
  6.3 14.1 %copy-start.5 = (s32[768,2]{0,1:T(2,128)S(1)}, s32[768,2]{0,1:T(2,128)}, u32[]{:S(2)}) copy-start(s32[768,2]{0,1:T(2,128)} %param.7) | copy-start | bytes 18436
  6.3 20.1 %copy-start.1 = (s32[32,48]{1,0:T(8,128)S(1)}, s32[32,48]{1,0:T(8,128)}, u32[]{:S(2)}) copy-start(s32[32,48]{1,0:T(8,128)} %param.6) | copy-start | bytes 18436
  6.3 63.0 %all-to-all-start = ((bf16[64,4,4096]{2,1,0:T(4,128)(2,1)}), bf16[64,4,4096]{2,1,0:T(4,128)(2,1)S(1)}, u32[]{:S(2)}, u32[]{:S(2)}) async-start(bf16[64,4,4096]{2,1,0:T(4,128)(2,1)} %gather_fusion), calls=%async_computation | async-start | bytes 4194304 | tf_op jit(solution)/shard_map/all_to_all | solution.py:121
  27.4 1.9 copy-start.3
  27.5 2.0 copy-start.2
  71.2 0.8 copy-start.9
  71.2 0.9 copy-start.11
  71.2 1.5 copy-start.10
  71.7 1.4 copy-start.4
  73.1 2.1 copy-start.6
  73.1 2.1 copy-start.8
  73.7 2.1 copy-start.7
  79.3 32.6 %all-to-all-start.1 = ((bf16[12,9,11,128]{3,2,1,0:T(8,128)(2,1)}), bf16[12,9,11,128]{3,2,1,0:T(8,128)(2,1)S(1)}, u32[]{:S(2)}, u32[]{:S(2)}) async-start(bf16[12,9,11,128]{3,2,1,0:T(8,128)(2,1)} %copy.75), calls=%async_computation.1 | async-start | bytes 884736 | tf_op jit(solution)/shard_map/all_to_all | solution.py:163
  116.6 62.3 %all-to-all-start.2 = ((bf16[64,140,128]{2,1,0:T(8,128)(2,1)}), bf16[64,140,128]{2,1,0:T(8,128)(2,1)S(1)}, u32[]{:S(2)}, u32[]{:S(2)}) async-start(bf16[64,140,128]{2,1,0:T(8,128)(2,1)} %reshape.401), calls=%async_computation.2 | async-start | bytes 4718592 | tf_op jit(solution)/shard_map/all_to_all | solution.py:184
  180.8 19.5 %collective-permute-start.1 = (f32[24,1408]{1,0:T(8,128)S(1)}, f32[24,1408]{1,0:T(8,128)S(1)}, u32[]{:S(2)}, u32[]{:S(2)}) collective-permute-start(f32[24,1408]{1,0:T(8,128)S(1)} %bitcast.218), channel_id=1, source_target_pairs={{0,6},{1,7},{2,8},{3,9},{4,10},{5,11},{6,0},{7,1},{8,2},{9,3},{10,... | collective-permute-start | bytes 405512 | tf_op jit(solution)/shard_map/ppermute | solution.py:216
  185.5 18.2 %collective-permute-start = (f32[24,1408]{1,0:T(8,128)S(1)}, f32[24,1408]{1,0:T(8,128)S(1)}, u32[]{:S(2)}, u32[]{:S(2)}) collective-permute-start(f32[24,1408]{1,0:T(8,128)S(1)} %bitcast.219), channel_id=1, source_target_pairs={{0,3},{1,4},{2,5},{3,6},{4,7},{5,8},{6,9},{7,10},{8,11},{9,0},{10,... | collective-permute-start | bytes 405512 | tf_op jit(solution)/shard_map/ppermute | solution.py:216
  190.9 12.8 %collective-permute-start.2 = (f32[24,1408]{1,0:T(8,128)S(1)}, f32[24,1408]{1,0:T(8,128)S(1)}, u32[]{:S(2)}, u32[]{:S(2)}) collective-permute-start(f32[24,1408]{1,0:T(8,128)S(1)} %bitcast.220), channel_id=1, source_target_pairs={{0,9},{1,10},{2,11},{3,0},{4,1},{5,2},{6,3},{7,4},{8,5},{9,6},{10,... | collective-permute-start | bytes 405512 | tf_op jit(solution)/shard_map/ppermute | solution.py:216
  203.8 42.2 %collective-permute-start.3 = (f32[4,24,1408]{2,1,0:T(8,128)S(1)}, f32[4,24,1408]{2,1,0:T(8,128)S(1)}, u32[]{:S(2)}, u32[]{:S(2)}) collective-permute-start(f32[4,24,1408]{2,1,0:T(8,128)S(1)} %pad_maximum_fusion.1), channel_id=1, source_target_pairs={{0,11},{1,0},{2,1},{3,2},{4,3},{5,4},{6,5},{7,6},{8,7},{9,8},{10,9... | collective-permute-start | bytes 1622024 | tf_op jit(solution)/shard_map/ppermute | solution.py:216
  228.8 17.2 %all-to-all-start.4 = ((f32[64,1,512]{2,1,0:T(1,128)}), f32[64,1,512]{2,1,0:T(1,128)S(1)}, u32[]{:S(2)}, u32[]{:S(2)}) async-start(f32[64,1,512]{2,1,0:T(1,128)} %broadcast_in_dim.19), calls=%async_computation.4 | async-start | bytes 262144 | tf_op jit(solution)/shard_map/all_to_all | solution.py:203
  237.1 17.4 %collective-permute-start.4 = (f32[4,24,1408]{2,1,0:T(8,128)S(1)}, f32[4,24,1408]{2,1,0:T(8,128)S(1)}, u32[]{:S(2)}, u32[]{:S(2)}) collective-permute-start(f32[4,24,1408]{2,1,0:T(8,128)S(1)} %pad_maximum_fusion.1), channel_id=1, source_target_pairs={{0,1},{1,2},{2,3},{3,4},{4,5},{5,6},{6,7},{7,8},{8,9},{9,10},{10,1... | collective-permute-start | bytes 1622024 | tf_op jit(solution)/shard_map/ppermute | solution.py:216

commit v8 on v7

--- a/solution.py
+++ b/solution.py
@@ -197,12 +197,13 @@
     all_sel = all_sel.reshape(owners, layers, tiles_dev)
     my_slice = jnp.einsum("qtk,qtx->kx", all_sel, from_owners, preferred_element_type=jnp.float32)
 
-    spread = jnp.broadcast_to(probe_row[None], (layers, piece_len))
-    probe_piece = jnp.sum(lax.all_to_all(spread, "tile", 0, 0, tiled=True), axis=0)
+    probe_cut = jnp.pad(probe_row, (0, cut_len - piece_len))[None]
+    gathered = ring_gather(jnp.concatenate([my_slice, probe_cut], axis=0), layers)
+    slices = gathered[:, :tiles_dev]
+    tile_total = slices.transpose(1, 0, 2).reshape(tiles_dev, layers * cut_len)[:, :tile_px]
+    probe_piece = jnp.sum(gathered[:, tiles_dev, :piece_len], axis=0)
     spread = jnp.broadcast_to(probe_piece[None], (owners, piece_len))
     probe_total = lax.all_to_all(spread, "pos", 0, 0, tiled=True).reshape(probe_part.shape)
-    slices = ring_gather(my_slice, layers)
-    tile_total = slices.transpose(1, 0, 2).reshape(tiles_dev, layers * cut_len)[:, :tile_px]
     return (tile_total.reshape(tiles_dev, n_comps, tile_edge * tile_edge), probe_total)
 
 

time: 267 us -> 268 us (level)
  waiting for transfers between devices: 128 us -> 147 us
  blocking collectives: 17.9 us -> 0 us
  starting transfers between devices: 64.8 us -> 60.3 us
    ppermute x5, waiting for transfers between devices: 17.3 us -> 36.2 us  [shifted(): lax.ppermute(x, 'tile', [(i, (i + shift) % size) for i in range(size)])]
    all_to_all x1 -> x0, blocking collectives: 17.9 us -> none  [per_device(): lax.all_to_all(spread, 'tile', 0, 0, tiled=True)]
    ppermute x5, starting transfers between devices: 22.3 us -> 18.8 us  [shifted(): lax.ppermute(x, 'tile', [(i, (i + shift) % size) for i in range(size)])]
    unnamed x40 -> x41, local copies, waits for them, and re-layouts: 8.36 us -> 8.68 us
  transfers between devices with their start and end apart: 9 -> 9, of which waited for: 7 -> 9; matrix products, arithmetic and copies ran while one was open for 6% -> 7% of each run, Pallas kernels for 0% -> 0%
where the time goes in v8:
time: 268 us; the launch traced here: 265 us
  waiting for transfers between devices  147 us (55%)
  starting transfers between devices  60.3 us (22%)
  local copies, waits for them, and re-layouts  32.5 us (12%)
  matrix products  14.2 us (5%)
  between operations  6.69 us (2%)
  other arithmetic  3.66 us (1%)
    all_to_all x1, waiting for transfers between devices, per_device(): lax.all_to_all(outgoing, 'pos', 0, 0, tiled=True).reshape(owners, slot_len)  53.3 us
    ppermute x5, waiting for transfers between devices, shifted(): lax.ppermute(x, 'tile', [(i, (i + shift) % size) for i in range(size)])  36.2 us
    all_to_all x1, waiting for transfers between devices, per_device(): lax.all_to_all(chosen, 'pos', split_axis=0, concat_axis=0, tiled=True)  31.3 us
    all_to_all x1, waiting for transfers between devices, per_device(): from_column = lax.all_to_all(cut, 'tile', 0, 0, tiled=True)  20.2 us
    ppermute x5, starting transfers between devices, shifted(): lax.ppermute(x, 'tile', [(i, (i + shift) % size) for i in range(size)])  18.8 us
    all_to_all x1, starting transfers between devices, per_device(): lax.all_to_all(chosen, 'pos', split_axis=0, concat_axis=0, tiled=True)  14.1 us
    all_to_all x1, starting transfers between devices, per_device(): from_column = lax.all_to_all(cut, 'tile', 0, 0, tiled=True)  12 us
    dot_general x16, matrix products, matmul_hi(): jnp.dot(left_op, right_op, precision=lax.Precision.HIGHEST, preferred_ele...  11 us
  transfers between devices with their start and end apart: 9, of which 9 were waited for; matrix products, arithmetic and copies ran while one was open for 7% of the time, Pallas kernels for 0%

profile of v8, /device:TPU:6, one launch (start us, length us, event | category | flops | bytes accessed | tf_op | source)
XLA Modules:
  0.0 264.8 jit_solution(13454039490150158173)
XLA Ops:
  2.8 3.6 %gather_fusion = bf16[64,4,4096]{2,1,0:T(4,128)(2,1)} fusion(bf16[24,4,4096]{2,1,0:T(4,128)(2,1)S(1)} %copy-done, s32[1024]{0:T(1024)S(1)} %pad_clamp_fusion.2), kind=kCustom, calls=%fused_computation | custom fusion | bytes 4194560 | tf_op jit(solution)/shard_map/gather | solution.py:103
  6.3 14.1 %all-to-all-start = ((bf16[64,4,4096]{2,1,0:T(4,128)(2,1)}), bf16[64,4,4096]{2,1,0:T(4,128)(2,1)S(1)}, u32[]{:S(2)}, u32[]{:S(2)}) async-start(bf16[64,4,4096]{2,1,0:T(4,128)(2,1)} %gather_fusion), calls=%async_computation | async-start | bytes 4194304 | tf_op jit(solution)/shard_map/all_to_all | solution.py:121
  27.8 1.9 gather_fusion.3
  38.0 31.3 %all-to-all-done = bf16[64,4,4096]{2,1,0:T(4,128)(2,1)S(1)} async-done(((bf16[64,4,4096]{2,1,0:T(4,128)(2,1)}), bf16[64,4,4096]{2,1,0:T(4,128)(2,1)S(1)}, u32[]{:S(2)}, u32[]{:S(2)}) %all-to-all-start) | async-done | bytes 2097184 | tf_op jit(solution)/shard_map/all_to_all | solution.py:121
  79.3 12.0 %all-to-all-start.1 = ((bf16[12,9,11,128]{3,2,1,0:T(8,128)(2,1)}), bf16[12,9,11,128]{3,2,1,0:T(8,128)(2,1)S(1)}, u32[]{:S(2)}, u32[]{:S(2)}) async-start(bf16[12,9,11,128]{3,2,1,0:T(8,128)(2,1)} %copy.57), calls=%async_computation.1 | async-start | bytes 884736 | tf_op jit(solution)/shard_map/all_to_all | solution.py:163
  91.7 20.2 %all-to-all-done.1 = bf16[12,9,11,128]{3,2,1,0:T(8,128)(2,1)S(1)} async-done(((bf16[12,9,11,128]{3,2,1,0:T(8,128)(2,1)}), bf16[12,9,11,128]{3,2,1,0:T(8,128)(2,1)S(1)}, u32[]{:S(2)}, u32[]{:S(2)}) %all-to-all-start.1) | async-done | bytes 304160 | tf_op jit(solution)/shard_map/all_to_all | solution.py:163
  112.1 1.6 fusion
  114.1 2.5 reshape.390
  116.6 8.1 %all-to-all-start.2 = ((bf16[64,140,128]{2,1,0:T(8,128)(2,1)}), bf16[64,140,128]{2,1,0:T(8,128)(2,1)S(1)}, u32[]{:S(2)}, u32[]{:S(2)}) async-start(bf16[64,140,128]{2,1,0:T(8,128)(2,1)} %reshape.390), calls=%async_computation.2 | async-start | bytes 4718592 | tf_op jit(solution)/shard_map/all_to_all | solution.py:184
  125.6 53.3 %all-to-all-done.2 = bf16[64,140,128]{2,1,0:T(8,128)(2,1)S(1)} async-done(((bf16[64,140,128]{2,1,0:T(8,128)(2,1)}), bf16[64,140,128]{2,1,0:T(8,128)(2,1)S(1)}, u32[]{:S(2)}, u32[]{:S(2)}) %all-to-all-start.2) | async-done | bytes 2293792 | tf_op jit(solution)/shard_map/all_to_all | solution.py:184
  180.2 4.7 %collective-permute-start = (f32[25,1408]{1,0:T(8,128)S(1)}, f32[25,1408]{1,0:T(8,128)S(1)}, u32[]{:S(2)}, u32[]{:S(2)}) collective-permute-start(f32[25,1408]{1,0:T(8,128)S(1)} %get-tuple-element.41), channel_id=1, source_target_pairs={{0,3},{1,4},{2,5},{3,6},{4,7},{5,8},{6,9},{7,10},{8,11},{9,0},{10,... | collective-permute-start | bytes 422408 | tf_op jit(solution)/shard_map/ppermute | solution.py:217
  184.9 6.0 %collective-permute-start.1 = (f32[25,1408]{1,0:T(8,128)S(1)}, f32[25,1408]{1,0:T(8,128)S(1)}, u32[]{:S(2)}, u32[]{:S(2)}) collective-permute-start(f32[25,1408]{1,0:T(8,128)S(1)} %get-tuple-element.41), channel_id=1, source_target_pairs={{0,6},{1,7},{2,8},{3,9},{4,10},{5,11},{6,0},{7,1},{8,2},{9,3},{10,... | collective-permute-start | bytes 422408 | tf_op jit(solution)/shard_map/ppermute | solution.py:217
  191.0 2.3 collective-permute-start.2
  193.2 4.8 %collective-permute-done = f32[25,1408]{1,0:T(8,128)S(1)} collective-permute-done((f32[25,1408]{1,0:T(8,128)S(1)}, f32[25,1408]{1,0:T(8,128)S(1)}, u32[]{:S(2)}, u32[]{:S(2)}) %collective-permute-start) | collective-permute-done | bytes 140832 | tf_op jit(solution)/shard_map/ppermute | solution.py:217
  198.0 13.1 %collective-permute-done.1 = f32[25,1408]{1,0:T(8,128)S(1)} collective-permute-done((f32[25,1408]{1,0:T(8,128)S(1)}, f32[25,1408]{1,0:T(8,128)S(1)}, u32[]{:S(2)}, u32[]{:S(2)}) %collective-permute-start.1) | collective-permute-done | bytes 140832 | tf_op jit(solution)/shard_map/ppermute | solution.py:217
  211.1 5.4 %collective-permute-done.2 = f32[25,1408]{1,0:T(8,128)S(1)} collective-permute-done((f32[25,1408]{1,0:T(8,128)S(1)}, f32[25,1408]{1,0:T(8,128)S(1)}, u32[]{:S(2)}, u32[]{:S(2)}) %collective-permute-start.2) | collective-permute-done | bytes 140832 | tf_op jit(solution)/shard_map/ppermute | solution.py:217
  217.0 1.9 collective-permute-start.3
  219.6 3.9 %collective-permute-start.4 = (f32[4,25,1408]{2,0,1:T(4,128)S(1)}, f32[4,25,1408]{2,0,1:T(4,128)S(1)}, u32[]{:S(2)}, u32[]{:S(2)}) collective-permute-start(f32[4,25,1408]{2,0,1:T(4,128)S(1)} %copy.63), channel_id=1, source_target_pairs={{0,1},{1,2},{2,3},{3,4},{4,5},{5,6},{6,7},{7,8},{8,9},{9,10},{10,1... | collective-permute-start | bytes 1689608 | tf_op jit(solution)/shard_map/ppermute | solution.py:217
  223.5 10.1 %collective-permute-done.3 = f32[4,25,1408]{2,0,1:T(4,128)S(1)} collective-permute-done((f32[4,25,1408]{2,0,1:T(4,128)S(1)}, f32[4,25,1408]{2,0,1:T(4,128)S(1)}, u32[]{:S(2)}, u32[]{:S(2)}) %collective-permute-start.3) | collective-permute-done | bytes 563232 | tf_op jit(solution)/shard_map/ppermute | solution.py:217
  234.7 2.8 %collective-permute-done.4 = f32[4,25,1408]{2,0,1:T(4,128)S(1)} collective-permute-done((f32[4,25,1408]{2,0,1:T(4,128)S(1)}, f32[4,25,1408]{2,0,1:T(4,128)S(1)}, u32[]{:S(2)}, u32[]{:S(2)}) %collective-permute-start.4) | collective-permute-done | bytes 563232 | tf_op jit(solution)/shard_map/ppermute | solution.py:217
  244.8 2.3 gather_fusion.4
  247.8 7.4 %all-to-all-start.3 = ((f32[64,1,512]{2,1,0:T(1,128)}), f32[64,1,512]{2,1,0:T(1,128)S(1)}, u32[]{:S(2)}, u32[]{:S(2)}) async-start(f32[64,1,512]{2,1,0:T(1,128)} %broadcast_in_dim.19), calls=%async_computation.3 | async-start | bytes 262144 | tf_op jit(solution)/shard_map/all_to_all | solution.py:206
  255.6 2.2 reshape.394
  257.8 6.3 %all-to-all-done.3 = f32[64,1,512]{2,1,0:T(1,128)S(1)} async-done(((f32[64,1,512]{2,1,0:T(1,128)}), f32[64,1,512]{2,1,0:T(1,128)S(1)}, u32[]{:S(2)}, u32[]{:S(2)}) %all-to-all-start.3) | async-done | bytes 131104 | tf_op jit(solution)/shard_map/all_to_all | solution.py:206
  (142 shorter events, 36.3 us)
Async XLA Ops:
  0.6 2.1 copy-start
  6.3 14.1 %copy-start.5 = (s32[768,2]{0,1:T(2,128)S(1)}, s32[768,2]{0,1:T(2,128)}, u32[]{:S(2)}) copy-start(s32[768,2]{0,1:T(2,128)} %param.7) | copy-start | bytes 18436
  6.3 20.1 %copy-start.1 = (s32[32,48]{1,0:T(8,128)S(1)}, s32[32,48]{1,0:T(8,128)}, u32[]{:S(2)}) copy-start(s32[32,48]{1,0:T(8,128)} %param.6) | copy-start | bytes 18436
  6.3 20.8 %copy-start.2 = (f32[2,128,128]{2,1,0:T(8,128)S(1)}, f32[2,128,128]{2,1,0:T(8,128)}, u32[]{:S(2)}) copy-start(f32[2,128,128]{2,1,0:T(8,128)} %param.8) | copy-start | bytes 393220
  6.3 63.0 %all-to-all-start = ((bf16[64,4,4096]{2,1,0:T(4,128)(2,1)}), bf16[64,4,4096]{2,1,0:T(4,128)(2,1)S(1)}, u32[]{:S(2)}, u32[]{:S(2)}) async-start(bf16[64,4,4096]{2,1,0:T(4,128)(2,1)} %gather_fusion), calls=%async_computation | async-start | bytes 4194304 | tf_op jit(solution)/shard_map/all_to_all | solution.py:121
  20.4 7.0 %copy-start.3 = (f32[1,128,128]{2,1,0:T(8,128)S(1)}, f32[1,128,128]{2,1,0:T(8,128)}, u32[]{:S(2)}) copy-start(f32[1,128,128]{2,1,0:T(8,128)} %param.9) | copy-start | bytes 196612
  70.6 1.4 copy-start.9
  70.7 1.4 copy-start.11
  70.7 2.0 copy-start.10
  71.2 1.9 copy-start.4
  72.6 2.6 copy-start.6
  72.6 2.6 copy-start.8
  73.1 2.8 %copy-start.7 = (f32[128,128]{0,1:T(8,128)S(1)}, f32[128,128]{0,1:T(8,128)}, u32[]{:S(2)}) copy-start(f32[128,128]{0,1:T(8,128)} %get-tuple-element.59) | copy-start | bytes 196612
  79.3 32.6 %all-to-all-start.1 = ((bf16[12,9,11,128]{3,2,1,0:T(8,128)(2,1)}), bf16[12,9,11,128]{3,2,1,0:T(8,128)(2,1)S(1)}, u32[]{:S(2)}, u32[]{:S(2)}) async-start(bf16[12,9,11,128]{3,2,1,0:T(8,128)(2,1)} %copy.57), calls=%async_computation.1 | async-start | bytes 884736 | tf_op jit(solution)/shard_map/all_to_all | solution.py:163
  116.6 62.3 %all-to-all-start.2 = ((bf16[64,140,128]{2,1,0:T(8,128)(2,1)}), bf16[64,140,128]{2,1,0:T(8,128)(2,1)S(1)}, u32[]{:S(2)}, u32[]{:S(2)}) async-start(bf16[64,140,128]{2,1,0:T(8,128)(2,1)} %reshape.390), calls=%async_computation.2 | async-start | bytes 4718592 | tf_op jit(solution)/shard_map/all_to_all | solution.py:184
  180.2 17.8 %collective-permute-start = (f32[25,1408]{1,0:T(8,128)S(1)}, f32[25,1408]{1,0:T(8,128)S(1)}, u32[]{:S(2)}, u32[]{:S(2)}) collective-permute-start(f32[25,1408]{1,0:T(8,128)S(1)} %get-tuple-element.41), channel_id=1, source_target_pairs={{0,3},{1,4},{2,5},{3,6},{4,7},{5,8},{6,9},{7,10},{8,11},{9,0},{10,... | collective-permute-start | bytes 422408 | tf_op jit(solution)/shard_map/ppermute | solution.py:217
  184.9 26.2 %collective-permute-start.1 = (f32[25,1408]{1,0:T(8,128)S(1)}, f32[25,1408]{1,0:T(8,128)S(1)}, u32[]{:S(2)}, u32[]{:S(2)}) collective-permute-start(f32[25,1408]{1,0:T(8,128)S(1)} %get-tuple-element.41), channel_id=1, source_target_pairs={{0,6},{1,7},{2,8},{3,9},{4,10},{5,11},{6,0},{7,1},{8,2},{9,3},{10,... | collective-permute-start | bytes 422408 | tf_op jit(solution)/shard_map/ppermute | solution.py:217
  191.0 25.6 %collective-permute-start.2 = (f32[25,1408]{1,0:T(8,128)S(1)}, f32[25,1408]{1,0:T(8,128)S(1)}, u32[]{:S(2)}, u32[]{:S(2)}) collective-permute-start(f32[25,1408]{1,0:T(8,128)S(1)} %get-tuple-element.41), channel_id=1, source_target_pairs={{0,9},{1,10},{2,11},{3,0},{4,1},{5,2},{6,3},{7,4},{8,5},{9,6},{10,... | collective-permute-start | bytes 422408 | tf_op jit(solution)/shard_map/ppermute | solution.py:217
  217.0 16.7 %collective-permute-start.3 = (f32[4,25,1408]{2,0,1:T(4,128)S(1)}, f32[4,25,1408]{2,0,1:T(4,128)S(1)}, u32[]{:S(2)}, u32[]{:S(2)}) collective-permute-start(f32[4,25,1408]{2,0,1:T(4,128)S(1)} %copy.63), channel_id=1, source_target_pairs={{0,11},{1,0},{2,1},{3,2},{4,3},{5,4},{6,5},{7,6},{8,7},{9,8},{10,9... | collective-permute-start | bytes 1689608 | tf_op jit(solution)/shard_map/ppermute | solution.py:217
  219.6 17.9 %collective-permute-start.4 = (f32[4,25,1408]{2,0,1:T(4,128)S(1)}, f32[4,25,1408]{2,0,1:T(4,128)S(1)}, u32[]{:S(2)}, u32[]{:S(2)}) collective-permute-start(f32[4,25,1408]{2,0,1:T(4,128)S(1)} %copy.63), channel_id=1, source_target_pairs={{0,1},{1,2},{2,3},{3,4},{4,5},{5,6},{6,7},{7,8},{8,9},{9,10},{10,1... | collective-permute-start | bytes 1689608 | tf_op jit(solution)/shard_map/ppermute | solution.py:217
  247.8 16.3 %all-to-all-start.3 = ((f32[64,1,512]{2,1,0:T(1,128)}), f32[64,1,512]{2,1,0:T(1,128)S(1)}, u32[]{:S(2)}, u32[]{:S(2)}) async-start(f32[64,1,512]{2,1,0:T(1,128)} %broadcast_in_dim.19), calls=%async_computation.3 | async-start | bytes 262144 | tf_op jit(solution)/shard_map/all_to_all | solution.py:206

commit v9 on v6

--- a/solution.py
+++ b/solution.py
@@ -198,17 +198,18 @@
     my_slice = jnp.einsum("qtk,qtx->kx", all_sel, from_owners, preferred_element_type=jnp.float32)
 
     probe_cut = jnp.pad(probe_row, (0, cut_len - piece_len))[None]
-    gathered = ring_gather(jnp.concatenate([my_slice, probe_cut], axis=0), layers)
-    slices = gathered[:, :tiles_dev]
-    tile_total = slices.transpose(1, 0, 2).reshape(tiles_dev, layers * cut_len)[:, :tile_px]
-    probe_piece = jnp.sum(gathered[:, tiles_dev, :piece_len], axis=0)
+    by_offset = ring_pieces(jnp.concatenate([my_slice, probe_cut], axis=0), layers)
+    flat = jnp.concatenate(by_offset, axis=1)
+    start = (layers - me_tile) % layers * cut_len
+    ordered = lax.dynamic_slice_in_dim(jnp.concatenate([flat, flat], axis=1), start, layers * cut_len, 1)
+    tile_total = ordered[:tiles_dev, :tile_px]
+    probe_piece = jnp.sum(ordered[tiles_dev].reshape(layers, cut_len)[:, :piece_len], axis=0)
     spread = jnp.broadcast_to(probe_piece[None], (owners, piece_len))
     probe_total = lax.all_to_all(spread, "pos", 0, 0, tiled=True).reshape(probe_part.shape)
     return (tile_total.reshape(tiles_dev, n_comps, tile_edge * tile_edge), probe_total)
 
 
-def ring_gather(values, size):
-    me = lax.axis_index("tile")
+def ring_pieces(values, size):
     to_right = [(i, (i + 1) % size) for i in range(size)]
     to_left = [(i, (i - 1) % size) for i in range(size)]
     back = [values]
@@ -221,9 +222,7 @@
         if step < size - size // 2:
             going_left = lax.ppermute(going_left, "tile", to_left)
             ahead.append(going_left)
-    by_offset = [back[0]] + ahead + [back[size - d] for d in range(len(ahead) + 1, size)]
-    order = (jnp.arange(size, dtype=jnp.int32) - me) % size
-    return jnp.stack(by_offset)[order]
+    return [back[0]] + ahead + [back[size - d] for d in range(len(ahead) + 1, size)]
 
 
 def reduce_probe(probe_part, owners, layers):

time: 266 us -> 274 us (1.030)
  local copies, waits for them, and re-layouts: 31.3 us -> 39.2 us
    unnamed x41 -> x51, local copies, waits for them, and re-layouts: 8.67 us -> 16.2 us
where the time goes in v9:
time: 274 us; the launch traced here: 271 us
  waiting for transfers between devices  128 us (47%)
  starting transfers between devices  78.4 us (29%)
  local copies, waits for them, and re-layouts  39.2 us (14%)
  matrix products  14.3 us (5%)
  between operations  6.75 us (2%)
  other arithmetic  4.25 us (2%)
    all_to_all x1, waiting for transfers between devices, per_device(): lax.all_to_all(outgoing, 'pos', 0, 0, tiled=True).reshape(owners, slot_len)  53.3 us
    all_to_all x1, waiting for transfers between devices, per_device(): lax.all_to_all(chosen, 'pos', split_axis=0, concat_axis=0, tiled=True)  31.3 us
    ppermute x5, starting transfers between devices, ring_pieces(): going_left = lax.ppermute(going_left, 'tile', to_left)  25.2 us
    all_to_all x1, waiting for transfers between devices, per_device(): from_column = lax.all_to_all(cut, 'tile', 0, 0, tiled=True)  20.2 us
    unnamed x51, local copies, waits for them, and re-layouts  16.2 us
    all_to_all x1, starting transfers between devices, per_device(): lax.all_to_all(chosen, 'pos', split_axis=0, concat_axis=0, tiled=True)  14.1 us
    ppermute x6, waiting for transfers between devices, ring_pieces(): going_right = lax.ppermute(going_right, 'tile', to_right)  14 us
    ppermute x6, starting transfers between devices, ring_pieces(): going_right = lax.ppermute(going_right, 'tile', to_right)  12.4 us
  transfers between devices with their start and end apart: 15, of which 14 were waited for; matrix products, arithmetic and copies ran while one was open for 8% of the time, Pallas kernels for 0%

profile of v9, /device:TPU:6, one launch (start us, length us, event | category | flops | bytes accessed | tf_op | source)
XLA Modules:
  0.0 270.9 jit_solution(8819994502207734750)
XLA Ops:
  2.8 3.6 %gather_fusion = bf16[64,4,4096]{2,1,0:T(4,128)(2,1)} fusion(bf16[24,4,4096]{2,1,0:T(4,128)(2,1)S(1)} %copy-done, s32[1024]{0:T(1024)S(1)} %pad_clamp_fusion.1), kind=kCustom, calls=%fused_computation | custom fusion | bytes 4194560 | tf_op jit(solution)/shard_map/gather | solution.py:103
  6.4 14.1 %all-to-all-start = ((bf16[64,4,4096]{2,1,0:T(4,128)(2,1)}), bf16[64,4,4096]{2,1,0:T(4,128)(2,1)S(1)}, u32[]{:S(2)}, u32[]{:S(2)}) async-start(bf16[64,4,4096]{2,1,0:T(4,128)(2,1)} %gather_fusion), calls=%async_computation | async-start | bytes 4194304 | tf_op jit(solution)/shard_map/all_to_all | solution.py:121
  38.1 31.3 %all-to-all-done = bf16[64,4,4096]{2,1,0:T(4,128)(2,1)S(1)} async-done(((bf16[64,4,4096]{2,1,0:T(4,128)(2,1)}), bf16[64,4,4096]{2,1,0:T(4,128)(2,1)S(1)}, u32[]{:S(2)}, u32[]{:S(2)}) %all-to-all-start) | async-done | bytes 2097184 | tf_op jit(solution)/shard_map/all_to_all | solution.py:121
  79.3 12.0 %all-to-all-start.1 = ((bf16[12,9,11,128]{3,2,1,0:T(8,128)(2,1)}), bf16[12,9,11,128]{3,2,1,0:T(8,128)(2,1)S(1)}, u32[]{:S(2)}, u32[]{:S(2)}) async-start(bf16[12,9,11,128]{3,2,1,0:T(8,128)(2,1)} %copy.55), calls=%async_computation.1 | async-start | bytes 884736 | tf_op jit(solution)/shard_map/all_to_all | solution.py:163
  91.7 20.2 %all-to-all-done.1 = bf16[12,9,11,128]{3,2,1,0:T(8,128)(2,1)S(1)} async-done(((bf16[12,9,11,128]{3,2,1,0:T(8,128)(2,1)}), bf16[12,9,11,128]{3,2,1,0:T(8,128)(2,1)S(1)}, u32[]{:S(2)}, u32[]{:S(2)}) %all-to-all-start.1) | async-done | bytes 304160 | tf_op jit(solution)/shard_map/all_to_all | solution.py:163
  114.1 2.6 reshape.353
  116.7 8.1 %all-to-all-start.2 = ((bf16[64,140,128]{2,1,0:T(8,128)(2,1)}), bf16[64,140,128]{2,1,0:T(8,128)(2,1)S(1)}, u32[]{:S(2)}, u32[]{:S(2)}) async-start(bf16[64,140,128]{2,1,0:T(8,128)(2,1)} %reshape.353), calls=%async_computation.2 | async-start | bytes 4718592 | tf_op jit(solution)/shard_map/all_to_all | solution.py:184
  125.7 53.3 %all-to-all-done.2 = bf16[64,140,128]{2,1,0:T(8,128)(2,1)S(1)} async-done(((bf16[64,140,128]{2,1,0:T(8,128)(2,1)}), bf16[64,140,128]{2,1,0:T(8,128)(2,1)S(1)}, u32[]{:S(2)}, u32[]{:S(2)}) %all-to-all-start.2) | async-done | bytes 2293792 | tf_op jit(solution)/shard_map/all_to_all | solution.py:184
  181.0 4.0 %collective-permute-start = (f32[25,1408]{1,0:T(8,128)S(1)}, f32[25,1408]{1,0:T(8,128)S(1)}, u32[]{:S(2)}, u32[]{:S(2)}) collective-permute-start(f32[25,1408]{1,0:T(8,128)S(1)} %get-tuple-element.32), channel_id=1, source_target_pairs={{0,11},{1,0},{2,1},{3,2},{4,3},{5,4},{6,5},{7,6},{8,7},{9,8},{10,9... | collective-permute-start | bytes 422408 | tf_op jit(solution)/shard_map/ppermute | solution.py:223
  185.0 2.8 %collective-permute-start.5 = (f32[25,1408]{1,0:T(8,128)S(1)}, f32[25,1408]{1,0:T(8,128)S(1)}, u32[]{:S(2)}, u32[]{:S(2)}) collective-permute-start(f32[25,1408]{1,0:T(8,128)S(1)} %get-tuple-element.32), channel_id=1, source_target_pairs={{0,1},{1,2},{2,3},{3,4},{4,5},{5,6},{6,7},{7,8},{8,9},{9,10},{10,1... | collective-permute-start | bytes 422408 | tf_op jit(solution)/shard_map/ppermute | solution.py:220
  189.5 4.5 %collective-permute-start.1 = (f32[25,1408]{1,0:T(8,128)S(1)}, f32[25,1408]{1,0:T(8,128)S(1)}, u32[]{:S(2)}, u32[]{:S(2)}) collective-permute-start(f32[25,1408]{1,0:T(8,128)S(1)} %collective-permute-done), channel_id=1, source_target_pairs={{0,11},{1,0},{2,1},{3,2},{4,3},{5,4},{6,5},{7,6},{8,7},{9,8},{10,9... | collective-permute-start | bytes 422408 | tf_op jit(solution)/shard_map/ppermute | solution.py:223
  194.3 1.9 collective-permute-start.6
  198.6 5.6 %collective-permute-start.2 = (f32[25,1408]{1,0:T(8,128)S(1)}, f32[25,1408]{1,0:T(8,128)S(1)}, u32[]{:S(2)}, u32[]{:S(2)}) collective-permute-start(f32[25,1408]{1,0:T(8,128)S(1)} %collective-permute-done.1), channel_id=1, source_target_pairs={{0,11},{1,0},{2,1},{3,2},{4,3},{5,4},{6,5},{7,6},{8,7},{9,8},{10,9... | collective-permute-start | bytes 422408 | tf_op jit(solution)/shard_map/ppermute | solution.py:223
  204.7 1.9 collective-permute-start.7
  208.3 5.6 %collective-permute-start.3 = (f32[25,1408]{1,0:T(8,128)S(1)}, f32[25,1408]{1,0:T(8,128)S(1)}, u32[]{:S(2)}, u32[]{:S(2)}) collective-permute-start(f32[25,1408]{1,0:T(8,128)S(1)} %collective-permute-done.2), channel_id=1, source_target_pairs={{0,11},{1,0},{2,1},{3,2},{4,3},{5,4},{6,5},{7,6},{8,7},{9,8},{10,9... | collective-permute-start | bytes 422408 | tf_op jit(solution)/shard_map/ppermute | solution.py:223
  214.4 1.9 collective-permute-start.8
  217.1 5.6 %collective-permute-start.4 = (f32[25,1408]{1,0:T(8,128)S(1)}, f32[25,1408]{1,0:T(8,128)S(1)}, u32[]{:S(2)}, u32[]{:S(2)}) collective-permute-start(f32[25,1408]{1,0:T(8,128)S(1)} %collective-permute-done.3), channel_id=1, source_target_pairs={{0,11},{1,0},{2,1},{3,2},{4,3},{5,4},{6,5},{7,6},{8,7},{9,8},{10,9... | collective-permute-start | bytes 422408 | tf_op jit(solution)/shard_map/ppermute | solution.py:223
  223.2 1.9 collective-permute-start.9
  225.8 6.0 %collective-permute-done.9 = f32[25,1408]{1,0:T(8,128)S(1)} collective-permute-done((f32[25,1408]{1,0:T(8,128)S(1)}, f32[25,1408]{1,0:T(8,128)S(1)}, u32[]{:S(2)}, u32[]{:S(2)}) %collective-permute-start.9) | collective-permute-done | bytes 140832 | tf_op jit(solution)/shard_map/ppermute | solution.py:220
  231.8 1.9 collective-permute-start.10
  234.4 6.0 %collective-permute-done.10 = f32[25,1408]{1,0:T(8,128)S(1)} collective-permute-done((f32[25,1408]{1,0:T(8,128)S(1)}, f32[25,1408]{1,0:T(8,128)S(1)}, u32[]{:S(2)}, u32[]{:S(2)}) %collective-permute-start.10) | collective-permute-done | bytes 140832 | tf_op jit(solution)/shard_map/ppermute | solution.py:220
  254.8 6.6 %all-to-all-start.3 = ((f32[64,1,512]{2,1,0:T(1,128)}), f32[64,1,512]{2,1,0:T(1,128)S(1)}, u32[]{:S(2)}, u32[]{:S(2)}) async-start(f32[64,1,512]{2,1,0:T(1,128)} %broadcast_in_dim.19), calls=%async_computation.3 | async-start | bytes 262144 | tf_op jit(solution)/shard_map/all_to_all | solution.py:208
  262.9 2.2 reshape.356
  265.1 5.1 %all-to-all-done.3 = f32[64,1,512]{2,1,0:T(1,128)S(1)} async-done(((f32[64,1,512]{2,1,0:T(1,128)}), f32[64,1,512]{2,1,0:T(1,128)S(1)}, u32[]{:S(2)}, u32[]{:S(2)}) %all-to-all-start.3) | async-done | bytes 131104 | tf_op jit(solution)/shard_map/all_to_all | solution.py:208
  (158 shorter events, 55.6 us)
Async XLA Ops:
  1.5 18.9 %copy-start.5 = (s32[768,2]{0,1:T(2,128)S(1)}, s32[768,2]{0,1:T(2,128)}, u32[]{:S(2)}) copy-start(s32[768,2]{0,1:T(2,128)} %param.7) | copy-start | bytes 18436
  2.5 24.0 %copy-start.1 = (s32[32,48]{1,0:T(8,128)S(1)}, s32[32,48]{1,0:T(8,128)}, u32[]{:S(2)}) copy-start(s32[32,48]{1,0:T(8,128)} %param.6) | copy-start | bytes 18436
  2.8 24.4 %copy-start.2 = (f32[2,128,128]{2,1,0:T(8,128)S(1)}, f32[2,128,128]{2,1,0:T(8,128)}, u32[]{:S(2)}) copy-start(f32[2,128,128]{2,1,0:T(8,128)} %param.8) | copy-start | bytes 393220
  6.4 21.0 %copy-start.3 = (f32[1,128,128]{2,1,0:T(8,128)S(1)}, f32[1,128,128]{2,1,0:T(8,128)}, u32[]{:S(2)}) copy-start(f32[1,128,128]{2,1,0:T(8,128)} %param.9) | copy-start | bytes 196612
  6.4 63.0 %all-to-all-start = ((bf16[64,4,4096]{2,1,0:T(4,128)(2,1)}), bf16[64,4,4096]{2,1,0:T(4,128)(2,1)S(1)}, u32[]{:S(2)}, u32[]{:S(2)}) async-start(bf16[64,4,4096]{2,1,0:T(4,128)(2,1)} %gather_fusion), calls=%async_computation | async-start | bytes 4194304 | tf_op jit(solution)/shard_map/all_to_all | solution.py:121
  70.2 2.5 copy-start.10
  70.2 2.9 %copy-start.4 = (f32[128,128]{1,0:T(8,128)S(1)}, f32[128,128]{1,0:T(8,128)}, u32[]{:S(2)}) copy-start(f32[128,128]{1,0:T(8,128)} %get-tuple-element.62) | copy-start | bytes 196612
  70.7 4.5 %copy-start.6 = (f32[128,128]{0,1:T(8,128)S(1)}, f32[128,128]{0,1:T(8,128)}, u32[]{:S(2)}) copy-start(f32[128,128]{0,1:T(8,128)} %convolution_subtract_fusion.1) | copy-start | bytes 196612
  70.7 4.5 %copy-start.8 = (f32[128,128]{0,1:T(8,128)S(1)}, f32[128,128]{0,1:T(8,128)}, u32[]{:S(2)}) copy-start(f32[128,128]{0,1:T(8,128)} %get-tuple-element.52) | copy-start | bytes 196612
  70.7 5.1 %copy-start.7 = (f32[128,128]{0,1:T(8,128)S(1)}, f32[128,128]{0,1:T(8,128)}, u32[]{:S(2)}) copy-start(f32[128,128]{0,1:T(8,128)} %get-tuple-element.51) | copy-start | bytes 196612
  79.3 32.6 %all-to-all-start.1 = ((bf16[12,9,11,128]{3,2,1,0:T(8,128)(2,1)}), bf16[12,9,11,128]{3,2,1,0:T(8,128)(2,1)S(1)}, u32[]{:S(2)}, u32[]{:S(2)}) async-start(bf16[12,9,11,128]{3,2,1,0:T(8,128)(2,1)} %copy.55), calls=%async_computation.1 | async-start | bytes 884736 | tf_op jit(solution)/shard_map/all_to_all | solution.py:163
  116.7 62.3 %all-to-all-start.2 = ((bf16[64,140,128]{2,1,0:T(8,128)(2,1)}), bf16[64,140,128]{2,1,0:T(8,128)(2,1)S(1)}, u32[]{:S(2)}, u32[]{:S(2)}) async-start(bf16[64,140,128]{2,1,0:T(8,128)(2,1)} %reshape.353), calls=%async_computation.2 | async-start | bytes 4718592 | tf_op jit(solution)/shard_map/all_to_all | solution.py:184
  181.0 8.5 %collective-permute-start = (f32[25,1408]{1,0:T(8,128)S(1)}, f32[25,1408]{1,0:T(8,128)S(1)}, u32[]{:S(2)}, u32[]{:S(2)}) collective-permute-start(f32[25,1408]{1,0:T(8,128)S(1)} %get-tuple-element.32), channel_id=1, source_target_pairs={{0,11},{1,0},{2,1},{3,2},{4,3},{5,4},{6,5},{7,6},{8,7},{9,8},{10,9... | collective-permute-start | bytes 422408 | tf_op jit(solution)/shard_map/ppermute | solution.py:223
  185.0 9.3 %collective-permute-start.5 = (f32[25,1408]{1,0:T(8,128)S(1)}, f32[25,1408]{1,0:T(8,128)S(1)}, u32[]{:S(2)}, u32[]{:S(2)}) collective-permute-start(f32[25,1408]{1,0:T(8,128)S(1)} %get-tuple-element.32), channel_id=1, source_target_pairs={{0,1},{1,2},{2,3},{3,4},{4,5},{5,6},{6,7},{7,8},{8,9},{9,10},{10,1... | collective-permute-start | bytes 422408 | tf_op jit(solution)/shard_map/ppermute | solution.py:220
  189.5 9.1 %collective-permute-start.1 = (f32[25,1408]{1,0:T(8,128)S(1)}, f32[25,1408]{1,0:T(8,128)S(1)}, u32[]{:S(2)}, u32[]{:S(2)}) collective-permute-start(f32[25,1408]{1,0:T(8,128)S(1)} %collective-permute-done), channel_id=1, source_target_pairs={{0,11},{1,0},{2,1},{3,2},{4,3},{5,4},{6,5},{7,6},{8,7},{9,8},{10,9... | collective-permute-start | bytes 422408 | tf_op jit(solution)/shard_map/ppermute | solution.py:223
  194.3 10.5 %collective-permute-start.6 = (f32[25,1408]{1,0:T(8,128)S(1)}, f32[25,1408]{1,0:T(8,128)S(1)}, u32[]{:S(2)}, u32[]{:S(2)}) collective-permute-start(f32[25,1408]{1,0:T(8,128)S(1)} %collective-permute-done.5), channel_id=1, source_target_pairs={{0,1},{1,2},{2,3},{3,4},{4,5},{5,6},{6,7},{7,8},{8,9},{9,10},{10,1... | collective-permute-start | bytes 422408 | tf_op jit(solution)/shard_map/ppermute | solution.py:220
  198.6 9.7 %collective-permute-start.2 = (f32[25,1408]{1,0:T(8,128)S(1)}, f32[25,1408]{1,0:T(8,128)S(1)}, u32[]{:S(2)}, u32[]{:S(2)}) collective-permute-start(f32[25,1408]{1,0:T(8,128)S(1)} %collective-permute-done.1), channel_id=1, source_target_pairs={{0,11},{1,0},{2,1},{3,2},{4,3},{5,4},{6,5},{7,6},{8,7},{9,8},{10,9... | collective-permute-start | bytes 422408 | tf_op jit(solution)/shard_map/ppermute | solution.py:223
  204.7 9.7 %collective-permute-start.7 = (f32[25,1408]{1,0:T(8,128)S(1)}, f32[25,1408]{1,0:T(8,128)S(1)}, u32[]{:S(2)}, u32[]{:S(2)}) collective-permute-start(f32[25,1408]{1,0:T(8,128)S(1)} %collective-permute-done.6), channel_id=1, source_target_pairs={{0,1},{1,2},{2,3},{3,4},{4,5},{5,6},{6,7},{7,8},{8,9},{9,10},{10,1... | collective-permute-start | bytes 422408 | tf_op jit(solution)/shard_map/ppermute | solution.py:220
  208.3 8.8 %collective-permute-start.3 = (f32[25,1408]{1,0:T(8,128)S(1)}, f32[25,1408]{1,0:T(8,128)S(1)}, u32[]{:S(2)}, u32[]{:S(2)}) collective-permute-start(f32[25,1408]{1,0:T(8,128)S(1)} %collective-permute-done.2), channel_id=1, source_target_pairs={{0,11},{1,0},{2,1},{3,2},{4,3},{5,4},{6,5},{7,6},{8,7},{9,8},{10,9... | collective-permute-start | bytes 422408 | tf_op jit(solution)/shard_map/ppermute | solution.py:223
  214.4 8.8 %collective-permute-start.8 = (f32[25,1408]{1,0:T(8,128)S(1)}, f32[25,1408]{1,0:T(8,128)S(1)}, u32[]{:S(2)}, u32[]{:S(2)}) collective-permute-start(f32[25,1408]{1,0:T(8,128)S(1)} %collective-permute-done.7), channel_id=1, source_target_pairs={{0,1},{1,2},{2,3},{3,4},{4,5},{5,6},{6,7},{7,8},{8,9},{9,10},{10,1... | collective-permute-start | bytes 422408 | tf_op jit(solution)/shard_map/ppermute | solution.py:220
  217.1 16.7 %collective-permute-start.4 = (f32[25,1408]{1,0:T(8,128)S(1)}, f32[25,1408]{1,0:T(8,128)S(1)}, u32[]{:S(2)}, u32[]{:S(2)}) collective-permute-start(f32[25,1408]{1,0:T(8,128)S(1)} %collective-permute-done.3), channel_id=1, source_target_pairs={{0,11},{1,0},{2,1},{3,2},{4,3},{5,4},{6,5},{7,6},{8,7},{9,8},{10,9... | collective-permute-start | bytes 422408 | tf_op jit(solution)/shard_map/ppermute | solution.py:223
  223.2 8.6 %collective-permute-start.9 = (f32[25,1408]{1,0:T(8,128)S(1)}, f32[25,1408]{1,0:T(8,128)S(1)}, u32[]{:S(2)}, u32[]{:S(2)}) collective-permute-start(f32[25,1408]{1,0:T(8,128)S(1)} %collective-permute-done.8), channel_id=1, source_target_pairs={{0,1},{1,2},{2,3},{3,4},{4,5},{5,6},{6,7},{7,8},{8,9},{9,10},{10,1... | collective-permute-start | bytes 422408 | tf_op jit(solution)/shard_map/ppermute | solution.py:220
  231.8 8.6 %collective-permute-start.10 = (f32[25,1408]{1,0:T(8,128)S(1)}, f32[25,1408]{1,0:T(8,128)S(1)}, u32[]{:S(2)}, u32[]{:S(2)}) collective-permute-start(f32[25,1408]{1,0:T(8,128)S(1)} %collective-permute-done.9), channel_id=1, source_target_pairs={{0,1},{1,2},{2,3},{3,4},{4,5},{5,6},{6,7},{7,8},{8,9},{9,10},{10,1... | collective-permute-start | bytes 422408 | tf_op jit(solution)/shard_map/ppermute | solution.py:220
  254.8 15.4 %all-to-all-start.3 = ((f32[64,1,512]{2,1,0:T(1,128)}), f32[64,1,512]{2,1,0:T(1,128)S(1)}, u32[]{:S(2)}, u32[]{:S(2)}) async-start(f32[64,1,512]{2,1,0:T(1,128)} %broadcast_in_dim.19), calls=%async_computation.3 | async-start | bytes 262144 | tf_op jit(solution)/shard_map/all_to_all | solution.py:208
  (3 other events, 5.9 us)

commit v10 on v6

--- a/solution.py
+++ b/solution.py
@@ -159,7 +159,7 @@
     cut_len = -(-cut_len // 128) * 128
     pad_px = cut_len * layers - tile_px
     cut = jnp.pad(tiles_cut, ((0, 0), (0, pad_px))).reshape(n_foot, layers, cut_len)
-    cut = cut.transpose(1, 0, 2).reshape(layers, n_foot, cut_len // 128, 128)
+    cut = cut.transpose(1, 0, 2).reshape(layers, n_foot * cut_len // 128, 128)
     from_column = lax.all_to_all(cut, "tile", 0, 0, tiled=True)
     from_column = from_column.reshape(layers, n_foot, cut_len)
 

time: 266 us -> 263 us (0.989)
  waiting for transfers between devices: 129 us -> 125 us
    all_to_all x1, waiting for transfers between devices: 20.2 us -> 16.8 us  [per_device(): from_column = lax.all_to_all(cut, 'tile', 0, 0, tiled=True)]
where the time goes in v10:
time: 263 us; the launch traced here: 260 us
  waiting for transfers between devices  125 us (48%)
  starting transfers between devices  78.2 us (30%)
  local copies, waits for them, and re-layouts  31.6 us (12%)
  matrix products  14.3 us (5%)
  between operations  6.73 us (3%)
  other arithmetic  3.59 us (1%)
    all_to_all x1, waiting for transfers between devices, per_device(): lax.all_to_all(outgoing, 'pos', 0, 0, tiled=True).reshape(owners, slot_len)  53.2 us
    all_to_all x1, waiting for transfers between devices, per_device(): lax.all_to_all(chosen, 'pos', split_axis=0, concat_axis=0, tiled=True)  31.3 us
    ppermute x5, starting transfers between devices, ring_gather(): going_left = lax.ppermute(going_left, 'tile', to_left)  25.5 us
    all_to_all x1, waiting for transfers between devices, per_device(): from_column = lax.all_to_all(cut, 'tile', 0, 0, tiled=True)  16.8 us
    all_to_all x1, starting transfers between devices, per_device(): lax.all_to_all(chosen, 'pos', split_axis=0, concat_axis=0, tiled=True)  14.1 us
    ppermute x6, waiting for transfers between devices, ring_gather(): going_right = lax.ppermute(going_right, 'tile', to_right)  14 us
    all_to_all x1, starting transfers between devices, per_device(): from_column = lax.all_to_all(cut, 'tile', 0, 0, tiled=True)  12 us
    ppermute x6, starting transfers between devices, ring_gather(): going_right = lax.ppermute(going_right, 'tile', to_right)  12 us
  transfers between devices with their start and end apart: 15, of which 14 were waited for; matrix products, arithmetic and copies ran while one was open for 8% of the time, Pallas kernels for 0%

profile of v10, /device:TPU:6, one launch (start us, length us, event | category | flops | bytes accessed | tf_op | source)
XLA Modules:
  0.0 259.7 jit_solution(7713347966815198961)
XLA Ops:
  2.8 3.6 %gather_fusion = bf16[64,4,4096]{2,1,0:T(4,128)(2,1)} fusion(bf16[24,4,4096]{2,1,0:T(4,128)(2,1)S(1)} %copy-done, s32[1024]{0:T(1024)S(1)} %pad_clamp_fusion.2), kind=kCustom, calls=%fused_computation | custom fusion | bytes 4194560 | tf_op jit(solution)/shard_map/gather | solution.py:103
  6.3 14.1 %all-to-all-start = ((bf16[64,4,4096]{2,1,0:T(4,128)(2,1)}), bf16[64,4,4096]{2,1,0:T(4,128)(2,1)S(1)}, u32[]{:S(2)}, u32[]{:S(2)}) async-start(bf16[64,4,4096]{2,1,0:T(4,128)(2,1)} %gather_fusion), calls=%async_computation | async-start | bytes 4194304 | tf_op jit(solution)/shard_map/all_to_all | solution.py:121
  38.0 31.3 %all-to-all-done = bf16[64,4,4096]{2,1,0:T(4,128)(2,1)S(1)} async-done(((bf16[64,4,4096]{2,1,0:T(4,128)(2,1)}), bf16[64,4,4096]{2,1,0:T(4,128)(2,1)S(1)}, u32[]{:S(2)}, u32[]{:S(2)}) %all-to-all-start) | async-done | bytes 2097184 | tf_op jit(solution)/shard_map/all_to_all | solution.py:121
  79.4 12.0 %all-to-all-start.1 = ((bf16[12,99,128]{2,1,0:T(8,128)(2,1)}), bf16[12,99,128]{2,1,0:T(8,128)(2,1)S(1)}, u32[]{:S(2)}, u32[]{:S(2)}) async-start(bf16[12,99,128]{2,1,0:T(8,128)(2,1)} %reshape.386), calls=%async_computation.1 | async-start | bytes 638976 | tf_op jit(solution)/shard_map/all_to_all | solution.py:163
  91.9 16.8 %all-to-all-done.1 = bf16[12,99,128]{2,1,0:T(8,128)(2,1)S(1)} async-done(((bf16[12,99,128]{2,1,0:T(8,128)(2,1)}), bf16[12,99,128]{2,1,0:T(8,128)(2,1)S(1)}, u32[]{:S(2)}, u32[]{:S(2)}) %all-to-all-start.1) | async-done | bytes 304160 | tf_op jit(solution)/shard_map/all_to_all | solution.py:163
  111.0 2.6 reshape.390
  113.5 8.1 %all-to-all-start.2 = ((bf16[64,140,128]{2,1,0:T(8,128)(2,1)}), bf16[64,140,128]{2,1,0:T(8,128)(2,1)S(1)}, u32[]{:S(2)}, u32[]{:S(2)}) async-start(bf16[64,140,128]{2,1,0:T(8,128)(2,1)} %reshape.390), calls=%async_computation.2 | async-start | bytes 4718592 | tf_op jit(solution)/shard_map/all_to_all | solution.py:184
  122.6 53.2 %all-to-all-done.2 = bf16[64,140,128]{2,1,0:T(8,128)(2,1)S(1)} async-done(((bf16[64,140,128]{2,1,0:T(8,128)(2,1)}), bf16[64,140,128]{2,1,0:T(8,128)(2,1)S(1)}, u32[]{:S(2)}, u32[]{:S(2)}) %all-to-all-start.2) | async-done | bytes 2293792 | tf_op jit(solution)/shard_map/all_to_all | solution.py:184
  177.2 3.8 %collective-permute-start = (f32[25,1408]{1,0:T(8,128)S(1)}, f32[25,1408]{1,0:T(8,128)S(1)}, u32[]{:S(2)}, u32[]{:S(2)}) collective-permute-start(f32[25,1408]{1,0:T(8,128)S(1)} %pad_maximum_fusion.7), channel_id=1, source_target_pairs={{0,11},{1,0},{2,1},{3,2},{4,3},{5,4},{6,5},{7,6},{8,7},{9,8},{10,9... | collective-permute-start | bytes 422408 | tf_op jit(solution)/shard_map/ppermute | solution.py:222
  181.0 2.4 collective-permute-start.5
  185.1 4.9 %collective-permute-start.1 = (f32[25,1408]{1,0:T(8,128)S(1)}, f32[25,1408]{1,0:T(8,128)S(1)}, u32[]{:S(2)}, u32[]{:S(2)}) collective-permute-start(f32[25,1408]{1,0:T(8,128)S(1)} %collective-permute-done), channel_id=1, source_target_pairs={{0,11},{1,0},{2,1},{3,2},{4,3},{5,4},{6,5},{7,6},{8,7},{9,8},{10,9... | collective-permute-start | bytes 422408 | tf_op jit(solution)/shard_map/ppermute | solution.py:222
  190.3 1.9 collective-permute-start.6
  194.6 5.6 %collective-permute-start.2 = (f32[25,1408]{1,0:T(8,128)S(1)}, f32[25,1408]{1,0:T(8,128)S(1)}, u32[]{:S(2)}, u32[]{:S(2)}) collective-permute-start(f32[25,1408]{1,0:T(8,128)S(1)} %collective-permute-done.1), channel_id=1, source_target_pairs={{0,11},{1,0},{2,1},{3,2},{4,3},{5,4},{6,5},{7,6},{8,7},{9,8},{10,9... | collective-permute-start | bytes 422408 | tf_op jit(solution)/shard_map/ppermute | solution.py:222
  200.8 1.9 collective-permute-start.7
  204.3 5.6 %collective-permute-start.3 = (f32[25,1408]{1,0:T(8,128)S(1)}, f32[25,1408]{1,0:T(8,128)S(1)}, u32[]{:S(2)}, u32[]{:S(2)}) collective-permute-start(f32[25,1408]{1,0:T(8,128)S(1)} %collective-permute-done.2), channel_id=1, source_target_pairs={{0,11},{1,0},{2,1},{3,2},{4,3},{5,4},{6,5},{7,6},{8,7},{9,8},{10,9... | collective-permute-start | bytes 422408 | tf_op jit(solution)/shard_map/ppermute | solution.py:222
  210.4 1.9 collective-permute-start.8
  213.1 5.6 %collective-permute-start.4 = (f32[25,1408]{1,0:T(8,128)S(1)}, f32[25,1408]{1,0:T(8,128)S(1)}, u32[]{:S(2)}, u32[]{:S(2)}) collective-permute-start(f32[25,1408]{1,0:T(8,128)S(1)} %collective-permute-done.3), channel_id=1, source_target_pairs={{0,11},{1,0},{2,1},{3,2},{4,3},{5,4},{6,5},{7,6},{8,7},{9,8},{10,9... | collective-permute-start | bytes 422408 | tf_op jit(solution)/shard_map/ppermute | solution.py:222
  219.3 1.9 collective-permute-start.9
  221.9 6.0 %collective-permute-done.9 = f32[25,1408]{1,0:T(8,128)S(1)} collective-permute-done((f32[25,1408]{1,0:T(8,128)S(1)}, f32[25,1408]{1,0:T(8,128)S(1)}, u32[]{:S(2)}, u32[]{:S(2)}) %collective-permute-start.9) | collective-permute-done | bytes 140832 | tf_op jit(solution)/shard_map/ppermute | solution.py:219
  230.5 6.0 %collective-permute-done.10 = f32[25,1408]{1,0:T(8,128)S(1)} collective-permute-done((f32[25,1408]{1,0:T(8,128)S(1)}, f32[25,1408]{1,0:T(8,128)S(1)}, u32[]{:S(2)}, u32[]{:S(2)}) %collective-permute-start.10) | collective-permute-done | bytes 140832 | tf_op jit(solution)/shard_map/ppermute | solution.py:219
  240.6 2.3 gather_fusion.4
  243.6 6.6 %all-to-all-start.3 = ((f32[64,1,512]{2,1,0:T(1,128)}), f32[64,1,512]{2,1,0:T(1,128)S(1)}, u32[]{:S(2)}, u32[]{:S(2)}) async-start(f32[64,1,512]{2,1,0:T(1,128)} %broadcast_in_dim.19), calls=%async_computation.3 | async-start | bytes 262144 | tf_op jit(solution)/shard_map/all_to_all | solution.py:206
  250.5 2.2 reshape.394
  252.7 6.3 %all-to-all-done.3 = f32[64,1,512]{2,1,0:T(1,128)S(1)} async-done(((f32[64,1,512]{2,1,0:T(1,128)}), f32[64,1,512]{2,1,0:T(1,128)S(1)}, u32[]{:S(2)}, u32[]{:S(2)}) %all-to-all-start.3) | async-done | bytes 131104 | tf_op jit(solution)/shard_map/all_to_all | solution.py:206
  (150 shorter events, 46.5 us)
Async XLA Ops:
  0.6 2.1 copy-start
  6.3 14.1 %copy-start.5 = (s32[768,2]{0,1:T(2,128)S(1)}, s32[768,2]{0,1:T(2,128)}, u32[]{:S(2)}) copy-start(s32[768,2]{0,1:T(2,128)} %param.7) | copy-start | bytes 18436
  6.3 20.1 %copy-start.1 = (s32[32,48]{1,0:T(8,128)S(1)}, s32[32,48]{1,0:T(8,128)}, u32[]{:S(2)}) copy-start(s32[32,48]{1,0:T(8,128)} %param.6) | copy-start | bytes 18436
  6.3 20.8 %copy-start.2 = (f32[2,128,128]{2,1,0:T(8,128)S(1)}, f32[2,128,128]{2,1,0:T(8,128)}, u32[]{:S(2)}) copy-start(f32[2,128,128]{2,1,0:T(8,128)} %param.8) | copy-start | bytes 393220
  6.3 63.0 %all-to-all-start = ((bf16[64,4,4096]{2,1,0:T(4,128)(2,1)}), bf16[64,4,4096]{2,1,0:T(4,128)(2,1)S(1)}, u32[]{:S(2)}, u32[]{:S(2)}) async-start(bf16[64,4,4096]{2,1,0:T(4,128)(2,1)} %gather_fusion), calls=%async_computation | async-start | bytes 4194304 | tf_op jit(solution)/shard_map/all_to_all | solution.py:121
  20.4 7.0 %copy-start.3 = (f32[1,128,128]{2,1,0:T(8,128)S(1)}, f32[1,128,128]{2,1,0:T(8,128)}, u32[]{:S(2)}) copy-start(f32[1,128,128]{2,1,0:T(8,128)} %param.9) | copy-start | bytes 196612
  70.7 2.0 copy-start.10
  72.6 2.6 copy-start.6
  72.6 2.6 copy-start.8
  73.0 2.8 %copy-start.7 = (f32[128,128]{0,1:T(8,128)S(1)}, f32[128,128]{0,1:T(8,128)}, u32[]{:S(2)}) copy-start(f32[128,128]{0,1:T(8,128)} %get-tuple-element.49) | copy-start | bytes 196612
  79.4 29.2 %all-to-all-start.1 = ((bf16[12,99,128]{2,1,0:T(8,128)(2,1)}), bf16[12,99,128]{2,1,0:T(8,128)(2,1)S(1)}, u32[]{:S(2)}, u32[]{:S(2)}) async-start(bf16[12,99,128]{2,1,0:T(8,128)(2,1)} %reshape.386), calls=%async_computation.1 | async-start | bytes 638976 | tf_op jit(solution)/shard_map/all_to_all | solution.py:163
  113.5 62.3 %all-to-all-start.2 = ((bf16[64,140,128]{2,1,0:T(8,128)(2,1)}), bf16[64,140,128]{2,1,0:T(8,128)(2,1)S(1)}, u32[]{:S(2)}, u32[]{:S(2)}) async-start(bf16[64,140,128]{2,1,0:T(8,128)(2,1)} %reshape.390), calls=%async_computation.2 | async-start | bytes 4718592 | tf_op jit(solution)/shard_map/all_to_all | solution.py:184
  177.2 7.9 %collective-permute-start = (f32[25,1408]{1,0:T(8,128)S(1)}, f32[25,1408]{1,0:T(8,128)S(1)}, u32[]{:S(2)}, u32[]{:S(2)}) collective-permute-start(f32[25,1408]{1,0:T(8,128)S(1)} %pad_maximum_fusion.7), channel_id=1, source_target_pairs={{0,11},{1,0},{2,1},{3,2},{4,3},{5,4},{6,5},{7,6},{8,7},{9,8},{10,9... | collective-permute-start | bytes 422408 | tf_op jit(solution)/shard_map/ppermute | solution.py:222
  181.0 9.3 %collective-permute-start.5 = (f32[25,1408]{1,0:T(8,128)S(1)}, f32[25,1408]{1,0:T(8,128)S(1)}, u32[]{:S(2)}, u32[]{:S(2)}) collective-permute-start(f32[25,1408]{1,0:T(8,128)S(1)} %pad_maximum_fusion.7), channel_id=1, source_target_pairs={{0,1},{1,2},{2,3},{3,4},{4,5},{5,6},{6,7},{7,8},{8,9},{9,10},{10,1... | collective-permute-start | bytes 422408 | tf_op jit(solution)/shard_map/ppermute | solution.py:219
  185.1 9.5 %collective-permute-start.1 = (f32[25,1408]{1,0:T(8,128)S(1)}, f32[25,1408]{1,0:T(8,128)S(1)}, u32[]{:S(2)}, u32[]{:S(2)}) collective-permute-start(f32[25,1408]{1,0:T(8,128)S(1)} %collective-permute-done), channel_id=1, source_target_pairs={{0,11},{1,0},{2,1},{3,2},{4,3},{5,4},{6,5},{7,6},{8,7},{9,8},{10,9... | collective-permute-start | bytes 422408 | tf_op jit(solution)/shard_map/ppermute | solution.py:222
  190.3 10.5 %collective-permute-start.6 = (f32[25,1408]{1,0:T(8,128)S(1)}, f32[25,1408]{1,0:T(8,128)S(1)}, u32[]{:S(2)}, u32[]{:S(2)}) collective-permute-start(f32[25,1408]{1,0:T(8,128)S(1)} %collective-permute-done.5), channel_id=1, source_target_pairs={{0,1},{1,2},{2,3},{3,4},{4,5},{5,6},{6,7},{7,8},{8,9},{9,10},{10,1... | collective-permute-start | bytes 422408 | tf_op jit(solution)/shard_map/ppermute | solution.py:219
  194.6 9.7 %collective-permute-start.2 = (f32[25,1408]{1,0:T(8,128)S(1)}, f32[25,1408]{1,0:T(8,128)S(1)}, u32[]{:S(2)}, u32[]{:S(2)}) collective-permute-start(f32[25,1408]{1,0:T(8,128)S(1)} %collective-permute-done.1), channel_id=1, source_target_pairs={{0,11},{1,0},{2,1},{3,2},{4,3},{5,4},{6,5},{7,6},{8,7},{9,8},{10,9... | collective-permute-start | bytes 422408 | tf_op jit(solution)/shard_map/ppermute | solution.py:222
  200.8 9.7 %collective-permute-start.7 = (f32[25,1408]{1,0:T(8,128)S(1)}, f32[25,1408]{1,0:T(8,128)S(1)}, u32[]{:S(2)}, u32[]{:S(2)}) collective-permute-start(f32[25,1408]{1,0:T(8,128)S(1)} %collective-permute-done.6), channel_id=1, source_target_pairs={{0,1},{1,2},{2,3},{3,4},{4,5},{5,6},{6,7},{7,8},{8,9},{9,10},{10,1... | collective-permute-start | bytes 422408 | tf_op jit(solution)/shard_map/ppermute | solution.py:219
  204.3 8.8 %collective-permute-start.3 = (f32[25,1408]{1,0:T(8,128)S(1)}, f32[25,1408]{1,0:T(8,128)S(1)}, u32[]{:S(2)}, u32[]{:S(2)}) collective-permute-start(f32[25,1408]{1,0:T(8,128)S(1)} %collective-permute-done.2), channel_id=1, source_target_pairs={{0,11},{1,0},{2,1},{3,2},{4,3},{5,4},{6,5},{7,6},{8,7},{9,8},{10,9... | collective-permute-start | bytes 422408 | tf_op jit(solution)/shard_map/ppermute | solution.py:222
  210.4 8.8 %collective-permute-start.8 = (f32[25,1408]{1,0:T(8,128)S(1)}, f32[25,1408]{1,0:T(8,128)S(1)}, u32[]{:S(2)}, u32[]{:S(2)}) collective-permute-start(f32[25,1408]{1,0:T(8,128)S(1)} %collective-permute-done.7), channel_id=1, source_target_pairs={{0,1},{1,2},{2,3},{3,4},{4,5},{5,6},{6,7},{7,8},{8,9},{9,10},{10,1... | collective-permute-start | bytes 422408 | tf_op jit(solution)/shard_map/ppermute | solution.py:219
  213.1 16.7 %collective-permute-start.4 = (f32[25,1408]{1,0:T(8,128)S(1)}, f32[25,1408]{1,0:T(8,128)S(1)}, u32[]{:S(2)}, u32[]{:S(2)}) collective-permute-start(f32[25,1408]{1,0:T(8,128)S(1)} %collective-permute-done.3), channel_id=1, source_target_pairs={{0,11},{1,0},{2,1},{3,2},{4,3},{5,4},{6,5},{7,6},{8,7},{9,8},{10,9... | collective-permute-start | bytes 422408 | tf_op jit(solution)/shard_map/ppermute | solution.py:222
  219.3 8.6 %collective-permute-start.9 = (f32[25,1408]{1,0:T(8,128)S(1)}, f32[25,1408]{1,0:T(8,128)S(1)}, u32[]{:S(2)}, u32[]{:S(2)}) collective-permute-start(f32[25,1408]{1,0:T(8,128)S(1)} %collective-permute-done.8), channel_id=1, source_target_pairs={{0,1},{1,2},{2,3},{3,4},{4,5},{5,6},{6,7},{7,8},{8,9},{9,10},{10,1... | collective-permute-start | bytes 422408 | tf_op jit(solution)/shard_map/ppermute | solution.py:219
  227.9 8.6 %collective-permute-start.10 = (f32[25,1408]{1,0:T(8,128)S(1)}, f32[25,1408]{1,0:T(8,128)S(1)}, u32[]{:S(2)}, u32[]{:S(2)}) collective-permute-start(f32[25,1408]{1,0:T(8,128)S(1)} %collective-permute-done.9), channel_id=1, source_target_pairs={{0,1},{1,2},{2,3},{3,4},{4,5},{5,6},{6,7},{7,8},{8,9},{9,10},{10,1... | collective-permute-start | bytes 422408 | tf_op jit(solution)/shard_map/ppermute | solution.py:219
  243.6 15.4 %all-to-all-start.3 = ((f32[64,1,512]{2,1,0:T(1,128)}), f32[64,1,512]{2,1,0:T(1,128)S(1)}, u32[]{:S(2)}, u32[]{:S(2)}) async-start(f32[64,1,512]{2,1,0:T(1,128)} %broadcast_in_dim.19), calls=%async_computation.3 | async-start | bytes 262144 | tf_op jit(solution)/shard_map/all_to_all | solution.py:206
  (3 other events, 4.6 us)

commit v11 on v10

--- a/solution.py
+++ b/solution.py
@@ -198,7 +198,8 @@
     my_slice = jnp.einsum("qtk,qtx->kx", all_sel, from_owners, preferred_element_type=jnp.float32)
 
     probe_cut = jnp.pad(probe_row, (0, cut_len - piece_len))[None]
-    gathered = ring_gather(jnp.concatenate([my_slice, probe_cut], axis=0), layers)
+    block = jnp.concatenate([my_slice, probe_cut], axis=0)
+    gathered = ring_gather(block.reshape(-1, 128), layers).reshape((layers,) + block.shape)
     slices = gathered[:, :tiles_dev]
     tile_total = slices.transpose(1, 0, 2).reshape(tiles_dev, layers * cut_len)[:, :tile_px]
     probe_piece = jnp.sum(gathered[:, tiles_dev, :piece_len], axis=0)

time: 263 us -> 258 us (0.981)
  waiting for transfers between devices: 125 us -> 115 us
  local copies, waits for them, and re-layouts: 31.6 us -> 35 us
    ppermute x6, waiting for transfers between devices: 14 us -> 7.97 us  [ring_gather(): going_right = lax.ppermute(going_right, 'tile', to_right)]
    ppermute x6, starting transfers between devices: 12 us -> 15.1 us  [ring_gather(): going_right = lax.ppermute(going_right, 'tile', to_right)]
    unnamed x41 -> x43, local copies, waits for them, and re-layouts: 8.67 us -> 10.7 us
  transfers between devices with their start and end apart: 15 -> 15, of which waited for: 14 -> 11; matrix products, arithmetic and copies ran while one was open for 8% -> 8% of each run, Pallas kernels for 0% -> 0%
where the time goes in v11:
time: 258 us; the launch traced here: 255 us
  waiting for transfers between devices  115 us (45%)
  starting transfers between devices  79.5 us (31%)
  local copies, waits for them, and re-layouts  35 us (14%)
  matrix products  14.3 us (6%)
  between operations  6.73 us (3%)
  other arithmetic  3.84 us (1%)
    all_to_all x1, waiting for transfers between devices, per_device(): lax.all_to_all(outgoing, 'pos', 0, 0, tiled=True).reshape(owners, slot_len)  53.2 us
    all_to_all x1, waiting for transfers between devices, per_device(): lax.all_to_all(chosen, 'pos', split_axis=0, concat_axis=0, tiled=True)  31.3 us
    ppermute x5, starting transfers between devices, ring_gather(): going_left = lax.ppermute(going_left, 'tile', to_left)  22.9 us
    all_to_all x1, waiting for transfers between devices, per_device(): from_column = lax.all_to_all(cut, 'tile', 0, 0, tiled=True)  16.8 us
    ppermute x6, starting transfers between devices, ring_gather(): going_right = lax.ppermute(going_right, 'tile', to_right)  15.1 us
    all_to_all x1, starting transfers between devices, per_device(): lax.all_to_all(chosen, 'pos', split_axis=0, concat_axis=0, tiled=True)  14.1 us
    all_to_all x1, starting transfers between devices, per_device(): from_column = lax.all_to_all(cut, 'tile', 0, 0, tiled=True)  12 us
    dot_general x16, matrix products, matmul_hi(): jnp.dot(left_op, right_op, precision=lax.Precision.HIGHEST, preferred_ele...  11 us
  transfers between devices with their start and end apart: 15, of which 11 were waited for; matrix products, arithmetic and copies ran while one was open for 8% of the time, Pallas kernels for 0%

profile of v11, /device:TPU:6, one launch (start us, length us, event | category | flops | bytes accessed | tf_op | source)
XLA Modules:
  0.0 254.6 jit_solution(14160554059773946706)
XLA Ops:
  2.8 3.6 %gather_fusion = bf16[64,4,4096]{2,1,0:T(4,128)(2,1)} fusion(bf16[24,4,4096]{2,1,0:T(4,128)(2,1)S(1)} %copy-done, s32[1024]{0:T(1024)S(1)} %pad_clamp_fusion.2), kind=kCustom, calls=%fused_computation | custom fusion | bytes 4194560 | tf_op jit(solution)/shard_map/gather | solution.py:103
  6.3 14.1 %all-to-all-start = ((bf16[64,4,4096]{2,1,0:T(4,128)(2,1)}), bf16[64,4,4096]{2,1,0:T(4,128)(2,1)S(1)}, u32[]{:S(2)}, u32[]{:S(2)}) async-start(bf16[64,4,4096]{2,1,0:T(4,128)(2,1)} %gather_fusion), calls=%async_computation | async-start | bytes 4194304 | tf_op jit(solution)/shard_map/all_to_all | solution.py:121
  38.0 31.3 %all-to-all-done = bf16[64,4,4096]{2,1,0:T(4,128)(2,1)S(1)} async-done(((bf16[64,4,4096]{2,1,0:T(4,128)(2,1)}), bf16[64,4,4096]{2,1,0:T(4,128)(2,1)S(1)}, u32[]{:S(2)}, u32[]{:S(2)}) %all-to-all-start) | async-done | bytes 2097184 | tf_op jit(solution)/shard_map/all_to_all | solution.py:121
  79.4 12.0 %all-to-all-start.1 = ((bf16[12,99,128]{2,1,0:T(8,128)(2,1)}), bf16[12,99,128]{2,1,0:T(8,128)(2,1)S(1)}, u32[]{:S(2)}, u32[]{:S(2)}) async-start(bf16[12,99,128]{2,1,0:T(8,128)(2,1)} %reshape.392), calls=%async_computation.1 | async-start | bytes 638976 | tf_op jit(solution)/shard_map/all_to_all | solution.py:163
  91.8 16.8 %all-to-all-done.1 = bf16[12,99,128]{2,1,0:T(8,128)(2,1)S(1)} async-done(((bf16[12,99,128]{2,1,0:T(8,128)(2,1)}), bf16[12,99,128]{2,1,0:T(8,128)(2,1)S(1)}, u32[]{:S(2)}, u32[]{:S(2)}) %all-to-all-start.1) | async-done | bytes 304160 | tf_op jit(solution)/shard_map/all_to_all | solution.py:163
  111.0 2.6 %reshape.396 = bf16[64,140,128]{2,1,0:T(8,128)(2,1)} reshape(bf16[64,17920]{1,0:T(8,128)(2,1)S(1)} %pad_maximum_fusion) | data formatting | bytes 4587520 | tf_op jit(solution)/shard_map/reshape | solution.py:183
  113.5 8.1 %all-to-all-start.2 = ((bf16[64,140,128]{2,1,0:T(8,128)(2,1)}), bf16[64,140,128]{2,1,0:T(8,128)(2,1)S(1)}, u32[]{:S(2)}, u32[]{:S(2)}) async-start(bf16[64,140,128]{2,1,0:T(8,128)(2,1)} %reshape.396), calls=%async_computation.2 | async-start | bytes 4718592 | tf_op jit(solution)/shard_map/all_to_all | solution.py:184
  122.6 53.2 %all-to-all-done.2 = bf16[64,140,128]{2,1,0:T(8,128)(2,1)S(1)} async-done(((bf16[64,140,128]{2,1,0:T(8,128)(2,1)}), bf16[64,140,128]{2,1,0:T(8,128)(2,1)S(1)}, u32[]{:S(2)}, u32[]{:S(2)}) %all-to-all-start.2) | async-done | bytes 2293792 | tf_op jit(solution)/shard_map/all_to_all | solution.py:184
  177.2 4.3 %collective-permute-start.5 = (f32[275,128]{1,0:T(8,128)S(1)}, f32[275,128]{1,0:T(8,128)S(1)}, u32[]{:S(2)}, u32[]{:S(2)}) collective-permute-start(f32[275,128]{1,0:T(8,128)S(1)} %reshape.399), channel_id=1, source_target_pairs={{0,1},{1,2},{2,3},{3,4},{4,5},{5,6},{6,7},{7,8},{8,9},{9,10},{10,1... | collective-permute-start | bytes 422408 | tf_op jit(solution)/shard_map/ppermute | solution.py:220
  181.5 2.7 %collective-permute-start = (f32[275,128]{1,0:T(8,128)S(1)}, f32[275,128]{1,0:T(8,128)S(1)}, u32[]{:S(2)}, u32[]{:S(2)}) collective-permute-start(f32[275,128]{1,0:T(8,128)S(1)} %reshape.399), channel_id=1, source_target_pairs={{0,11},{1,0},{2,1},{3,2},{4,3},{5,4},{6,5},{7,6},{8,7},{9,8},{10,9... | collective-permute-start | bytes 422408 | tf_op jit(solution)/shard_map/ppermute | solution.py:223
  185.4 3.1 %collective-permute-start.6 = (f32[275,128]{1,0:T(8,128)S(1)}, f32[275,128]{1,0:T(8,128)S(1)}, u32[]{:S(2)}, u32[]{:S(2)}) collective-permute-start(f32[275,128]{1,0:T(8,128)S(1)} %collective-permute-done.5), channel_id=1, source_target_pairs={{0,1},{1,2},{2,3},{3,4},{4,5},{5,6},{6,7},{7,8},{8,9},{9,10},{10,1... | collective-permute-start | bytes 422408 | tf_op jit(solution)/shard_map/ppermute | solution.py:220
  188.9 3.9 %collective-permute-start.1 = (f32[275,128]{1,0:T(8,128)S(1)}, f32[275,128]{1,0:T(8,128)S(1)}, u32[]{:S(2)}, u32[]{:S(2)}) collective-permute-start(f32[275,128]{1,0:T(8,128)S(1)} %collective-permute-done), channel_id=1, source_target_pairs={{0,11},{1,0},{2,1},{3,2},{4,3},{5,4},{6,5},{7,6},{8,7},{9,8},{10,9... | collective-permute-start | bytes 422408 | tf_op jit(solution)/shard_map/ppermute | solution.py:223
  194.8 1.9 collective-permute-start.7
  197.3 5.1 %collective-permute-start.2 = (f32[275,128]{1,0:T(8,128)S(1)}, f32[275,128]{1,0:T(8,128)S(1)}, u32[]{:S(2)}, u32[]{:S(2)}) collective-permute-start(f32[275,128]{1,0:T(8,128)S(1)} %collective-permute-done.1), channel_id=1, source_target_pairs={{0,11},{1,0},{2,1},{3,2},{4,3},{5,4},{6,5},{7,6},{8,7},{9,8},{10,9... | collective-permute-start | bytes 422408 | tf_op jit(solution)/shard_map/ppermute | solution.py:223
  203.7 1.9 collective-permute-start.8
  205.7 5.6 %collective-permute-start.3 = (f32[275,128]{1,0:T(8,128)S(1)}, f32[275,128]{1,0:T(8,128)S(1)}, u32[]{:S(2)}, u32[]{:S(2)}) collective-permute-start(f32[275,128]{1,0:T(8,128)S(1)} %collective-permute-done.2), channel_id=1, source_target_pairs={{0,11},{1,0},{2,1},{3,2},{4,3},{5,4},{6,5},{7,6},{8,7},{9,8},{10,9... | collective-permute-start | bytes 422408 | tf_op jit(solution)/shard_map/ppermute | solution.py:223
  212.0 1.9 collective-permute-start.9
  213.9 5.6 %collective-permute-start.4 = (f32[275,128]{1,0:T(8,128)S(1)}, f32[275,128]{1,0:T(8,128)S(1)}, u32[]{:S(2)}, u32[]{:S(2)}) collective-permute-start(f32[275,128]{1,0:T(8,128)S(1)} %collective-permute-done.3), channel_id=1, source_target_pairs={{0,11},{1,0},{2,1},{3,2},{4,3},{5,4},{6,5},{7,6},{8,7},{9,8},{10,9... | collective-permute-start | bytes 422408 | tf_op jit(solution)/shard_map/ppermute | solution.py:223
  220.2 1.9 collective-permute-start.10
  222.8 5.6 %collective-permute-done.10 = f32[275,128]{1,0:T(8,128)S(1)} collective-permute-done((f32[275,128]{1,0:T(8,128)S(1)}, f32[275,128]{1,0:T(8,128)S(1)}, u32[]{:S(2)}, u32[]{:S(2)}) %collective-permute-start.10) | collective-permute-done | bytes 140832 | tf_op jit(solution)/shard_map/ppermute | solution.py:220
  232.4 2.1 gather_fusion.4
  237.8 7.3 %all-to-all-start.3 = ((f32[64,1,512]{2,1,0:T(1,128)}), f32[64,1,512]{2,1,0:T(1,128)S(1)}, u32[]{:S(2)}, u32[]{:S(2)}) async-start(f32[64,1,512]{2,1,0:T(1,128)} %broadcast_in_dim.19), calls=%async_computation.3 | async-start | bytes 262144 | tf_op jit(solution)/shard_map/all_to_all | solution.py:207
  246.9 2.2 reshape.402
  249.1 4.9 %all-to-all-done.3 = f32[64,1,512]{2,1,0:T(1,128)S(1)} async-done(((f32[64,1,512]{2,1,0:T(1,128)}), f32[64,1,512]{2,1,0:T(1,128)S(1)}, u32[]{:S(2)}, u32[]{:S(2)}) %all-to-all-start.3) | async-done | bytes 131104 | tf_op jit(solution)/shard_map/all_to_all | solution.py:207
  (153 shorter events, 46.2 us)
Async XLA Ops:
  0.6 2.1 copy-start
  6.3 14.1 %copy-start.5 = (s32[768,2]{0,1:T(2,128)S(1)}, s32[768,2]{0,1:T(2,128)}, u32[]{:S(2)}) copy-start(s32[768,2]{0,1:T(2,128)} %param.7) | copy-start | bytes 18436
  6.3 20.1 %copy-start.1 = (s32[32,48]{1,0:T(8,128)S(1)}, s32[32,48]{1,0:T(8,128)}, u32[]{:S(2)}) copy-start(s32[32,48]{1,0:T(8,128)} %param.6) | copy-start | bytes 18436
  6.3 63.0 %all-to-all-start = ((bf16[64,4,4096]{2,1,0:T(4,128)(2,1)}), bf16[64,4,4096]{2,1,0:T(4,128)(2,1)S(1)}, u32[]{:S(2)}, u32[]{:S(2)}) async-start(bf16[64,4,4096]{2,1,0:T(4,128)(2,1)} %gather_fusion), calls=%async_computation | async-start | bytes 4194304 | tf_op jit(solution)/shard_map/all_to_all | solution.py:121
  27.4 1.9 copy-start.3
  27.4 2.0 copy-start.2
  71.2 1.4 copy-start.10
  73.0 2.2 copy-start.6
  73.0 2.2 copy-start.8
  73.1 2.7 %copy-start.7 = (f32[128,128]{0,1:T(8,128)S(1)}, f32[128,128]{0,1:T(8,128)}, u32[]{:S(2)}) copy-start(f32[128,128]{0,1:T(8,128)} %get-tuple-element.49) | copy-start | bytes 196612
  79.4 29.2 %all-to-all-start.1 = ((bf16[12,99,128]{2,1,0:T(8,128)(2,1)}), bf16[12,99,128]{2,1,0:T(8,128)(2,1)S(1)}, u32[]{:S(2)}, u32[]{:S(2)}) async-start(bf16[12,99,128]{2,1,0:T(8,128)(2,1)} %reshape.392), calls=%async_computation.1 | async-start | bytes 638976 | tf_op jit(solution)/shard_map/all_to_all | solution.py:163
  113.5 62.3 %all-to-all-start.2 = ((bf16[64,140,128]{2,1,0:T(8,128)(2,1)}), bf16[64,140,128]{2,1,0:T(8,128)(2,1)S(1)}, u32[]{:S(2)}, u32[]{:S(2)}) async-start(bf16[64,140,128]{2,1,0:T(8,128)(2,1)} %reshape.396), calls=%async_computation.2 | async-start | bytes 4718592 | tf_op jit(solution)/shard_map/all_to_all | solution.py:184
  177.2 8.2 %collective-permute-start.5 = (f32[275,128]{1,0:T(8,128)S(1)}, f32[275,128]{1,0:T(8,128)S(1)}, u32[]{:S(2)}, u32[]{:S(2)}) collective-permute-start(f32[275,128]{1,0:T(8,128)S(1)} %reshape.399), channel_id=1, source_target_pairs={{0,1},{1,2},{2,3},{3,4},{4,5},{5,6},{6,7},{7,8},{8,9},{9,10},{10,1... | collective-permute-start | bytes 422408 | tf_op jit(solution)/shard_map/ppermute | solution.py:220
  181.5 7.3 %collective-permute-start = (f32[275,128]{1,0:T(8,128)S(1)}, f32[275,128]{1,0:T(8,128)S(1)}, u32[]{:S(2)}, u32[]{:S(2)}) collective-permute-start(f32[275,128]{1,0:T(8,128)S(1)} %reshape.399), channel_id=1, source_target_pairs={{0,11},{1,0},{2,1},{3,2},{4,3},{5,4},{6,5},{7,6},{8,7},{9,8},{10,9... | collective-permute-start | bytes 422408 | tf_op jit(solution)/shard_map/ppermute | solution.py:223
  185.4 9.4 %collective-permute-start.6 = (f32[275,128]{1,0:T(8,128)S(1)}, f32[275,128]{1,0:T(8,128)S(1)}, u32[]{:S(2)}, u32[]{:S(2)}) collective-permute-start(f32[275,128]{1,0:T(8,128)S(1)} %collective-permute-done.5), channel_id=1, source_target_pairs={{0,1},{1,2},{2,3},{3,4},{4,5},{5,6},{6,7},{7,8},{8,9},{9,10},{10,1... | collective-permute-start | bytes 422408 | tf_op jit(solution)/shard_map/ppermute | solution.py:220
  188.9 8.4 %collective-permute-start.1 = (f32[275,128]{1,0:T(8,128)S(1)}, f32[275,128]{1,0:T(8,128)S(1)}, u32[]{:S(2)}, u32[]{:S(2)}) collective-permute-start(f32[275,128]{1,0:T(8,128)S(1)} %collective-permute-done), channel_id=1, source_target_pairs={{0,11},{1,0},{2,1},{3,2},{4,3},{5,4},{6,5},{7,6},{8,7},{9,8},{10,9... | collective-permute-start | bytes 422408 | tf_op jit(solution)/shard_map/ppermute | solution.py:223
  194.8 8.9 %collective-permute-start.7 = (f32[275,128]{1,0:T(8,128)S(1)}, f32[275,128]{1,0:T(8,128)S(1)}, u32[]{:S(2)}, u32[]{:S(2)}) collective-permute-start(f32[275,128]{1,0:T(8,128)S(1)} %collective-permute-done.6), channel_id=1, source_target_pairs={{0,1},{1,2},{2,3},{3,4},{4,5},{5,6},{6,7},{7,8},{8,9},{9,10},{10,1... | collective-permute-start | bytes 422408 | tf_op jit(solution)/shard_map/ppermute | solution.py:220
  197.3 8.4 %collective-permute-start.2 = (f32[275,128]{1,0:T(8,128)S(1)}, f32[275,128]{1,0:T(8,128)S(1)}, u32[]{:S(2)}, u32[]{:S(2)}) collective-permute-start(f32[275,128]{1,0:T(8,128)S(1)} %collective-permute-done.1), channel_id=1, source_target_pairs={{0,11},{1,0},{2,1},{3,2},{4,3},{5,4},{6,5},{7,6},{8,7},{9,8},{10,9... | collective-permute-start | bytes 422408 | tf_op jit(solution)/shard_map/ppermute | solution.py:223
  203.7 8.3 %collective-permute-start.8 = (f32[275,128]{1,0:T(8,128)S(1)}, f32[275,128]{1,0:T(8,128)S(1)}, u32[]{:S(2)}, u32[]{:S(2)}) collective-permute-start(f32[275,128]{1,0:T(8,128)S(1)} %collective-permute-done.7), channel_id=1, source_target_pairs={{0,1},{1,2},{2,3},{3,4},{4,5},{5,6},{6,7},{7,8},{8,9},{9,10},{10,1... | collective-permute-start | bytes 422408 | tf_op jit(solution)/shard_map/ppermute | solution.py:220
  205.7 8.2 %collective-permute-start.3 = (f32[275,128]{1,0:T(8,128)S(1)}, f32[275,128]{1,0:T(8,128)S(1)}, u32[]{:S(2)}, u32[]{:S(2)}) collective-permute-start(f32[275,128]{1,0:T(8,128)S(1)} %collective-permute-done.2), channel_id=1, source_target_pairs={{0,11},{1,0},{2,1},{3,2},{4,3},{5,4},{6,5},{7,6},{8,7},{9,8},{10,9... | collective-permute-start | bytes 422408 | tf_op jit(solution)/shard_map/ppermute | solution.py:223
  212.0 8.2 %collective-permute-start.9 = (f32[275,128]{1,0:T(8,128)S(1)}, f32[275,128]{1,0:T(8,128)S(1)}, u32[]{:S(2)}, u32[]{:S(2)}) collective-permute-start(f32[275,128]{1,0:T(8,128)S(1)} %collective-permute-done.8), channel_id=1, source_target_pairs={{0,1},{1,2},{2,3},{3,4},{4,5},{5,6},{6,7},{7,8},{8,9},{9,10},{10,1... | collective-permute-start | bytes 422408 | tf_op jit(solution)/shard_map/ppermute | solution.py:220
  213.9 8.2 %collective-permute-start.4 = (f32[275,128]{1,0:T(8,128)S(1)}, f32[275,128]{1,0:T(8,128)S(1)}, u32[]{:S(2)}, u32[]{:S(2)}) collective-permute-start(f32[275,128]{1,0:T(8,128)S(1)} %collective-permute-done.3), channel_id=1, source_target_pairs={{0,11},{1,0},{2,1},{3,2},{4,3},{5,4},{6,5},{7,6},{8,7},{9,8},{10,9... | collective-permute-start | bytes 422408 | tf_op jit(solution)/shard_map/ppermute | solution.py:223
  220.2 8.2 %collective-permute-start.10 = (f32[275,128]{1,0:T(8,128)S(1)}, f32[275,128]{1,0:T(8,128)S(1)}, u32[]{:S(2)}, u32[]{:S(2)}) collective-permute-start(f32[275,128]{1,0:T(8,128)S(1)} %collective-permute-done.9), channel_id=1, source_target_pairs={{0,1},{1,2},{2,3},{3,4},{4,5},{5,6},{6,7},{7,8},{8,9},{9,10},{10,1... | collective-permute-start | bytes 422408 | tf_op jit(solution)/shard_map/ppermute | solution.py:220
  237.8 16.1 %all-to-all-start.3 = ((f32[64,1,512]{2,1,0:T(1,128)}), f32[64,1,512]{2,1,0:T(1,128)S(1)}, u32[]{:S(2)}, u32[]{:S(2)}) async-start(f32[64,1,512]{2,1,0:T(1,128)} %broadcast_in_dim.19), calls=%async_computation.3 | async-start | bytes 262144 | tf_op jit(solution)/shard_map/all_to_all | solution.py:207
  (3 other events, 4.1 us)
